TPU v7x, 32 devices: a whole 2x2x4 slice. The times are simulated.
32 devices in a mesh: runs: 2 (over x), tile: 16 (over z, y, core).
Axes of the slice: x: 2, y: 2, z: 4, core: 2. Of those that a mesh axis runs over, the one named last changes fastest.
Arguments:
- fluid_press: float32 [8192, 128], P(('runs', 'tile')), parts along dimension 0, may hold values from -6 to 6
- iterate: float32 [8192, 128], P(('runs', 'tile')), parts along dimension 0, may hold values from -6 to 6
- displace: float32 [4096, 128], P(('runs', 'tile')), parts along dimension 0, may hold values from -6 to 6
- velocity: float32 [4096, 128], P(('runs', 'tile')), parts along dimension 0, may hold values from -6 to 6
- stiffness: float32 [4096, 128], P(('runs', 'tile')), parts along dimension 0, may hold values from 0.08 to 0.45
- owners: int32 [4096, 1], P(('runs', 'tile')), parts along dimension 0, may hold values from 0 to 15; in each aligned block of 128 rows (0 to 127, 128 to 255, ...) at most 16 rows name the same one
- diff_cur: bfloat16 [40, 8192, 128], P(None, ('runs', 'tile')), parts along dimension 1, may hold values from -1.1048543 to 1.1048543
- step_cur: bfloat16 [40, 8192, 128], P(None, ('runs', 'tile')), parts along dimension 1, may hold values from -6 to 6
- diff_past: bfloat16 [30, 8192, 128], P(None, ('runs', 'tile')), parts along dimension 1, may hold values from -1.1048543 to 1.1048543
- step_past: bfloat16 [30, 8192, 128], P(None, ('runs', 'tile')), parts along dimension 1, may hold values from -6 to 6
Outputs:
- new_iterate: float32 [8192, 128], P(('runs', 'tile')), parts along dimension 0
- displace_out: float32 [4096, 128], P(('runs', 'tile')), parts along dimension 0
- velocity_out: float32 [4096, 128], P(('runs', 'tile')), parts along dimension 0
There are 2 independent parts, one for each index of `runs`. A program takes and returns all parts, laid end to end along the dimension named above; each array names one. Nothing has to cross between parts.
Inputs may be any that keep to these rules, and one draw needn't show every extreme that they name: `owners`: in the 128 lines of one device no partition is named more than 16 times; some partition is named exactly 16 times.
All inputs are finite; a program needn't handle non-finite values.
Results may differ from a plain program's by a relative error of at most 0.0042.
Values sent between devices are 32-bit elements; how exact they have to be, the bound alone decides.
No kernel may reach another device: no remote copies, remote signals or barrier semaphores. Data moves between devices by JAX's collectives and lax.ppermute only.
A program may use at most 64 MiB of HBM per device.

v0:
```python
import jax
import jax.numpy as jnp
from jax import lax
from jax.sharding import PartitionSpec as P

SUBSTEPS = 4


step_dt = 1.0
damping = 0.05


def padded_2(cells, sides, width):
    for axis, dim in sides:
        count = lax.axis_size(axis)
        head = lax.slice_in_dim(cells, 0, width, axis=dim)
        tail = lax.slice_in_dim(cells, cells.shape[dim] - width, cells.shape[dim], axis=dim)
        cells = jnp.concatenate(
            [
                lax.ppermute(tail, axis, [(i, (i + 1) % count) for i in range(count)]),
                cells,
                lax.ppermute(head, axis, [((i + 1) % count, i) for i in range(count)]),
            ],
            axis=dim,
        )
    return cells


def sides(center):
    zero_col = jnp.zeros((center.shape[0], 1), jnp.float32)
    left = jnp.concatenate([zero_col, center[:, :-1]], 1)
    right = jnp.concatenate([center[:, 1:], zero_col], 1)
    return left + right


def solve_spd(matrix, vector):
    factor = jnp.linalg.cholesky(matrix)
    inner = lax.linalg.triangular_solve(factor, vector[:, None], left_side=True, lower=True)
    outer = lax.linalg.triangular_solve(factor, inner, left_side=True, lower=True, transpose_a=True)
    return outer[:, 0]


def local(
    fluid_press,
    iterate,
    displace,
    velocity,
    stiffness,
    owners,
    diff_cur,
    step_cur,
    diff_past,
    step_past,
):
    high = lax.Precision.HIGHEST
    tile_count = lax.axis_size("tile")
    line_count = displace.shape[0]
    slot_count = iterate.shape[0]
    per_pair = slot_count // tile_count
    owner_list = owners[:, 0]
    onehot = (owner_list[:, None] == jnp.arange(tile_count, dtype=jnp.int32)[None, :]).astype(
        jnp.float32
    )
    below = (jnp.arange(line_count)[:, None] > jnp.arange(line_count)[None, :]).astype(jnp.float32)
    earlier = jnp.dot(below, onehot, precision=high)
    rank_in = jnp.sum(earlier * onehot, axis=1).astype(jnp.int32)
    slot_of = owner_list * per_pair + rank_in
    chooser = (slot_of[:, None] == jnp.arange(slot_count, dtype=jnp.int32)[None, :]).astype(
        jnp.float32
    )
    returned = lax.all_to_all(fluid_press, "tile", split_axis=0, concat_axis=0, tiled=True)
    pressure = jnp.dot(chooser, returned, precision=high)
    field, speed = (displace, velocity)
    for substep in range(SUBSTEPS):
        padded = padded_2(field, (("tile", 0),), 1)
        lapl = padded[:-2] + padded[2:] + sides(field) - 4.0 * field
        speed = speed + step_dt * (stiffness * lapl + pressure - damping * speed)
        field = field + step_dt * speed
    outgoing = jnp.dot(chooser.T, field, precision=high)
    flags = jnp.sum(chooser, axis=0)
    x_tilde, mask = (
        lax.all_to_all(outgoing, "tile", split_axis=0, concat_axis=0, tiled=True),
        lax.all_to_all(flags, "tile", split_axis=0, concat_axis=0, tiled=True),
    )
    mask_half = mask.astype(jnp.bfloat16)
    cur_cols = (diff_cur * mask_half[None, :, None]).reshape(diff_cur.shape[0], -1)
    past_cols = (diff_past * mask_half[None, :, None]).reshape(diff_past.shape[0], -1)
    resid = (mask[:, None] * (x_tilde - iterate)).astype(jnp.bfloat16).reshape(-1)
    gram_cur = lax.dot_general(
        cur_cols, cur_cols, (((1,), (1,)), ((), ())), preferred_element_type=jnp.float32
    )
    rhs_cur = jnp.dot(cur_cols, resid, preferred_element_type=jnp.float32)
    gram_past = lax.dot_general(
        past_cols, past_cols, (((1,), (1,)), ((), ())), preferred_element_type=jnp.float32
    )
    gram_cur, rhs_cur, gram_past = lax.psum((gram_cur, rhs_cur, gram_past), "tile")
    coeff = -solve_spd(gram_cur, rhs_cur)
    proj = resid.astype(jnp.float32) + jnp.dot(
        coeff, cur_cols, precision=high, preferred_element_type=jnp.float32
    )
    projected = lax.psum(
        jnp.dot(past_cols, proj, precision=high, preferred_element_type=jnp.float32), "tile"
    )
    past = solve_spd(gram_past, projected)
    upd_cur = jnp.dot(
        coeff.astype(jnp.bfloat16),
        step_cur.reshape(step_cur.shape[0], -1),
        preferred_element_type=jnp.float32,
    )
    upd_past = jnp.dot(
        past.astype(jnp.bfloat16),
        step_past.reshape(step_past.shape[0], -1),
        preferred_element_type=jnp.float32,
    )
    update = (upd_cur - upd_past).reshape(x_tilde.shape)
    new_iterate = mask[:, None] * (x_tilde + update)
    return (new_iterate, field, speed)


def solution(mesh):
    placed = (
        P(("runs", "tile"), None),
        P(("runs", "tile"), None),
        P(("runs", "tile"), None),
        P(("runs", "tile"), None),
        P(("runs", "tile"), None),
        P(("runs", "tile"), None),
        P(None, ("runs", "tile"), None),
        P(None, ("runs", "tile"), None),
        P(None, ("runs", "tile"), None),
        P(None, ("runs", "tile"), None),
    )
    return jax.shard_map(
        local,
        mesh=mesh,
        in_specs=placed,
        out_specs=(P(("runs", "tile"), None), P(("runs", "tile"), None), P(("runs", "tile"), None)),
        check_vma=False,
    )
```

profile of v0, /device:TPU:0, one launch (start us, length us, event | category | flops | bytes accessed | tf_op | source)
XLA Modules:
  0.0 210.6 jit_solution(13058534543472758253)
XLA Ops:
  0.6 0.7 fusion.90
  1.3 0.5 collective-permute-start
  1.8 5.0 %collective-permute-start.1 = (f32[1,128]{1,0:T(1,128)S(1)}, f32[1,128]{1,0:T(1,128)S(1)}, u32[]{:S(2)}, u32[]{:S(2)}) collective-permute-start(f32[1,128]{1,0:T(1,128)S(1)} %get-tuple-element.28), channel_id=1, source_target_pairs={{1,0},{2,1},{3,2},{4,3},{5,4},{6,5},{7,6},{8,7},{9,8},{10,9},{11,1... | collective-permute-start | bytes 1544 | tf_op jit(solution)/shard_map/ppermute | solution.py:22
  6.8 0.9 fusion.18
  7.7 0.7 fusion.74
  8.5 0.7 all_to_all.22
  9.2 3.7 %all-to-all-start = ((f32[16,16,1]{1,2,0:T(1,128)}), f32[16,16,1]{1,2,0:T(1,128)S(1)}, u32[]{:S(2)}, u32[]{:S(2)}) async-start(f32[16,16,1]{1,2,0:T(1,128)} %bitcast.3), calls=%async_computation | async-start | bytes 16384 | tf_op jit(solution)/shard_map/all_to_all | solution.py:83
  12.9 1.0 fusion.91
  13.8 1.8 pad.41
  15.6 2.7 %copy.55 = bf16[4,8,256,128]{3,1,2,0:T(8,128)(2,1)} copy(bf16[4,8,256,128]{3,2,1,0:T(8,128)(2,1)S(1)} %bitcast.116) | data formatting | bytes 4194304
  18.3 0.9 all-to-all-done
  19.2 5.1 %all-to-all-start.1 = ((f32[16,16,128]{2,1,0:T(8,128)}), f32[16,16,128]{2,1,0:T(8,128)S(1)}, u32[]{:S(2)}, u32[]{:S(2)}) async-start(f32[16,16,128]{2,1,0:T(8,128)} %bitcast.4), calls=%async_computation.1 | async-start | bytes 262144 | tf_op jit(solution)/shard_map/all_to_all | solution.py:71
  24.3 0.5 broadcast.160
  24.9 0.7 reduce.15
  25.6 2.1 %broadcast_multiply_fusion = bf16[40,256,128]{2,1,0:T(8,128)(2,1)S(1)} fusion(bf16[40,256,128]{2,1,0:T(8,128)(2,1)} %param.16, bf16[256]{0:T(256)(128)(2,1)S(1)} %convert_element_type.45), kind=kLoop, calls=%fused_computation.12 | loop fusion | flops 1310720 | bytes 5243392 | tf_op jit(solution)/shard_map/mul | solution.py:86
  28.0 0.2 broadcast_multiply_fusion.1
  28.2 3.5 %fusion.12 = f32[40,40]{0,1:T(8,128)S(1)} fusion(bf16[40,256,128]{2,1,0:T(8,128)(2,1)S(1)} %broadcast_multiply_fusion), kind=kOutput, calls=%fused_computation.13 | convolution fusion | flops 104857600 | bytes 2627840 | tf_op jit(solution)/shard_map/dot_general | solution.py:89
  31.7 0.2 pad.40
  32.0 2.7 %copy.53 = bf16[4,8,256,128]{3,1,2,0:T(8,128)(2,1)} copy(bf16[4,8,256,128]{3,2,1,0:T(8,128)(2,1)S(1)} %bitcast.115) | data formatting | bytes 4194304
  34.8 0.3 fusion.82
  35.0 0.5 collective-permute-start.2
  35.5 4.0 %collective-permute-start.3 = (f32[1,128]{1,0:T(1,128)S(1)}, f32[1,128]{1,0:T(1,128)S(1)}, u32[]{:S(2)}, u32[]{:S(2)}) collective-permute-start(f32[1,128]{1,0:T(1,128)S(1)} %get-tuple-element.24), channel_id=1, source_target_pairs={{1,0},{2,1},{3,2},{4,3},{5,4},{6,5},{7,6},{8,7},{9,8},{10,9},{11,1... | collective-permute-start | bytes 1544 | tf_op jit(solution)/shard_map/ppermute | solution.py:22
  39.6 1.2 collective-permute-done.2
  41.0 4.4 %collective-permute-start.5 = (f32[1,128]{1,0:T(1,128)S(1)}, f32[1,128]{1,0:T(1,128)S(1)}, u32[]{:S(2)}, u32[]{:S(2)}) collective-permute-start(f32[1,128]{1,0:T(1,128)S(1)} %get-tuple-element.20), channel_id=1, source_target_pairs={{1,0},{2,1},{3,2},{4,3},{5,4},{6,5},{7,6},{8,7},{9,8},{10,9},{11,1... | collective-permute-start | bytes 1544 | tf_op jit(solution)/shard_map/ppermute | solution.py:22
  45.5 1.1 collective-permute-done.4
  46.9 4.4 %collective-permute-start.7 = (f32[1,128]{1,0:T(1,128)S(1)}, f32[1,128]{1,0:T(1,128)S(1)}, u32[]{:S(2)}, u32[]{:S(2)}) collective-permute-start(f32[1,128]{1,0:T(1,128)S(1)} %get-tuple-element.16), channel_id=1, source_target_pairs={{1,0},{2,1},{3,2},{4,3},{5,4},{6,5},{7,6},{8,7},{9,8},{10,9},{11,1... | collective-permute-start | bytes 1544 | tf_op jit(solution)/shard_map/ppermute | solution.py:22
  51.5 1.1 collective-permute-done.6
  52.7 0.7 fusion.76
  53.4 1.0 fusion.29
  54.4 5.8 %all-to-all-start.2 = ((f32[16,16,128]{2,1,0:T(8,128)}), f32[16,16,128]{2,1,0:T(8,128)S(1)}, u32[]{:S(2)}, u32[]{:S(2)}) async-start(f32[16,16,128]{2,1,0:T(8,128)} %bitcast.6), calls=%async_computation.2 | async-start | bytes 262144 | tf_op jit(solution)/shard_map/all_to_all | solution.py:82
  60.2 4.4 %fusion.15 = f32[30,30]{0,1:T(8,128)S(1)} fusion(bf16[30,256,128]{2,1,0:T(8,128)(2,1)} %copy-done.1), kind=kOutput, calls=%fused_computation.14 | convolution fusion | flops 58982400 | bytes 1969680 | tf_op jit(solution)/shard_map/dot_general | solution.py:93
  64.6 3.5 %all-to-all-done.2 = f32[16,16,128]{2,1,0:T(8,128)S(1)} async-done(((f32[16,16,128]{2,1,0:T(8,128)}), f32[16,16,128]{2,1,0:T(8,128)S(1)}, u32[]{:S(2)}, u32[]{:S(2)}) %all-to-all-start.2) | async-done | bytes 131104 | tf_op jit(solution)/shard_map/all_to_all | solution.py:82
  68.2 2.1 %fusion.19 = f32[40]{0:T(128)S(1)} fusion(bf16[40,256,128]{2,1,0:T(8,128)(2,1)S(1)} %broadcast_multiply_fusion, bf16[256,128,1]{1,0,2:T(8,128)(2,1)S(1)} %bitcast.123), kind=kOutput, calls=%fused_computation.17 | convolution fusion | flops 2621440 | bytes 2687136 | tf_op jit(solution)/shard_map/dot_general | solution.py:92
  70.3 58.4 %all-reduce.9 = (f32[40,40]{0,1:T(8,128)S(1)}, f32[40]{0:T(128)S(1)}) all-reduce(f32[40,40]{0,1:T(8,128)S(1)} %fusion.12, f32[40]{0:T(128)S(1)} %fusion.19), channel_id=1, replica_groups=mesh['runs'=2,'tile'=16] {'tile'}, use_global_device_ids=true, to_apply=%region_2.0 | all-reduce | flops 1640 | bytes 13120 | tf_op jit(solution)/shard_map/psum | solution.py:96
  128.8 3.6 %cholesky.29 = f32[40,40]{1,0:T(8,128)S(1)} custom-call(f32[40,40]{1,0:T(8,128)S(1)} %fusion.64), custom_call_target="Cholesky" | custom-call | tf_op jit(solution)/shard_map/jit(cholesky)/cholesky | solution.py:37
  132.5 0.6 compare_reduce_fusion.1
  133.1 0.7 fusion.61
  133.8 3.1 %custom-call.16 = f32[1,40,40]{1,2,0:T(8,128)S(1)} custom-call(f32[1,40,40]{2,1,0:T(8,128)S(1)} %fusion.61), custom_call_target="InvertDiagBlocksLowerTriangular" | custom-call | tf_op jit(solution)/shard_map/triangular_solve | solution.py:39
  137.1 2.4 %fusion = f32[1,32768]{1,0:T(1,128)S(1)} fusion(bf16[5,8,256,128]{3,2,1,0:T(8,128)(2,1)S(1)} %bitcast.113, f32[40]{0:T(128)S(1)} %fusion.22), kind=kOutput, calls=%fused_computation | convolution fusion | flops 15728640 | bytes 2752672 | tf_op jit(solution)/shard_map/dot_general | solution.py:98
  139.6 1.7 convolution_bitcast_fusion.4
  141.4 57.8 %all-reduce.8 = (f32[30,30]{0,1:T(8,128)S(1)}, f32[30]{0:T(128)S(1)}) all-reduce(f32[30,30]{0,1:T(8,128)S(1)} %fusion.15, f32[30]{0:T(128)S(1)} %convolution_bitcast_fusion.4), channel_id=1, replica_groups=mesh['runs'=2,'tile'=16] {'tile'}, use_global_device_ids=true, to_apply=%region_6.7 | all-reduce | flops 930 | bytes 7440 | tf_op jit(solution)/shard_map/psum | solution.py:96
  199.3 2.7 %cholesky.61 = f32[30,30]{1,0:T(8,128)S(1)} custom-call(f32[30,30]{1,0:T(8,128)S(1)} %fusion.68), custom_call_target="Cholesky" | custom-call | tf_op jit(solution)/shard_map/jit(cholesky)/cholesky | solution.py:37
  202.1 0.6 compare_reduce_fusion
  202.7 0.7 fusion.65
  203.4 2.3 %custom-call.17 = f32[1,30,30]{1,2,0:T(8,128)S(1)} custom-call(f32[1,30,30]{2,1,0:T(8,128)S(1)} %fusion.65), custom_call_target="InvertDiagBlocksLowerTriangular" | custom-call | tf_op jit(solution)/shard_map/triangular_solve | solution.py:39
  206.0 3.5 %fusion.3 = f32[1,32768]{1,0:T(1,128)S(1)} fusion(bf16[5,8,256,128]{3,2,1,0:T(8,128)(2,1)} %bitcast.117, f32[40]{0:T(128)S(1)} %fusion.22), kind=kOutput, calls=%fused_computation.3 | convolution fusion | flops 2621480 | bytes 2752672 | tf_op jit(solution)/shard_map/dot_general | solution.py:105
  209.4 0.4 fusion.92
  209.8 0.8 fusion.25
  (49 shorter events, 2.1 us)
Async XLA Ops:
  1.3 33.4 %collective-permute-start = (f32[1,128]{1,0:T(1,128)S(1)}, f32[1,128]{1,0:T(1,128)S(1)}, u32[]{:S(2)}, u32[]{:S(2)}) collective-permute-start(f32[1,128]{1,0:T(1,128)S(1)} %get-tuple-element.27), channel_id=1, source_target_pairs={{0,1},{1,2},{2,3},{3,4},{4,5},{5,6},{6,7},{7,8},{8,9},{9,10},{10,1... | collective-permute-start | bytes 1544 | tf_op jit(solution)/shard_map/ppermute | solution.py:20
  1.8 32.9 %collective-permute-start.1 = (f32[1,128]{1,0:T(1,128)S(1)}, f32[1,128]{1,0:T(1,128)S(1)}, u32[]{:S(2)}, u32[]{:S(2)}) collective-permute-start(f32[1,128]{1,0:T(1,128)S(1)} %get-tuple-element.28), channel_id=1, source_target_pairs={{1,0},{2,1},{3,2},{4,3},{5,4},{6,5},{7,6},{8,7},{9,8},{10,9},{11,1... | collective-permute-start | bytes 1544 | tf_op jit(solution)/shard_map/ppermute | solution.py:22
  9.2 10.1 %all-to-all-start = ((f32[16,16,1]{1,2,0:T(1,128)}), f32[16,16,1]{1,2,0:T(1,128)S(1)}, u32[]{:S(2)}, u32[]{:S(2)}) async-start(f32[16,16,1]{1,2,0:T(1,128)} %bitcast.3), calls=%async_computation | async-start | bytes 16384 | tf_op jit(solution)/shard_map/all_to_all | solution.py:83
  19.2 15.5 %all-to-all-start.1 = ((f32[16,16,128]{2,1,0:T(8,128)}), f32[16,16,128]{2,1,0:T(8,128)S(1)}, u32[]{:S(2)}, u32[]{:S(2)}) async-start(f32[16,16,128]{2,1,0:T(8,128)} %bitcast.4), calls=%async_computation.1 | async-start | bytes 262144 | tf_op jit(solution)/shard_map/all_to_all | solution.py:71
  25.6 2.3 %copy-start.3 = (bf16[30,256,128]{2,1,0:T(8,128)(2,1)S(1)}, bf16[30,256,128]{2,1,0:T(8,128)(2,1)}, u32[]{:S(2)}) copy-start(bf16[30,256,128]{2,1,0:T(8,128)(2,1)} %param.18) | copy-start | bytes 5898244
  28.2 3.8 %copy-start.1 = (bf16[30,256,128]{2,1,0:T(8,128)(2,1)}, bf16[30,256,128]{2,1,0:T(8,128)(2,1)S(1)}, u32[]{:S(2)}) copy-start(bf16[30,256,128]{2,1,0:T(8,128)(2,1)S(1)} %broadcast_multiply_fusion.1) | copy-start | bytes 5898244
  32.0 2.7 %copy-start.4 = (f32[128,128]{1,0:T(8,128)S(1)}, f32[128,128]{1,0:T(8,128)}, u32[]{:S(2)}) copy-start(f32[128,128]{1,0:T(8,128)} %param.14) | copy-start | bytes 196612
  32.0 2.7 %copy-start.5 = (f32[128,128]{1,0:T(8,128)S(1)}, f32[128,128]{1,0:T(8,128)}, u32[]{:S(2)}) copy-start(f32[128,128]{1,0:T(8,128)} %param.12) | copy-start | bytes 196612
  32.0 2.7 %copy-start.8 = (f32[128,128]{1,0:T(8,128)S(1)}, f32[128,128]{1,0:T(8,128)}, u32[]{:S(2)}) copy-start(f32[128,128]{1,0:T(8,128)} %param.13) | copy-start | bytes 196612
  35.0 5.7 %collective-permute-start.2 = (f32[1,128]{1,0:T(1,128)S(1)}, f32[1,128]{1,0:T(1,128)S(1)}, u32[]{:S(2)}, u32[]{:S(2)}) collective-permute-start(f32[1,128]{1,0:T(1,128)S(1)} %get-tuple-element.23), channel_id=1, source_target_pairs={{0,1},{1,2},{2,3},{3,4},{4,5},{5,6},{6,7},{7,8},{8,9},{9,10},{10,1... | collective-permute-start | bytes 1544 | tf_op jit(solution)/shard_map/ppermute | solution.py:20
  35.5 5.3 %collective-permute-start.3 = (f32[1,128]{1,0:T(1,128)S(1)}, f32[1,128]{1,0:T(1,128)S(1)}, u32[]{:S(2)}, u32[]{:S(2)}) collective-permute-start(f32[1,128]{1,0:T(1,128)S(1)} %get-tuple-element.24), channel_id=1, source_target_pairs={{1,0},{2,1},{3,2},{4,3},{5,4},{6,5},{7,6},{8,7},{9,8},{10,9},{11,1... | collective-permute-start | bytes 1544 | tf_op jit(solution)/shard_map/ppermute | solution.py:22
  40.9 5.7 %collective-permute-start.4 = (f32[1,128]{1,0:T(1,128)S(1)}, f32[1,128]{1,0:T(1,128)S(1)}, u32[]{:S(2)}, u32[]{:S(2)}) collective-permute-start(f32[1,128]{1,0:T(1,128)S(1)} %get-tuple-element.19), channel_id=1, source_target_pairs={{0,1},{1,2},{2,3},{3,4},{4,5},{5,6},{6,7},{7,8},{8,9},{9,10},{10,1... | collective-permute-start | bytes 1544 | tf_op jit(solution)/shard_map/ppermute | solution.py:20
  41.0 5.7 %collective-permute-start.5 = (f32[1,128]{1,0:T(1,128)S(1)}, f32[1,128]{1,0:T(1,128)S(1)}, u32[]{:S(2)}, u32[]{:S(2)}) collective-permute-start(f32[1,128]{1,0:T(1,128)S(1)} %get-tuple-element.20), channel_id=1, source_target_pairs={{1,0},{2,1},{3,2},{4,3},{5,4},{6,5},{7,6},{8,7},{9,8},{10,9},{11,1... | collective-permute-start | bytes 1544 | tf_op jit(solution)/shard_map/ppermute | solution.py:22
  46.7 21.4 %copy-start.7 = (f32[256,128]{1,0:T(8,128)S(1)}, f32[256,128]{1,0:T(8,128)}, u32[]{:S(2)}) copy-start(f32[256,128]{1,0:T(8,128)} %param.11) | copy-start | bytes 393220
  46.9 5.7 %collective-permute-start.6 = (f32[1,128]{1,0:T(1,128)S(1)}, f32[1,128]{1,0:T(1,128)S(1)}, u32[]{:S(2)}, u32[]{:S(2)}) collective-permute-start(f32[1,128]{1,0:T(1,128)S(1)} %get-tuple-element.15), channel_id=1, source_target_pairs={{0,1},{1,2},{2,3},{3,4},{4,5},{5,6},{6,7},{7,8},{8,9},{9,10},{10,1... | collective-permute-start | bytes 1544 | tf_op jit(solution)/shard_map/ppermute | solution.py:20
  46.9 5.7 %collective-permute-start.7 = (f32[1,128]{1,0:T(1,128)S(1)}, f32[1,128]{1,0:T(1,128)S(1)}, u32[]{:S(2)}, u32[]{:S(2)}) collective-permute-start(f32[1,128]{1,0:T(1,128)S(1)} %get-tuple-element.16), channel_id=1, source_target_pairs={{1,0},{2,1},{3,2},{4,3},{5,4},{6,5},{7,6},{8,7},{9,8},{10,9},{11,1... | collective-permute-start | bytes 1544 | tf_op jit(solution)/shard_map/ppermute | solution.py:22
  53.4 16.9 %copy-start.6 = (f32[128,128]{1,0:T(8,128)}, f32[128,128]{1,0:T(8,128)S(1)}, u32[]{:S(2)}) copy-start(f32[128,128]{1,0:T(8,128)S(1)} %get-tuple-element.7) | copy-start | bytes 196612
  54.4 13.7 %all-to-all-start.2 = ((f32[16,16,128]{2,1,0:T(8,128)}), f32[16,16,128]{2,1,0:T(8,128)S(1)}, u32[]{:S(2)}, u32[]{:S(2)}) async-start(f32[16,16,128]{2,1,0:T(8,128)} %bitcast.6), calls=%async_computation.2 | async-start | bytes 262144 | tf_op jit(solution)/shard_map/all_to_all | solution.py:82
  136.8 2.8 %copy-start.2 = (bf16[4,8,256,128]{3,1,2,0:T(8,128)(2,1)S(1)}, bf16[4,8,256,128]{3,1,2,0:T(8,128)(2,1)}, u32[]{:S(2)}) copy-start(bf16[4,8,256,128]{3,1,2,0:T(8,128)(2,1)} %copy.53) | copy-start | bytes 6291460
  139.6 69.8 %copy-start = (bf16[4,8,256,128]{3,1,2,0:T(8,128)(2,1)S(1)}, bf16[4,8,256,128]{3,1,2,0:T(8,128)(2,1)}, u32[]{:S(2)}) copy-start(bf16[4,8,256,128]{3,1,2,0:T(8,128)(2,1)} %copy.55) | copy-start | bytes 6291460
where the time goes:
time: 211 us
  blocking collectives  116 us (55%)
  starting transfers between devices  33.6 us (16%)
  matrix products  20.9 us (10%)
  other arithmetic  20 us (9%)
  local copies, waits for them, and re-layouts  11 us (5%)
  waiting for transfers between devices  8 us (4%)
    psum x2, blocking collectives, local(): lax.psum((gram_cur, rhs_cur, gram_past), 'tile')  116 us
    ppermute x4, starting transfers between devices, padded_2(): lax.ppermute(head, axis, [((i + 1) % count, i) for i in range(count)])  17.9 us
    another operation x6, other arithmetic, solve_spd(): factor = jnp.linalg.cholesky(matrix)  7.73 us
    unnamed x22, local copies, waits for them, and re-layouts  7.61 us
    another operation x4, other arithmetic, solve_spd(): lax.linalg.triangular_solve(factor, inner, left_side=True, lower=True, tr...  6.64 us
    all_to_all x1, starting transfers between devices, local(): lax.all_to_all(outgoing, 'tile', split_axis=0, concat_axis=0, tiled=True)  5.78 us
    all_to_all x1, starting transfers between devices, local(): lax.all_to_all(fluid_press, 'tile', split_axis=0, concat_axis=0, tiled=True)  5.12 us
    dot_general x1, matrix products, local(): lax.dot_general(past_cols, past_cols, (((1,), (1,)), ((), ())), preferred...  4.43 us
  transfers between devices with their start and end apart: 11, of which 7 were waited for; matrix products, arithmetic and copies ran while one was open for 10% of the time, Pallas kernels for 0%

commit v1 on v0

v1 whole, which is shorter than its diff:
```python
import jax
import jax.numpy as jnp
from jax import lax
from jax.sharding import PartitionSpec as P

SUBSTEPS = 4


step_dt = 1.0
damping = 0.05


def tree_sum(value, axis):
    count = lax.axis_size(axis)
    if count & (count - 1):
        return lax.psum(value, axis)
    stride = 1
    while stride < count:
        value = value + lax.ppermute(value, axis, [(i, i ^ stride) for i in range(count)])
        stride *= 2
    return value


def with_halo(cells, width, axis):
    count = lax.axis_size(axis)
    below = lax.ppermute(cells[-width:], axis, [(i, (i + 1) % count) for i in range(count)])
    above = lax.ppermute(cells[:width], axis, [((i + 1) % count, i) for i in range(count)])
    return jnp.concatenate([below, cells, above], axis=0)


def sides(center):
    zero_col = jnp.zeros((center.shape[0], 1), jnp.float32)
    left = jnp.concatenate([zero_col, center[:, :-1]], 1)
    right = jnp.concatenate([center[:, 1:], zero_col], 1)
    return left + right


def solve_spd(factor, vector):
    inner = lax.linalg.triangular_solve(factor, vector[:, None], left_side=True, lower=True)
    outer = lax.linalg.triangular_solve(factor, inner, left_side=True, lower=True, transpose_a=True)
    return outer[:, 0]


def local(
    fluid_press,
    iterate,
    displace,
    velocity,
    stiffness,
    owners,
    diff_cur,
    step_cur,
    diff_past,
    step_past,
):
    high = lax.Precision.HIGHEST
    tile_count = lax.axis_size("tile")
    line_count = displace.shape[0]
    slot_count = iterate.shape[0]
    per_pair = slot_count // tile_count
    n_cur = diff_cur.shape[0]
    owner_list = owners[:, 0]
    onehot = (owner_list[:, None] == jnp.arange(tile_count, dtype=jnp.int32)[None, :]).astype(
        jnp.float32
    )
    below = (jnp.arange(line_count)[:, None] > jnp.arange(line_count)[None, :]).astype(jnp.float32)
    earlier = jnp.dot(below, onehot, precision=high)
    rank_in = jnp.sum(earlier * onehot, axis=1).astype(jnp.int32)
    slot_of = owner_list * per_pair + rank_in
    chooser = (slot_of[:, None] == jnp.arange(slot_count, dtype=jnp.int32)[None, :]).astype(
        jnp.float32
    )
    flags = jnp.sum(chooser, axis=0)
    mask = lax.all_to_all(flags, "tile", split_axis=0, concat_axis=0, tiled=True)
    mask_half = mask.astype(jnp.bfloat16)

    cols = jnp.concatenate(
        [
            (diff_cur * mask_half[None, :, None]).reshape(n_cur, -1),
            (diff_past * mask_half[None, :, None]).reshape(diff_past.shape[0], -1),
        ],
        axis=0,
    )
    gram = lax.dot_general(cols, cols, (((1,), (1,)), ((), ())), preferred_element_type=jnp.float32)
    gram = tree_sum(gram, "tile")
    gram_cur = gram[:n_cur, :n_cur]
    gram_past = gram[n_cur:, n_cur:]
    cross = gram[n_cur:, :n_cur]
    factor_cur = jnp.linalg.cholesky(gram_cur)
    factor_past = jnp.linalg.cholesky(gram_past)

    returned = lax.all_to_all(fluid_press, "tile", split_axis=0, concat_axis=0, tiled=True)
    pressure = jnp.dot(chooser, returned, precision=high)

    width = SUBSTEPS
    packed = with_halo(jnp.concatenate([displace, velocity, stiffness, pressure], axis=1), width, "tile")
    lanes = displace.shape[1]
    field = packed[:, :lanes]
    speed = packed[:, lanes : 2 * lanes]
    stiff = packed[:, 2 * lanes : 3 * lanes]
    press = packed[:, 3 * lanes :]
    for substep in range(SUBSTEPS):
        lapl = jnp.roll(field, 1, 0) + jnp.roll(field, -1, 0) + sides(field) - 4.0 * field
        speed = speed + step_dt * (stiff * lapl + press - damping * speed)
        field = field + step_dt * speed
    field = field[width : width + line_count]
    speed = speed[width : width + line_count]

    outgoing = jnp.dot(chooser.T, field, precision=high)
    x_tilde = lax.all_to_all(outgoing, "tile", split_axis=0, concat_axis=0, tiled=True)
    resid = (mask[:, None] * (x_tilde - iterate)).astype(jnp.bfloat16).reshape(-1)
    inner = tree_sum(jnp.dot(cols, resid, preferred_element_type=jnp.float32), "tile")
    rhs_cur = inner[:n_cur]
    rhs_past = inner[n_cur:]
    coeff = -solve_spd(factor_cur, rhs_cur)
    projected = rhs_past + jnp.dot(cross, coeff, precision=high)
    past = solve_spd(factor_past, projected)
    upd_cur = jnp.dot(
        coeff.astype(jnp.bfloat16),
        step_cur.reshape(step_cur.shape[0], -1),
        preferred_element_type=jnp.float32,
    )
    upd_past = jnp.dot(
        past.astype(jnp.bfloat16),
        step_past.reshape(step_past.shape[0], -1),
        preferred_element_type=jnp.float32,
    )
    update = (upd_cur - upd_past).reshape(x_tilde.shape)
    new_iterate = mask[:, None] * (x_tilde + update)
    return (new_iterate, field, speed)


def solution(mesh):
    placed = (
        P(("runs", "tile"), None),
        P(("runs", "tile"), None),
        P(("runs", "tile"), None),
        P(("runs", "tile"), None),
        P(("runs", "tile"), None),
        P(("runs", "tile"), None),
        P(None, ("runs", "tile"), None),
        P(None, ("runs", "tile"), None),
        P(None, ("runs", "tile"), None),
        P(None, ("runs", "tile"), None),
    )
    return jax.shard_map(
        local,
        mesh=mesh,
        in_specs=placed,
        out_specs=(P(("runs", "tile"), None), P(("runs", "tile"), None), P(("runs", "tile"), None)),
        check_vma=False,
    )
```

time: 211 us -> 97.8 us (0.46)
  blocking collectives: 116 us -> 13.6 us
  starting transfers between devices: 33.6 us -> 12 us
  waiting for transfers between devices: 8 us -> 29 us
  matrix products: 20.9 us -> 12.1 us
    psum x2 -> x0, blocking collectives: 116 us -> none  [local(): lax.psum((gram_cur, rhs_cur, gram_past), 'tile')]
    ppermute x8 -> x10, waiting for transfers between devices: 3.65 us -> 23.6 us  [the longest x8 15.1 us: tree_sum(): lax.ppermute(value, axis, [(i, i ^ stride) for i in range(count)])]
    ppermute x8 -> x10, starting transfers between devices: 19 us -> 4.49 us  [the longest x1 2.62 us: with_halo(): lax.ppermute(cells[:width], axis, [((i + 1) % count, i) for i in range(co...]
    all_to_all x0 -> x1, blocking collectives: none -> 13.6 us  [local(): lax.all_to_all(flags, 'tile', split_axis=0, concat_axis=0, tiled=True)]
    dot_general x5 -> x3, matrix products: 14.3 us -> 5.37 us  [the longest x1 3.66 us: local(): jnp.dot(cols, resid, preferred_element_type=jnp.float32)]
    all_to_all x1 -> x0, starting transfers between devices: 3.68 us -> none  [local(): lax.all_to_all(flags, 'tile', split_axis=0, concat_axis=0, tiled=True)]
    unnamed x22 -> x24, local copies, waits for them, and re-layouts: 7.61 us -> 7.5 us
  transfers between devices with their start and end apart: 11 -> 12, of which waited for: 7 -> 10; matrix products, arithmetic and copies ran while one was open for 10% -> 19% of each run, Pallas kernels for 0% -> 0%
where the time goes in v1:
time: 97.8 us; the launch traced here: 97.3 us
  waiting for transfers between devices  29 us (30%)
  other arithmetic  20 us (20%)
  blocking collectives  13.6 us (14%)
  matrix products  12.1 us (12%)
  starting transfers between devices  12 us (12%)
  local copies, waits for them, and re-layouts  9.61 us (10%)
  between operations  1.06 us (1%)
    ppermute x8, waiting for transfers between devices, tree_sum(): lax.ppermute(value, axis, [(i, i ^ stride) for i in range(count)])  15.1 us
    all_to_all x1, blocking collectives, local(): lax.all_to_all(flags, 'tile', split_axis=0, concat_axis=0, tiled=True)  13.6 us
    unnamed x24, local copies, waits for them, and re-layouts  7.5 us
    another operation x4, other arithmetic, solve_spd(): lax.linalg.triangular_solve(factor, inner, left_side=True, lower=True, tr...  6.68 us
    ppermute x1, waiting for transfers between devices, with_halo(): lax.ppermute(cells[-width:], axis, [(i, (i + 1) % count) for i in range(c...  4.6 us
    another operation x3, other arithmetic, local(): factor_cur = jnp.linalg.cholesky(gram_cur)  4.31 us
    ppermute x1, waiting for transfers between devices, with_halo(): lax.ppermute(cells[:width], axis, [((i + 1) % count, i) for i in range(co...  3.86 us
    all_to_all x1, starting transfers between devices, local(): lax.all_to_all(fluid_press, 'tile', split_axis=0, concat_axis=0, tiled=True)  3.79 us
  transfers between devices with their start and end apart: 12, of which 10 were waited for; matrix products, arithmetic and copies ran while one was open for 19% of the time, Pallas kernels for 0%

profile of v1, /device:TPU:0, one launch (start us, length us, event | category | flops | bytes accessed | tf_op | source)
XLA Modules:
  0.0 97.3 jit_solution(7167102422350808884)
XLA Ops:
  0.6 0.9 fusion.3
  1.5 0.7 fusion.54
  2.4 13.6 %all_to_all.33 = f32[16,16,1]{1,2,0:T(1,128)S(1)} all-to-all(f32[16,16,1]{1,2,0:T(1,128)S(1)} %bitcast.115), channel_id=1, replica_groups=mesh['runs'=2,'tile'=16] {'tile'}, dimensions={0} | all-to-all | bytes 2048 | tf_op jit(solution)/shard_map/all_to_all | solution.py:74
  16.0 0.5 broadcast.160
  16.5 0.7 reduce.15
  17.3 2.0 %broadcast_multiply_fusion = bf16[40,256,128]{2,1,0:T(8,128)(2,1)S(1)} fusion(bf16[40,256,128]{2,1,0:T(8,128)(2,1)} %param.16, bf16[256]{0:T(256)(128)(2,1)S(1)} %convert_element_type.39), kind=kLoop, calls=%fused_computation.4 | loop fusion | flops 1310720 | bytes 5243392 | tf_op jit(solution)/shard_map/mul | solution.py:79
  19.3 1.5 %bitcast_dynamic-update-slice_fusion = bf16[70,32768]{1,0:T(8,128)(2,1)S(1)} fusion(bf16[5,8,256,128]{3,2,1,0:T(8,128)(2,1)S(1)} %bitcast.105), kind=kLoop, calls=%fused_computation.3 | loop fusion | bytes 5242880
  21.1 0.3 pad.34
  21.4 1.4 %copy.57 = bf16[4,8,256,128]{3,1,2,0:T(8,128)(2,1)S(1)} copy(bf16[4,8,256,128]{3,2,1,0:T(8,128)(2,1)S(1)} %bitcast.108) | data formatting | bytes 4194304
  23.0 1.5 %fusion.77 = f32[70,70]{0,1:T(8,128)S(1)} fusion(bf16[70,32768]{1,0:T(8,128)(2,1)S(1)} %constant_dynamic-update-slice_fusion), kind=kOutput, calls=%fused_computation.111 | convolution fusion | flops 321126400 | bytes 4607120 | tf_op jit(solution)/shard_map/dot_general | solution.py:84
  24.4 0.8 copy-done
  25.3 1.2 %collective-permute-done.2 = f32[70,70]{0,1:T(8,128)S(1)} collective-permute-done((f32[70,70]{0,1:T(8,128)S(1)}, f32[70,70]{0,1:T(8,128)S(1)}, u32[]{:S(2)}, u32[]{:S(2)}) %collective-permute-start.2) | collective-permute-done | bytes 19632 | tf_op jit(solution)/shard_map/ppermute | solution.py:19
  26.5 0.5 collective-permute-start.3
  27.0 3.5 %collective-permute-done.3 = f32[70,70]{0,1:T(8,128)S(1)} collective-permute-done((f32[70,70]{0,1:T(8,128)S(1)}, f32[70,70]{0,1:T(8,128)S(1)}, u32[]{:S(2)}, u32[]{:S(2)}) %collective-permute-start.3) | collective-permute-done | bytes 19632 | tf_op jit(solution)/shard_map/ppermute | solution.py:19
  30.5 0.5 collective-permute-start.4
  31.0 3.4 %collective-permute-done.4 = f32[70,70]{0,1:T(8,128)S(1)} collective-permute-done((f32[70,70]{0,1:T(8,128)S(1)}, f32[70,70]{0,1:T(8,128)S(1)}, u32[]{:S(2)}, u32[]{:S(2)}) %collective-permute-start.4) | collective-permute-done | bytes 19632 | tf_op jit(solution)/shard_map/ppermute | solution.py:19
  34.4 0.5 collective-permute-start.5
  35.0 3.8 %all-to-all-start.1 = ((f32[16,16,128]{2,1,0:T(8,128)}), f32[16,16,128]{2,1,0:T(8,128)S(1)}, u32[]{:S(2)}, u32[]{:S(2)}) async-start(f32[16,16,128]{2,1,0:T(8,128)} %bitcast.4), calls=%async_computation.1 | async-start | bytes 262144 | tf_op jit(solution)/shard_map/all_to_all | solution.py:92
  39.1 0.3 pad.35
  39.4 1.4 %copy.59 = bf16[4,8,256,128]{3,1,2,0:T(8,128)(2,1)S(1)} copy(bf16[4,8,256,128]{3,2,1,0:T(8,128)(2,1)S(1)} %bitcast.109) | data formatting | bytes 4194304
  41.0 3.7 %cholesky.29 = f32[40,40]{1,0:T(8,128)S(1)} custom-call(f32[40,40]{1,0:T(8,128)S(1)} %copy.51), custom_call_target="Cholesky" | custom-call | tf_op jit(solution)/shard_map/jit(cholesky)/cholesky | solution.py:89
  44.9 1.8 %all-to-all-done.1 = f32[16,16,128]{2,1,0:T(8,128)S(1)} async-done(((f32[16,16,128]{2,1,0:T(8,128)}), f32[16,16,128]{2,1,0:T(8,128)S(1)}, u32[]{:S(2)}, u32[]{:S(2)}) %all-to-all-start.1) | async-done | bytes 131104 | tf_op jit(solution)/shard_map/all_to_all | solution.py:92
  46.7 0.3 fusion.35
  47.1 2.6 %collective-permute-start.1 = (f32[4,512]{0,1:T(8,128)S(1)}, f32[4,512]{0,1:T(8,128)S(1)}, u32[]{:S(2)}, u32[]{:S(2)}) collective-permute-start(f32[4,512]{0,1:T(8,128)S(1)} %get-tuple-element.26), channel_id=1, source_target_pairs={{1,0},{2,1},{3,2},{4,3},{5,4},{6,5},{7,6},{8,7},{9,8},{10,9},{11,1... | collective-permute-start | bytes 24584 | tf_op jit(solution)/shard_map/ppermute | solution.py:27
  49.8 3.9 %collective-permute-done.1 = f32[4,512]{0,1:T(8,128)S(1)} collective-permute-done((f32[4,512]{0,1:T(8,128)S(1)}, f32[4,512]{0,1:T(8,128)S(1)}, u32[]{:S(2)}, u32[]{:S(2)}) %collective-permute-start.1) | collective-permute-done | bytes 8224 | tf_op jit(solution)/shard_map/ppermute | solution.py:27
  53.7 4.6 %collective-permute-done = f32[4,512]{0,1:T(8,128)S(1)} collective-permute-done((f32[4,512]{0,1:T(8,128)S(1)}, f32[4,512]{0,1:T(8,128)S(1)}, u32[]{:S(2)}, u32[]{:S(2)}) %collective-permute-start) | collective-permute-done | bytes 8224 | tf_op jit(solution)/shard_map/ppermute | solution.py:26
  58.3 0.3 pad_maximum_fusion
  60.1 1.0 %fusion.36 = f32[256,128]{1,0:T(8,128)} fusion(f32[128,128]{0,1:T(8,128)S(1)} %get-tuple-element.28, s32[128]{0:T(128)S(1)} %fusion.54), kind=kOutput, calls=%fused_computation.57 | convolution fusion | flops 50397184 | bytes 197120 | tf_op jit(solution)/shard_map/dot_general | solution.py:109
  61.1 3.7 %all-to-all-start.2 = ((f32[16,16,128]{2,1,0:T(8,128)}), f32[16,16,128]{2,1,0:T(8,128)S(1)}, u32[]{:S(2)}, u32[]{:S(2)}) async-start(f32[16,16,128]{2,1,0:T(8,128)} %bitcast.6), calls=%async_computation.2 | async-start | bytes 262144 | tf_op jit(solution)/shard_map/all_to_all | solution.py:110
  64.8 0.6 compare_reduce_fusion.1
  65.4 2.7 %cholesky.61 = f32[30,30]{1,0:T(8,128)S(1)} custom-call(f32[30,30]{1,0:T(8,128)S(1)} %fusion.48), custom_call_target="Cholesky" | custom-call | tf_op jit(solution)/shard_map/jit(cholesky)/cholesky | solution.py:90
  68.1 0.7 fusion.40
  68.8 3.7 %all-to-all-done.2 = f32[16,16,128]{2,1,0:T(8,128)S(1)} async-done(((f32[16,16,128]{2,1,0:T(8,128)}), f32[16,16,128]{2,1,0:T(8,128)S(1)}, u32[]{:S(2)}, u32[]{:S(2)}) %all-to-all-start.2) | async-done | bytes 131104 | tf_op jit(solution)/shard_map/all_to_all | solution.py:110
  72.7 3.7 %convolution_bitcast_fusion = f32[70]{0:T(128)S(1)} fusion(bf16[70,32768]{1,0:T(8,128)(2,1)} %copy-done, bf16[32768,1]{0,1:T(2,128)(2,1)S(1)} %reshape.88), kind=kOutput, calls=%fused_computation.7 | convolution fusion | flops 4587520 | bytes 4653336 | tf_op jit(solution)/shard_map/dot_general | solution.py:112
  76.4 1.1 %collective-permute-done.6 = f32[70]{0:T(128)S(1)} collective-permute-done((f32[70]{0:T(128)S(1)}, f32[70]{0:T(128)S(1)}, u32[]{:S(2)}, u32[]{:S(2)}) %collective-permute-start.6) | collective-permute-done | bytes 312 | tf_op jit(solution)/shard_map/ppermute | solution.py:19
  77.5 0.6 compare_reduce_fusion
  78.1 2.9 %collective-permute-done.7 = f32[70]{0:T(128)S(1)} collective-permute-done((f32[70]{0:T(128)S(1)}, f32[70]{0:T(128)S(1)}, u32[]{:S(2)}, u32[]{:S(2)}) %collective-permute-start.7) | collective-permute-done | bytes 312 | tf_op jit(solution)/shard_map/ppermute | solution.py:19
  81.1 0.7 fusion.45
  81.7 2.9 %collective-permute-done.8 = f32[70]{0:T(128)S(1)} collective-permute-done((f32[70]{0:T(128)S(1)}, f32[70]{0:T(128)S(1)}, u32[]{:S(2)}, u32[]{:S(2)}) %collective-permute-start.8) | collective-permute-done | bytes 312 | tf_op jit(solution)/shard_map/ppermute | solution.py:19
  84.6 0.3 collective-permute-start.9
  85.0 3.1 %custom-call.16 = f32[1,40,40]{1,2,0:T(8,128)S(1)} custom-call(f32[1,40,40]{2,1,0:T(8,128)S(1)} %fusion.40), custom_call_target="InvertDiagBlocksLowerTriangular" | custom-call | tf_op jit(solution)/shard_map/triangular_solve | solution.py:40
  88.0 2.3 %custom-call.17 = f32[1,30,30]{1,2,0:T(8,128)S(1)} custom-call(f32[1,30,30]{2,1,0:T(8,128)S(1)} %fusion.45), custom_call_target="InvertDiagBlocksLowerTriangular" | custom-call | tf_op jit(solution)/shard_map/triangular_solve | solution.py:40
  90.3 0.8 copy.53
  91.1 0.7 copy.54
  92.1 0.2 convolution_bitcast_fusion.3
  92.3 3.5 %fusion = f32[1,32768]{1,0:T(1,128)S(1)} fusion(bf16[5,8,256,128]{3,2,1,0:T(8,128)(2,1)} %bitcast.110, f32[40]{0:T(128)S(1)} %fusion.4), kind=kOutput, calls=%fused_computation | convolution fusion | flops 2621480 | bytes 2752672 | tf_op jit(solution)/shard_map/dot_general | solution.py:118
  96.1 0.4 fusion.78
  96.5 0.8 fusion.31
  (72 shorter events, 3.8 us)
Async XLA Ops:
  19.3 1.5 %copy-start.1 = (bf16[30,256,128]{2,1,0:T(8,128)(2,1)S(1)}, bf16[30,256,128]{2,1,0:T(8,128)(2,1)}, u32[]{:S(2)}) copy-start(bf16[30,256,128]{2,1,0:T(8,128)(2,1)} %param.18) | copy-start | bytes 5898244
  22.9 2.4 %copy-start = (bf16[70,32768]{1,0:T(8,128)(2,1)}, bf16[70,32768]{1,0:T(8,128)(2,1)S(1)}, u32[]{:S(2)}) copy-start(bf16[70,32768]{1,0:T(8,128)(2,1)S(1)} %constant_dynamic-update-slice_fusion) | copy-start | bytes 13762564
  22.9 15.9 %copy-start.4 = (f32[128,128]{1,0:T(8,128)S(1)}, f32[128,128]{1,0:T(8,128)}, u32[]{:S(2)}) copy-start(f32[128,128]{1,0:T(8,128)} %param.14) | copy-start | bytes 196612
  22.9 16.0 %copy-start.5 = (f32[128,128]{1,0:T(8,128)S(1)}, f32[128,128]{1,0:T(8,128)}, u32[]{:S(2)}) copy-start(f32[128,128]{1,0:T(8,128)} %param.13) | copy-start | bytes 196612
  22.9 16.0 %copy-start.6 = (f32[128,128]{1,0:T(8,128)S(1)}, f32[128,128]{1,0:T(8,128)}, u32[]{:S(2)}) copy-start(f32[128,128]{1,0:T(8,128)} %param.12) | copy-start | bytes 196612
  22.9 16.1 %copy-start.2 = (bf16[30,256,128]{2,1,0:T(8,128)(2,1)S(1)}, bf16[30,256,128]{2,1,0:T(8,128)(2,1)}, u32[]{:S(2)}) copy-start(bf16[30,256,128]{2,1,0:T(8,128)(2,1)} %param.19) | copy-start | bytes 5898244
  25.3 1.2 %collective-permute-start.2 = (f32[70,70]{0,1:T(8,128)S(1)}, f32[70,70]{0,1:T(8,128)S(1)}, u32[]{:S(2)}, u32[]{:S(2)}) collective-permute-start(f32[70,70]{0,1:T(8,128)S(1)} %fusion.77), channel_id=1, source_target_pairs={{0,1},{1,0},{2,3},{3,2},{4,5},{5,4},{6,7},{7,6},{8,9},{9,8},{10,11... | collective-permute-start | bytes 58808 | tf_op jit(solution)/shard_map/ppermute | solution.py:19
  26.5 4.0 %collective-permute-start.3 = (f32[70,70]{0,1:T(8,128)S(1)}, f32[70,70]{0,1:T(8,128)S(1)}, u32[]{:S(2)}, u32[]{:S(2)}) collective-permute-start(f32[70,70]{0,1:T(8,128)S(1)} %add.173), channel_id=1, source_target_pairs={{0,2},{1,3},{2,0},{3,1},{4,6},{5,7},{6,4},{7,5},{8,10},{9,11},{10,... | collective-permute-start | bytes 58808 | tf_op jit(solution)/shard_map/ppermute | solution.py:19
  30.5 4.0 %collective-permute-start.4 = (f32[70,70]{0,1:T(8,128)S(1)}, f32[70,70]{0,1:T(8,128)S(1)}, u32[]{:S(2)}, u32[]{:S(2)}) collective-permute-start(f32[70,70]{0,1:T(8,128)S(1)} %add.174), channel_id=1, source_target_pairs={{0,4},{1,5},{2,6},{3,7},{4,0},{5,1},{6,2},{7,3},{8,12},{9,13},{10,... | collective-permute-start | bytes 58808 | tf_op jit(solution)/shard_map/ppermute | solution.py:19
  34.4 6.3 %collective-permute-start.5 = (f32[70,70]{0,1:T(8,128)S(1)}, f32[70,70]{0,1:T(8,128)S(1)}, u32[]{:S(2)}, u32[]{:S(2)}) collective-permute-start(f32[70,70]{0,1:T(8,128)S(1)} %add.175), channel_id=1, source_target_pairs={{0,8},{1,9},{2,10},{3,11},{4,12},{5,13},{6,14},{7,15},{8,0},{9,1},... | collective-permute-start | bytes 58808 | tf_op jit(solution)/shard_map/ppermute | solution.py:19
  35.0 11.7 %all-to-all-start.1 = ((f32[16,16,128]{2,1,0:T(8,128)}), f32[16,16,128]{2,1,0:T(8,128)S(1)}, u32[]{:S(2)}, u32[]{:S(2)}) async-start(f32[16,16,128]{2,1,0:T(8,128)} %bitcast.4), calls=%async_computation.1 | async-start | bytes 262144 | tf_op jit(solution)/shard_map/all_to_all | solution.py:92
  47.1 6.5 %collective-permute-start.1 = (f32[4,512]{0,1:T(8,128)S(1)}, f32[4,512]{0,1:T(8,128)S(1)}, u32[]{:S(2)}, u32[]{:S(2)}) collective-permute-start(f32[4,512]{0,1:T(8,128)S(1)} %get-tuple-element.26), channel_id=1, source_target_pairs={{1,0},{2,1},{3,2},{4,3},{5,4},{6,5},{7,6},{8,7},{9,8},{10,9},{11,1... | collective-permute-start | bytes 24584 | tf_op jit(solution)/shard_map/ppermute | solution.py:27
  49.8 8.5 %collective-permute-start = (f32[4,512]{0,1:T(8,128)S(1)}, f32[4,512]{0,1:T(8,128)S(1)}, u32[]{:S(2)}, u32[]{:S(2)}) collective-permute-start(f32[4,512]{0,1:T(8,128)S(1)} %get-tuple-element.25), channel_id=1, source_target_pairs={{0,1},{1,2},{2,3},{3,4},{4,5},{5,6},{6,7},{7,8},{8,9},{9,10},{10,1... | collective-permute-start | bytes 24584 | tf_op jit(solution)/shard_map/ppermute | solution.py:26
  59.4 13.1 %copy-start.3 = (f32[256,128]{1,0:T(8,128)S(1)}, f32[256,128]{1,0:T(8,128)}, u32[]{:S(2)}) copy-start(f32[256,128]{1,0:T(8,128)} %param.11) | copy-start | bytes 393220
  61.1 11.4 %all-to-all-start.2 = ((f32[16,16,128]{2,1,0:T(8,128)}), f32[16,16,128]{2,1,0:T(8,128)S(1)}, u32[]{:S(2)}, u32[]{:S(2)}) async-start(f32[16,16,128]{2,1,0:T(8,128)} %bitcast.6), calls=%async_computation.2 | async-start | bytes 262144 | tf_op jit(solution)/shard_map/all_to_all | solution.py:110
  76.3 1.2 %collective-permute-start.6 = (f32[70]{0:T(128)S(1)}, f32[70]{0:T(128)S(1)}, u32[]{:S(2)}, u32[]{:S(2)}) collective-permute-start(f32[70]{0:T(128)S(1)} %convolution_bitcast_fusion), channel_id=1, source_target_pairs={{0,1},{1,0},{2,3},{3,2},{4,5},{5,4},{6,7},{7,6},{8,9},{9,8},{10,11... | collective-permute-start | bytes 848 | tf_op jit(solution)/shard_map/ppermute | solution.py:19
  77.5 3.6 %collective-permute-start.7 = (f32[70]{0:T(128)S(1)}, f32[70]{0:T(128)S(1)}, u32[]{:S(2)}, u32[]{:S(2)}) collective-permute-start(f32[70]{0:T(128)S(1)} %add.178), channel_id=1, source_target_pairs={{0,2},{1,3},{2,0},{3,1},{4,6},{5,7},{6,4},{7,5},{8,10},{9,11},{10,... | collective-permute-start | bytes 848 | tf_op jit(solution)/shard_map/ppermute | solution.py:19
  81.1 3.6 %collective-permute-start.8 = (f32[70]{0:T(128)S(1)}, f32[70]{0:T(128)S(1)}, u32[]{:S(2)}, u32[]{:S(2)}) collective-permute-start(f32[70]{0:T(128)S(1)} %add.179), channel_id=1, source_target_pairs={{0,4},{1,5},{2,6},{3,7},{4,0},{5,1},{6,2},{7,3},{8,12},{9,13},{10,... | collective-permute-start | bytes 848 | tf_op jit(solution)/shard_map/ppermute | solution.py:19
  84.6 7.2 %collective-permute-start.9 = (f32[70]{0:T(128)S(1)}, f32[70]{0:T(128)S(1)}, u32[]{:S(2)}, u32[]{:S(2)}) collective-permute-start(f32[70]{0:T(128)S(1)} %add.180), channel_id=1, source_target_pairs={{0,8},{1,9},{2,10},{3,11},{4,12},{5,13},{6,14},{7,15},{8,0},{9,1},... | collective-permute-start | bytes 848 | tf_op jit(solution)/shard_map/ppermute | solution.py:19

commit v2 on v1

--- a/solution.py
+++ b/solution.py
@@ -21,11 +21,11 @@
     return value
 
 
-def with_halo(cells, width, axis):
+def halo_pair(cells, width, axis):
     count = lax.axis_size(axis)
     below = lax.ppermute(cells[-width:], axis, [(i, (i + 1) % count) for i in range(count)])
     above = lax.ppermute(cells[:width], axis, [((i + 1) % count, i) for i in range(count)])
-    return jnp.concatenate([below, cells, above], axis=0)
+    return below, above
 
 
 def sides(center):
@@ -35,10 +35,16 @@
     return left + right
 
 
-def solve_spd(factor, vector):
-    inner = lax.linalg.triangular_solve(factor, vector[:, None], left_side=True, lower=True)
-    outer = lax.linalg.triangular_solve(factor, inner, left_side=True, lower=True, transpose_a=True)
-    return outer[:, 0]
+def inverse_factor(matrix):
+    factor = jnp.linalg.cholesky(matrix)
+    eye = jnp.eye(matrix.shape[0], dtype=matrix.dtype)
+    return lax.linalg.triangular_solve(factor, eye, left_side=True, lower=True)
+
+
+def solve_spd(inverse, vector):
+    high = lax.Precision.HIGHEST
+    inner = jnp.dot(inverse, vector, precision=high)
+    return jnp.dot(inverse.T, inner, precision=high)
 
 
 def local(
@@ -71,7 +77,18 @@
         jnp.float32
     )
     flags = jnp.sum(chooser, axis=0)
-    mask = lax.all_to_all(flags, "tile", split_axis=0, concat_axis=0, tiled=True)
+    lanes = fluid_press.shape[1]
+    width = SUBSTEPS
+
+    edge = jnp.concatenate([displace, velocity, stiffness], axis=1)
+    edge_below, edge_above = halo_pair(edge, width, "tile")
+
+    flag_rows = jnp.zeros((tile_count, 1, lanes), jnp.float32)
+    flag_rows = flag_rows.at[:, 0, :per_pair].set(flags.reshape(tile_count, per_pair))
+    sent = jnp.concatenate([fluid_press.reshape(tile_count, per_pair, lanes), flag_rows], axis=1)
+    got = lax.all_to_all(sent, "tile", split_axis=0, concat_axis=0, tiled=True)
+    returned = got[:, :per_pair, :].reshape(slot_count, lanes)
+    mask = got[:, per_pair, :per_pair].reshape(slot_count)
     mask_half = mask.astype(jnp.bfloat16)
 
     cols = jnp.concatenate(
@@ -83,18 +100,20 @@
     )
     gram = lax.dot_general(cols, cols, (((1,), (1,)), ((), ())), preferred_element_type=jnp.float32)
     gram = tree_sum(gram, "tile")
-    gram_cur = gram[:n_cur, :n_cur]
-    gram_past = gram[n_cur:, n_cur:]
     cross = gram[n_cur:, :n_cur]
-    factor_cur = jnp.linalg.cholesky(gram_cur)
-    factor_past = jnp.linalg.cholesky(gram_past)
+    inv_cur = inverse_factor(gram[:n_cur, :n_cur])
+    inv_past = inverse_factor(gram[n_cur:, n_cur:])
 
-    returned = lax.all_to_all(fluid_press, "tile", split_axis=0, concat_axis=0, tiled=True)
     pressure = jnp.dot(chooser, returned, precision=high)
-
-    width = SUBSTEPS
-    packed = with_halo(jnp.concatenate([displace, velocity, stiffness, pressure], axis=1), width, "tile")
-    lanes = displace.shape[1]
+    press_below, press_above = halo_pair(pressure, width, "tile")
+    packed = jnp.concatenate(
+        [
+            jnp.concatenate([edge_below, press_below], axis=1),
+            jnp.concatenate([edge, pressure], axis=1),
+            jnp.concatenate([edge_above, press_above], axis=1),
+        ],
+        axis=0,
+    )
     field = packed[:, :lanes]
     speed = packed[:, lanes : 2 * lanes]
     stiff = packed[:, 2 * lanes : 3 * lanes]
@@ -112,9 +131,9 @@
     inner = tree_sum(jnp.dot(cols, resid, preferred_element_type=jnp.float32), "tile")
     rhs_cur = inner[:n_cur]
     rhs_past = inner[n_cur:]
-    coeff = -solve_spd(factor_cur, rhs_cur)
+    coeff = -solve_spd(inv_cur, rhs_cur)
     projected = rhs_past + jnp.dot(cross, coeff, precision=high)
-    past = solve_spd(factor_past, projected)
+    past = solve_spd(inv_past, projected)
     upd_cur = jnp.dot(
         coeff.astype(jnp.bfloat16),
         step_cur.reshape(step_cur.shape[0], -1),

time: 97.8 us -> 84.8 us (0.87)
  waiting for transfers between devices: 29 us -> 11.3 us
  starting transfers between devices: 12 us -> 27.5 us
  blocking collectives: 13.6 us -> 0 us
  other arithmetic: 20 us -> 21.2 us
  local copies, waits for them, and re-layouts: 9.61 us -> 10.7 us
    all_to_all x1 -> x0, blocking collectives: 13.6 us -> none  [local(): lax.all_to_all(flags, 'tile', split_axis=0, concat_axis=0, tiled=True)]
    ppermute x2 -> x4, waiting for transfers between devices: 8.47 us -> 0.01 us  [the longest x2 0.01 us: halo_pair(): lax.ppermute(cells[-width:], axis, [(i, (i + 1) % count) for i in range(c...]
    ppermute x8, starting transfers between devices: 1.87 us -> 8.22 us  [tree_sum(): lax.ppermute(value, axis, [(i, i ^ stride) for i in range(count)])]
    ppermute x2 -> x4, starting transfers between devices: 2.62 us -> 7.03 us  [the longest x2 6.56 us: halo_pair(): lax.ppermute(cells[:width], axis, [((i + 1) % count, i) for i in range(co...]
    ppermute x8, waiting for transfers between devices: 15.1 us -> 11.3 us  [tree_sum(): lax.ppermute(value, axis, [(i, i ^ stride) for i in range(count)])]
    all_to_all x1, waiting for transfers between devices: 3.65 us -> 0.01 us  [local(): lax.all_to_all(outgoing, 'tile', split_axis=0, concat_axis=0, tiled=True)]
    all_to_all x1, starting transfers between devices: 3.79 us -> 7.41 us  [local(): got = lax.all_to_all(sent, 'tile', split_axis=0, concat_axis=0, tiled=True)]
    all_to_all x1, waiting for transfers between devices: 1.79 us -> 0.01 us  [local(): got = lax.all_to_all(sent, 'tile', split_axis=0, concat_axis=0, tiled=True)]
  transfers between devices with their start and end apart: 12 -> 14, of which waited for: 10 -> 6; matrix products, arithmetic and copies ran while one was open for 19% -> 36% of each run, Pallas kernels for 0% -> 0%
where the time goes in v2:
time: 84.8 us; the launch traced here: 84.2 us
  starting transfers between devices  27.5 us (32%)
  other arithmetic  21.2 us (25%)
  matrix products  12.4 us (15%)
  waiting for transfers between devices  11.3 us (13%)
  local copies, waits for them, and re-layouts  10.7 us (13%)
  between operations  1.07 us (1%)
    ppermute x8, waiting for transfers between devices, tree_sum(): lax.ppermute(value, axis, [(i, i ^ stride) for i in range(count)])  11.3 us
    unnamed x21, local copies, waits for them, and re-layouts  8.69 us
    ppermute x8, starting transfers between devices, tree_sum(): lax.ppermute(value, axis, [(i, i ^ stride) for i in range(count)])  8.22 us
    another operation x6, other arithmetic, inverse_factor(): factor = jnp.linalg.cholesky(matrix)  7.82 us
    all_to_all x1, starting transfers between devices, local(): got = lax.all_to_all(sent, 'tile', split_axis=0, concat_axis=0, tiled=True)  7.41 us
    another operation x4, other arithmetic, inverse_factor(): return lax.linalg.triangular_solve(factor, eye, left_side=True, lower=True)  6.69 us
    ppermute x2, starting transfers between devices, halo_pair(): lax.ppermute(cells[:width], axis, [((i + 1) % count, i) for i in range(co...  6.56 us
    all_to_all x1, starting transfers between devices, local(): lax.all_to_all(outgoing, 'tile', split_axis=0, concat_axis=0, tiled=True)  4.87 us
  transfers between devices with their start and end apart: 14, of which 6 were waited for; matrix products, arithmetic and copies ran while one was open for 36% of the time, Pallas kernels for 0%

profile of v2, /device:TPU:0, one launch (start us, length us, event | category | flops | bytes accessed | tf_op | source)
XLA Modules:
  0.0 84.2 jit_solution(12243154680060657807)
XLA Ops:
  0.6 0.9 %fusion.3 = f32[128]{0:T(128)S(1)} fusion(s32[128]{0:T(128)} %bitcast.118), kind=kOutput, calls=%fused_computation.6 | convolution fusion | flops 548736 | bytes 1024 | tf_op jit(solution)/shard_map/dot_general | solution.py:73
  1.5 0.7 fusion.54
  2.4 1.6 %select_maximum_fusion = f32[16,17,128]{2,1,0:T(8,128)} fusion(f32[16,1,16]{2,1,0:T(1,128)S(1)} %reshape.105, f32[16,16,128]{2,1,0:T(8,128)} %bitcast.117), kind=kLoop, calls=%fused_computation.18 | loop fusion | flops 104448 | bytes 271360 | tf_op jit(solution)/shard_map/concatenate | solution.py:88
  4.0 7.4 %all-to-all-start = ((f32[16,17,128]{2,1,0:T(8,128)}), f32[16,17,128]{2,1,0:T(8,128)S(1)}, u32[]{:S(2)}, u32[]{:S(2)}) async-start(f32[16,17,128]{2,1,0:T(8,128)} %select_maximum_fusion), calls=%async_computation | async-start | bytes 393216 | tf_op jit(solution)/shard_map/all_to_all | solution.py:89
  11.4 0.8 %constant_dynamic-update-slice_fusion.2 = f32[128,384]{1,0:T(8,128)S(1)} fusion(f32[128,128]{1,0:T(8,128)} %param.14), kind=kLoop, calls=%fused_computation.85 | loop fusion | bytes 131072
  12.3 0.8 %constant_dynamic-update-slice_fusion.1 = f32[128,384]{1,0:T(8,128)S(1)} fusion(f32[128,384]{1,0:T(8,128)S(1)} %constant_dynamic-update-slice_fusion.2, f32[128,128]{1,0:T(8,128)} %param.15), kind=kLoop, calls=%fused_computation.84 | loop fusion | bytes 131072
  13.1 0.8 %constant_dynamic-update-slice_fusion = f32[128,384]{1,0:T(8,128)S(1)} fusion(f32[128,384]{1,0:T(8,128)S(1)} %constant_dynamic-update-slice_fusion.1, f32[128,128]{1,0:T(8,128)} %param.16), kind=kLoop, calls=%fused_computation.83 | loop fusion | bytes 131072 | tf_op jit(solution)/shard_map/concatenate | solution.py:83
  13.9 0.5 collective-permute-start
  14.4 4.0 %collective-permute-start.2 = (f32[4,384]{1,0:T(4,128)S(1)}, f32[4,384]{1,0:T(4,128)S(1)}, u32[]{:S(2)}, u32[]{:S(2)}) collective-permute-start(f32[4,384]{1,0:T(4,128)S(1)} %get-tuple-element.28), channel_id=1, source_target_pairs={{1,0},{2,1},{3,2},{4,3},{5,4},{6,5},{7,6},{8,7},{9,8},{10,9},{11,1... | collective-permute-start | bytes 18440 | tf_op jit(solution)/shard_map/ppermute | solution.py:27
  18.4 1.9 %pad.41 = bf16[32,256,128]{2,1,0:T(8,128)(2,1)S(1)} pad(bf16[30,256,128]{2,1,0:T(8,128)(2,1)} %param.21, bf16[]{:T(256)} %constant.151), padding=0_2x0_0x0_0 | pad | bytes 4063234
  20.3 1.4 %copy.27 = bf16[4,8,256,128]{3,1,2,0:T(8,128)(2,1)S(1)} copy(bf16[4,8,256,128]{3,2,1,0:T(8,128)(2,1)S(1)} %bitcast.111) | data formatting | bytes 4194304
  21.7 0.3 fusion.11
  22.0 2.5 %collective-permute-start.3 = (f32[4,128]{1,0:T(4,128)S(1)}, f32[4,128]{1,0:T(4,128)S(1)}, u32[]{:S(2)}, u32[]{:S(2)}) collective-permute-start(f32[4,128]{1,0:T(4,128)S(1)} %get-tuple-element.48), channel_id=1, source_target_pairs={{1,0},{2,1},{3,2},{4,3},{5,4},{6,5},{7,6},{8,7},{9,8},{10,9},{11,1... | collective-permute-start | bytes 6152 | tf_op jit(solution)/shard_map/ppermute | solution.py:27
  24.7 2.0 %broadcast_multiply_fusion = bf16[40,256,128]{2,1,0:T(8,128)(2,1)S(1)} fusion(bf16[40,256,128]{2,1,0:T(8,128)(2,1)} %param.18, bf16[256]{0:T(256)(128)(2,1)S(1)} %convert_element_type.39), kind=kLoop, calls=%fused_computation.4 | loop fusion | flops 1310720 | bytes 5243392 | tf_op jit(solution)/shard_map/mul | solution.py:96
  26.7 1.5 %bitcast_dynamic-update-slice_fusion = bf16[70,32768]{1,0:T(8,128)(2,1)S(1)} fusion(bf16[5,8,256,128]{3,2,1,0:T(8,128)(2,1)S(1)} %bitcast.107), kind=kLoop, calls=%fused_computation.3 | loop fusion | bytes 5242880
  28.2 0.2 broadcast_multiply_fusion.1
  28.4 0.3 pad.40
  28.7 1.4 %copy.25 = bf16[4,8,256,128]{3,1,2,0:T(8,128)(2,1)S(1)} copy(bf16[4,8,256,128]{3,2,1,0:T(8,128)(2,1)S(1)} %bitcast.109) | data formatting | bytes 4194304
  30.3 1.5 %fusion.77 = f32[70,70]{0,1:T(8,128)S(1)} fusion(bf16[70,32768]{1,0:T(8,128)(2,1)S(1)} %constant_dynamic-update-slice_fusion.3), kind=kOutput, calls=%fused_computation.117 | convolution fusion | flops 321126400 | bytes 4607120 | tf_op jit(solution)/shard_map/dot_general | solution.py:101
  31.8 0.6 copy-done
  33.2 0.3 collective-permute-done.4
  33.7 3.8 %collective-permute-done.5 = f32[70,70]{0,1:T(8,128)S(1)} collective-permute-done((f32[70,70]{0,1:T(8,128)S(1)}, f32[70,70]{0,1:T(8,128)S(1)}, u32[]{:S(2)}, u32[]{:S(2)}) %collective-permute-start.5) | collective-permute-done | bytes 19632 | tf_op jit(solution)/shard_map/ppermute | solution.py:19
  37.6 0.6 slice_add_fusion
  38.2 3.3 %collective-permute-done.6 = f32[70,70]{0,1:T(8,128)S(1)} collective-permute-done((f32[70,70]{0,1:T(8,128)S(1)}, f32[70,70]{0,1:T(8,128)S(1)}, u32[]{:S(2)}, u32[]{:S(2)}) %collective-permute-start.6) | collective-permute-done | bytes 19632 | tf_op jit(solution)/shard_map/ppermute | solution.py:19
  41.5 1.6 %collective-permute-start.7 = (f32[70,70]{0,1:T(8,128)S(1)}, f32[70,70]{0,1:T(8,128)S(1)}, u32[]{:S(2)}, u32[]{:S(2)}) collective-permute-start(f32[70,70]{0,1:T(8,128)S(1)} %add.175), channel_id=1, source_target_pairs={{0,8},{1,9},{2,10},{3,11},{4,12},{5,13},{6,14},{7,15},{8,0},{9,1},... | collective-permute-start | bytes 58808 | tf_op jit(solution)/shard_map/ppermute | solution.py:19
  43.2 1.0 %fusion.10 = f32[256,128]{1,0:T(8,128)} fusion(f32[128,128]{1,0:T(8,128)S(1)} %get-tuple-element.15, s32[128]{0:T(128)S(1)} %fusion.54), kind=kOutput, calls=%fused_computation.27 | convolution fusion | flops 50364416 | bytes 197120 | tf_op jit(solution)/shard_map/dot_general | solution.py:128
  44.2 4.9 %all-to-all-start.1 = ((f32[16,16,128]{2,1,0:T(8,128)}), f32[16,16,128]{2,1,0:T(8,128)S(1)}, u32[]{:S(2)}, u32[]{:S(2)}) async-start(f32[16,16,128]{2,1,0:T(8,128)} %bitcast.5), calls=%async_computation.1 | async-start | bytes 262144 | tf_op jit(solution)/shard_map/all_to_all | solution.py:129
  49.3 3.7 %cholesky.31 = f32[40,40]{1,0:T(8,128)S(1)} custom-call(f32[40,40]{1,0:T(8,128)S(1)} %copy.21), custom_call_target="Cholesky" | custom-call | tf_op jit(solution)/shard_map/jit(cholesky)/cholesky | solution.py:39
  53.0 0.7 compare_reduce_fusion.1
  53.9 0.7 fusion.38
  54.6 3.1 %custom-call.12 = f32[1,40,40]{1,2,0:T(8,128)S(1)} custom-call(f32[1,40,40]{2,1,0:T(8,128)S(1)} %fusion.38), custom_call_target="InvertDiagBlocksLowerTriangular" | custom-call | tf_op jit(solution)/shard_map/triangular_solve | solution.py:41
  57.7 2.7 %cholesky.65 = f32[30,30]{1,0:T(8,128)S(1)} custom-call(f32[30,30]{1,0:T(8,128)S(1)} %fusion.48), custom_call_target="Cholesky" | custom-call | tf_op jit(solution)/shard_map/jit(cholesky)/cholesky | solution.py:39
  60.4 0.2 fusion.41
  60.8 3.7 %convolution_bitcast_fusion = f32[70]{0:T(128)S(1)} fusion(bf16[70,32768]{1,0:T(8,128)(2,1)} %copy-done, bf16[32768,1]{0,1:T(2,128)(2,1)S(1)} %reshape.113), kind=kOutput, calls=%fused_computation.7 | convolution fusion | flops 4587520 | bytes 4653336 | tf_op jit(solution)/shard_map/dot_general | solution.py:131
  64.5 0.4 collective-permute-start.8
  65.0 0.8 collective-permute-done.8
  65.8 1.9 %collective-permute-start.9 = (f32[70]{0:T(128)S(1)}, f32[70]{0:T(128)S(1)}, u32[]{:S(2)}, u32[]{:S(2)}) collective-permute-start(f32[70]{0:T(128)S(1)} %add.178), channel_id=1, source_target_pairs={{0,2},{1,3},{2,0},{3,1},{4,6},{5,7},{6,4},{7,5},{8,10},{9,11},{10,... | collective-permute-start | bytes 848 | tf_op jit(solution)/shard_map/ppermute | solution.py:19
  67.6 0.6 compare_reduce_fusion
  68.2 1.1 %collective-permute-done.9 = f32[70]{0:T(128)S(1)} collective-permute-done((f32[70]{0:T(128)S(1)}, f32[70]{0:T(128)S(1)}, u32[]{:S(2)}, u32[]{:S(2)}) %collective-permute-start.9) | collective-permute-done | bytes 312 | tf_op jit(solution)/shard_map/ppermute | solution.py:19
  69.3 1.9 %collective-permute-start.10 = (f32[70]{0:T(128)S(1)}, f32[70]{0:T(128)S(1)}, u32[]{:S(2)}, u32[]{:S(2)}) collective-permute-start(f32[70]{0:T(128)S(1)} %add.179), channel_id=1, source_target_pairs={{0,4},{1,5},{2,6},{3,7},{4,0},{5,1},{6,2},{7,3},{8,12},{9,13},{10,... | collective-permute-start | bytes 848 | tf_op jit(solution)/shard_map/ppermute | solution.py:19
  71.2 0.7 fusion.44
  71.8 2.3 %custom-call.13 = f32[1,30,30]{1,2,0:T(8,128)S(1)} custom-call(f32[1,30,30]{2,1,0:T(8,128)S(1)} %fusion.44), custom_call_target="InvertDiagBlocksLowerTriangular" | custom-call | tf_op jit(solution)/shard_map/triangular_solve | solution.py:41
  74.2 2.4 %collective-permute-start.11 = (f32[70]{0:T(128)S(1)}, f32[70]{0:T(128)S(1)}, u32[]{:S(2)}, u32[]{:S(2)}) collective-permute-start(f32[70]{0:T(128)S(1)} %add.180), channel_id=1, source_target_pairs={{0,8},{1,9},{2,10},{3,11},{4,12},{5,13},{6,14},{7,15},{8,0},{9,1},... | collective-permute-start | bytes 848 | tf_op jit(solution)/shard_map/ppermute | solution.py:19
  76.8 1.9 %collective-permute-done.11 = f32[70]{0:T(128)S(1)} collective-permute-done((f32[70]{0:T(128)S(1)}, f32[70]{0:T(128)S(1)}, u32[]{:S(2)}, u32[]{:S(2)}) %collective-permute-start.11) | collective-permute-done | bytes 312 | tf_op jit(solution)/shard_map/ppermute | solution.py:19
  79.0 0.2 convolution_bitcast_fusion.3
  79.2 3.5 %fusion = f32[1,32768]{1,0:T(1,128)S(1)} fusion(bf16[5,8,256,128]{3,2,1,0:T(8,128)(2,1)} %bitcast.112, f32[40]{0:T(128)S(1)} %fusion.4), kind=kOutput, calls=%fused_computation | convolution fusion | flops 2621480 | bytes 2752672 | tf_op jit(solution)/shard_map/dot_general | solution.py:137
  83.0 0.4 fusion.78
  83.4 0.8 fusion.7
  (76 shorter events, 2.9 us)
Async XLA Ops:
  4.0 17.7 %all-to-all-start = ((f32[16,17,128]{2,1,0:T(8,128)}), f32[16,17,128]{2,1,0:T(8,128)S(1)}, u32[]{:S(2)}, u32[]{:S(2)}) async-start(f32[16,17,128]{2,1,0:T(8,128)} %select_maximum_fusion), calls=%async_computation | async-start | bytes 393216 | tf_op jit(solution)/shard_map/all_to_all | solution.py:89
  13.9 7.7 %collective-permute-start = (f32[4,384]{1,0:T(4,128)S(1)}, f32[4,384]{1,0:T(4,128)S(1)}, u32[]{:S(2)}, u32[]{:S(2)}) collective-permute-start(f32[4,384]{1,0:T(4,128)S(1)} %get-tuple-element.27), channel_id=1, source_target_pairs={{0,1},{1,2},{2,3},{3,4},{4,5},{5,6},{6,7},{7,8},{8,9},{9,10},{10,1... | collective-permute-start | bytes 18440 | tf_op jit(solution)/shard_map/ppermute | solution.py:26
  14.4 7.3 %collective-permute-start.2 = (f32[4,384]{1,0:T(4,128)S(1)}, f32[4,384]{1,0:T(4,128)S(1)}, u32[]{:S(2)}, u32[]{:S(2)}) collective-permute-start(f32[4,384]{1,0:T(4,128)S(1)} %get-tuple-element.28), channel_id=1, source_target_pairs={{1,0},{2,1},{3,2},{4,3},{5,4},{6,5},{7,6},{8,7},{9,8},{10,9},{11,1... | collective-permute-start | bytes 18440 | tf_op jit(solution)/shard_map/ppermute | solution.py:27
  22.0 10.4 %collective-permute-start.3 = (f32[4,128]{1,0:T(4,128)S(1)}, f32[4,128]{1,0:T(4,128)S(1)}, u32[]{:S(2)}, u32[]{:S(2)}) collective-permute-start(f32[4,128]{1,0:T(4,128)S(1)} %get-tuple-element.48), channel_id=1, source_target_pairs={{1,0},{2,1},{3,2},{4,3},{5,4},{6,5},{7,6},{8,7},{9,8},{10,9},{11,1... | collective-permute-start | bytes 6152 | tf_op jit(solution)/shard_map/ppermute | solution.py:27
  24.5 7.8 %collective-permute-start.1 = (f32[4,128]{1,0:T(4,128)S(1)}, f32[4,128]{1,0:T(4,128)S(1)}, u32[]{:S(2)}, u32[]{:S(2)}) collective-permute-start(f32[4,128]{1,0:T(4,128)S(1)} %get-tuple-element.47), channel_id=1, source_target_pairs={{0,1},{1,2},{2,3},{3,4},{4,5},{5,6},{6,7},{7,8},{8,9},{9,10},{10,1... | collective-permute-start | bytes 6152 | tf_op jit(solution)/shard_map/ppermute | solution.py:26
  26.7 1.5 %copy-start.1 = (bf16[30,256,128]{2,1,0:T(8,128)(2,1)S(1)}, bf16[30,256,128]{2,1,0:T(8,128)(2,1)}, u32[]{:S(2)}) copy-start(bf16[30,256,128]{2,1,0:T(8,128)(2,1)} %param.20) | copy-start | bytes 5898244
  30.2 2.1 %copy-start = (bf16[70,32768]{1,0:T(8,128)(2,1)}, bf16[70,32768]{1,0:T(8,128)(2,1)S(1)}, u32[]{:S(2)}) copy-start(bf16[70,32768]{1,0:T(8,128)(2,1)S(1)} %constant_dynamic-update-slice_fusion.3) | copy-start | bytes 13762564
  30.3 2.1 %copy-start.2 = (f32[128,128]{1,0:T(8,128)S(1)}, f32[128,128]{1,0:T(8,128)}, u32[]{:S(2)}) copy-start(f32[128,128]{1,0:T(8,128)} %param.14) | copy-start | bytes 196612
  30.3 2.1 %copy-start.3 = (f32[128,128]{1,0:T(8,128)S(1)}, f32[128,128]{1,0:T(8,128)}, u32[]{:S(2)}) copy-start(f32[128,128]{1,0:T(8,128)} %param.15) | copy-start | bytes 196612
  30.3 2.1 %copy-start.4 = (f32[128,128]{1,0:T(8,128)S(1)}, f32[128,128]{1,0:T(8,128)}, u32[]{:S(2)}) copy-start(f32[128,128]{1,0:T(8,128)} %param.16) | copy-start | bytes 196612
  32.4 1.2 %collective-permute-start.4 = (f32[70,70]{0,1:T(8,128)S(1)}, f32[70,70]{0,1:T(8,128)S(1)}, u32[]{:S(2)}, u32[]{:S(2)}) collective-permute-start(f32[70,70]{0,1:T(8,128)S(1)} %fusion.77), channel_id=1, source_target_pairs={{0,1},{1,0},{2,3},{3,2},{4,5},{5,4},{6,7},{7,6},{8,9},{9,8},{10,11... | collective-permute-start | bytes 58808 | tf_op jit(solution)/shard_map/ppermute | solution.py:19
  32.7 28.0 %copy-start.6 = (f32[256,128]{1,0:T(8,128)S(1)}, f32[256,128]{1,0:T(8,128)}, u32[]{:S(2)}) copy-start(f32[256,128]{1,0:T(8,128)} %param.13) | copy-start | bytes 393220
  33.6 4.0 %collective-permute-start.5 = (f32[70,70]{0,1:T(8,128)S(1)}, f32[70,70]{0,1:T(8,128)S(1)}, u32[]{:S(2)}, u32[]{:S(2)}) collective-permute-start(f32[70,70]{0,1:T(8,128)S(1)} %add.173), channel_id=1, source_target_pairs={{0,2},{1,3},{2,0},{3,1},{4,6},{5,7},{6,4},{7,5},{8,10},{9,11},{10,... | collective-permute-start | bytes 58808 | tf_op jit(solution)/shard_map/ppermute | solution.py:19
  37.6 4.0 %collective-permute-start.6 = (f32[70,70]{0,1:T(8,128)S(1)}, f32[70,70]{0,1:T(8,128)S(1)}, u32[]{:S(2)}, u32[]{:S(2)}) collective-permute-start(f32[70,70]{0,1:T(8,128)S(1)} %add.174), channel_id=1, source_target_pairs={{0,4},{1,5},{2,6},{3,7},{4,0},{5,1},{6,2},{7,3},{8,12},{9,13},{10,... | collective-permute-start | bytes 58808 | tf_op jit(solution)/shard_map/ppermute | solution.py:19
  38.2 26.3 %copy-start.5 = (f32[128,128]{1,0:T(8,128)}, f32[128,128]{1,0:T(8,128)S(1)}, u32[]{:S(2)}) copy-start(f32[128,128]{1,0:T(8,128)S(1)} %get-tuple-element.15) | copy-start | bytes 196612
  41.5 7.5 %collective-permute-start.7 = (f32[70,70]{0,1:T(8,128)S(1)}, f32[70,70]{0,1:T(8,128)S(1)}, u32[]{:S(2)}, u32[]{:S(2)}) collective-permute-start(f32[70,70]{0,1:T(8,128)S(1)} %add.175), channel_id=1, source_target_pairs={{0,8},{1,9},{2,10},{3,11},{4,12},{5,13},{6,14},{7,15},{8,0},{9,1},... | collective-permute-start | bytes 58808 | tf_op jit(solution)/shard_map/ppermute | solution.py:19
  44.2 16.5 %all-to-all-start.1 = ((f32[16,16,128]{2,1,0:T(8,128)}), f32[16,16,128]{2,1,0:T(8,128)S(1)}, u32[]{:S(2)}, u32[]{:S(2)}) async-start(f32[16,16,128]{2,1,0:T(8,128)} %bitcast.5), calls=%async_computation.1 | async-start | bytes 262144 | tf_op jit(solution)/shard_map/all_to_all | solution.py:129
  64.5 1.2 %collective-permute-start.8 = (f32[70]{0:T(128)S(1)}, f32[70]{0:T(128)S(1)}, u32[]{:S(2)}, u32[]{:S(2)}) collective-permute-start(f32[70]{0:T(128)S(1)} %convolution_bitcast_fusion), channel_id=1, source_target_pairs={{0,1},{1,0},{2,3},{3,2},{4,5},{5,4},{6,7},{7,6},{8,9},{9,8},{10,11... | collective-permute-start | bytes 848 | tf_op jit(solution)/shard_map/ppermute | solution.py:19
  65.8 3.6 %collective-permute-start.9 = (f32[70]{0:T(128)S(1)}, f32[70]{0:T(128)S(1)}, u32[]{:S(2)}, u32[]{:S(2)}) collective-permute-start(f32[70]{0:T(128)S(1)} %add.178), channel_id=1, source_target_pairs={{0,2},{1,3},{2,0},{3,1},{4,6},{5,7},{6,4},{7,5},{8,10},{9,11},{10,... | collective-permute-start | bytes 848 | tf_op jit(solution)/shard_map/ppermute | solution.py:19
  69.3 4.8 %collective-permute-start.10 = (f32[70]{0:T(128)S(1)}, f32[70]{0:T(128)S(1)}, u32[]{:S(2)}, u32[]{:S(2)}) collective-permute-start(f32[70]{0:T(128)S(1)} %add.179), channel_id=1, source_target_pairs={{0,4},{1,5},{2,6},{3,7},{4,0},{5,1},{6,2},{7,3},{8,12},{9,13},{10,... | collective-permute-start | bytes 848 | tf_op jit(solution)/shard_map/ppermute | solution.py:19
  74.2 4.5 %collective-permute-start.11 = (f32[70]{0:T(128)S(1)}, f32[70]{0:T(128)S(1)}, u32[]{:S(2)}, u32[]{:S(2)}) collective-permute-start(f32[70]{0:T(128)S(1)} %add.180), channel_id=1, source_target_pairs={{0,8},{1,9},{2,10},{3,11},{4,12},{5,13},{6,14},{7,15},{8,0},{9,1},... | collective-permute-start | bytes 848 | tf_op jit(solution)/shard_map/ppermute | solution.py:19

commit v3 on v2

--- a/solution.py
+++ b/solution.py
@@ -2,6 +2,7 @@
 import jax.numpy as jnp
 from jax import lax
 from jax.sharding import PartitionSpec as P
+
 
 SUBSTEPS = 4
 
@@ -47,7 +48,7 @@
     return jnp.dot(inverse.T, inner, precision=high)
 
 
-def local(
+def body(
     fluid_press,
     iterate,
     displace,
@@ -118,7 +119,7 @@
     speed = packed[:, lanes : 2 * lanes]
     stiff = packed[:, 2 * lanes : 3 * lanes]
     press = packed[:, 3 * lanes :]
-    for substep in range(SUBSTEPS):
+    for _ in range(SUBSTEPS):
         lapl = jnp.roll(field, 1, 0) + jnp.roll(field, -1, 0) + sides(field) - 4.0 * field
         speed = speed + step_dt * (stiff * lapl + press - damping * speed)
         field = field + step_dt * speed
@@ -163,7 +164,7 @@
         P(None, ("runs", "tile"), None),
     )
     return jax.shard_map(
-        local,
+        body,
         mesh=mesh,
         in_specs=placed,
         out_specs=(P(("runs", "tile"), None), P(("runs", "tile"), None), P(("runs", "tile"), None)),

time: 84.8 us -> 84.8 us (level)
  no operation moved by 1% of the time
where the time goes in v3:
time: 84.8 us; the launch traced here: 84.2 us
  starting transfers between devices  27.5 us (32%)
  other arithmetic  21.2 us (25%)
  matrix products  12.4 us (15%)
  waiting for transfers between devices  11.3 us (13%)
  local copies, waits for them, and re-layouts  10.7 us (13%)
  between operations  1.07 us (1%)
    ppermute x8, waiting for transfers between devices, tree_sum(): lax.ppermute(value, axis, [(i, i ^ stride) for i in range(count)])  11.3 us
    unnamed x21, local copies, waits for them, and re-layouts  8.69 us
    ppermute x8, starting transfers between devices, tree_sum(): lax.ppermute(value, axis, [(i, i ^ stride) for i in range(count)])  8.22 us
    another operation x6, other arithmetic, inverse_factor(): factor = jnp.linalg.cholesky(matrix)  7.82 us
    all_to_all x1, starting transfers between devices, body(): got = lax.all_to_all(sent, 'tile', split_axis=0, concat_axis=0, tiled=True)  7.41 us
    another operation x4, other arithmetic, inverse_factor(): return lax.linalg.triangular_solve(factor, eye, left_side=True, lower=True)  6.69 us
    ppermute x2, starting transfers between devices, halo_pair(): lax.ppermute(cells[:width], axis, [((i + 1) % count, i) for i in range(co...  6.56 us
    all_to_all x1, starting transfers between devices, body(): lax.all_to_all(outgoing, 'tile', split_axis=0, concat_axis=0, tiled=True)  4.87 us
  transfers between devices with their start and end apart: 14, of which 6 were waited for; matrix products, arithmetic and copies ran while one was open for 36% of the time, Pallas kernels for 0%

profile of v3, /device:TPU:0, one launch (start us, length us, event | category | flops | bytes accessed | tf_op | source)
XLA Modules:
  0.0 84.2 jit_solution(12243154680060657807)
XLA Ops:
  0.6 0.9 %fusion.3 = f32[128]{0:T(128)S(1)} fusion(s32[128]{0:T(128)} %bitcast.118), kind=kOutput, calls=%fused_computation.6 | convolution fusion | flops 548736 | bytes 1024 | tf_op jit(solution)/shard_map/dot_general | solution.py:74
  1.5 0.7 fusion.54
  2.4 1.6 %select_maximum_fusion = f32[16,17,128]{2,1,0:T(8,128)} fusion(f32[16,1,16]{2,1,0:T(1,128)S(1)} %reshape.105, f32[16,16,128]{2,1,0:T(8,128)} %bitcast.117), kind=kLoop, calls=%fused_computation.18 | loop fusion | flops 104448 | bytes 271360 | tf_op jit(solution)/shard_map/concatenate | solution.py:89
  4.0 7.4 %all-to-all-start = ((f32[16,17,128]{2,1,0:T(8,128)}), f32[16,17,128]{2,1,0:T(8,128)S(1)}, u32[]{:S(2)}, u32[]{:S(2)}) async-start(f32[16,17,128]{2,1,0:T(8,128)} %select_maximum_fusion), calls=%async_computation | async-start | bytes 393216 | tf_op jit(solution)/shard_map/all_to_all | solution.py:90
  11.4 0.8 %constant_dynamic-update-slice_fusion.2 = f32[128,384]{1,0:T(8,128)S(1)} fusion(f32[128,128]{1,0:T(8,128)} %param.14), kind=kLoop, calls=%fused_computation.85 | loop fusion | bytes 131072
  12.3 0.8 %constant_dynamic-update-slice_fusion.1 = f32[128,384]{1,0:T(8,128)S(1)} fusion(f32[128,384]{1,0:T(8,128)S(1)} %constant_dynamic-update-slice_fusion.2, f32[128,128]{1,0:T(8,128)} %param.15), kind=kLoop, calls=%fused_computation.84 | loop fusion | bytes 131072
  13.1 0.8 %constant_dynamic-update-slice_fusion = f32[128,384]{1,0:T(8,128)S(1)} fusion(f32[128,384]{1,0:T(8,128)S(1)} %constant_dynamic-update-slice_fusion.1, f32[128,128]{1,0:T(8,128)} %param.16), kind=kLoop, calls=%fused_computation.83 | loop fusion | bytes 131072 | tf_op jit(solution)/shard_map/concatenate | solution.py:84
  13.9 0.5 collective-permute-start
  14.4 4.0 %collective-permute-start.2 = (f32[4,384]{1,0:T(4,128)S(1)}, f32[4,384]{1,0:T(4,128)S(1)}, u32[]{:S(2)}, u32[]{:S(2)}) collective-permute-start(f32[4,384]{1,0:T(4,128)S(1)} %get-tuple-element.28), channel_id=1, source_target_pairs={{1,0},{2,1},{3,2},{4,3},{5,4},{6,5},{7,6},{8,7},{9,8},{10,9},{11,1... | collective-permute-start | bytes 18440 | tf_op jit(solution)/shard_map/ppermute | solution.py:28
  18.4 1.9 %pad.41 = bf16[32,256,128]{2,1,0:T(8,128)(2,1)S(1)} pad(bf16[30,256,128]{2,1,0:T(8,128)(2,1)} %param.21, bf16[]{:T(256)} %constant.151), padding=0_2x0_0x0_0 | pad | bytes 4063234
  20.3 1.4 %copy.27 = bf16[4,8,256,128]{3,1,2,0:T(8,128)(2,1)S(1)} copy(bf16[4,8,256,128]{3,2,1,0:T(8,128)(2,1)S(1)} %bitcast.111) | data formatting | bytes 4194304
  21.7 0.3 fusion.11
  22.0 2.5 %collective-permute-start.3 = (f32[4,128]{1,0:T(4,128)S(1)}, f32[4,128]{1,0:T(4,128)S(1)}, u32[]{:S(2)}, u32[]{:S(2)}) collective-permute-start(f32[4,128]{1,0:T(4,128)S(1)} %get-tuple-element.48), channel_id=1, source_target_pairs={{1,0},{2,1},{3,2},{4,3},{5,4},{6,5},{7,6},{8,7},{9,8},{10,9},{11,1... | collective-permute-start | bytes 6152 | tf_op jit(solution)/shard_map/ppermute | solution.py:28
  24.7 2.0 %broadcast_multiply_fusion = bf16[40,256,128]{2,1,0:T(8,128)(2,1)S(1)} fusion(bf16[40,256,128]{2,1,0:T(8,128)(2,1)} %param.18, bf16[256]{0:T(256)(128)(2,1)S(1)} %convert_element_type.39), kind=kLoop, calls=%fused_computation.4 | loop fusion | flops 1310720 | bytes 5243392 | tf_op jit(solution)/shard_map/mul | solution.py:97
  26.7 1.5 %bitcast_dynamic-update-slice_fusion = bf16[70,32768]{1,0:T(8,128)(2,1)S(1)} fusion(bf16[5,8,256,128]{3,2,1,0:T(8,128)(2,1)S(1)} %bitcast.107), kind=kLoop, calls=%fused_computation.3 | loop fusion | bytes 5242880
  28.2 0.2 broadcast_multiply_fusion.1
  28.4 0.3 pad.40
  28.7 1.4 %copy.25 = bf16[4,8,256,128]{3,1,2,0:T(8,128)(2,1)S(1)} copy(bf16[4,8,256,128]{3,2,1,0:T(8,128)(2,1)S(1)} %bitcast.109) | data formatting | bytes 4194304
  30.3 1.5 %fusion.77 = f32[70,70]{0,1:T(8,128)S(1)} fusion(bf16[70,32768]{1,0:T(8,128)(2,1)S(1)} %constant_dynamic-update-slice_fusion.3), kind=kOutput, calls=%fused_computation.117 | convolution fusion | flops 321126400 | bytes 4607120 | tf_op jit(solution)/shard_map/dot_general | solution.py:102
  31.8 0.6 copy-done
  33.2 0.3 collective-permute-done.4
  33.7 3.8 %collective-permute-done.5 = f32[70,70]{0,1:T(8,128)S(1)} collective-permute-done((f32[70,70]{0,1:T(8,128)S(1)}, f32[70,70]{0,1:T(8,128)S(1)}, u32[]{:S(2)}, u32[]{:S(2)}) %collective-permute-start.5) | collective-permute-done | bytes 19632 | tf_op jit(solution)/shard_map/ppermute | solution.py:20
  37.6 0.6 slice_add_fusion
  38.2 3.3 %collective-permute-done.6 = f32[70,70]{0,1:T(8,128)S(1)} collective-permute-done((f32[70,70]{0,1:T(8,128)S(1)}, f32[70,70]{0,1:T(8,128)S(1)}, u32[]{:S(2)}, u32[]{:S(2)}) %collective-permute-start.6) | collective-permute-done | bytes 19632 | tf_op jit(solution)/shard_map/ppermute | solution.py:20
  41.5 1.6 %collective-permute-start.7 = (f32[70,70]{0,1:T(8,128)S(1)}, f32[70,70]{0,1:T(8,128)S(1)}, u32[]{:S(2)}, u32[]{:S(2)}) collective-permute-start(f32[70,70]{0,1:T(8,128)S(1)} %add.175), channel_id=1, source_target_pairs={{0,8},{1,9},{2,10},{3,11},{4,12},{5,13},{6,14},{7,15},{8,0},{9,1},... | collective-permute-start | bytes 58808 | tf_op jit(solution)/shard_map/ppermute | solution.py:20
  43.2 1.0 %fusion.10 = f32[256,128]{1,0:T(8,128)} fusion(f32[128,128]{1,0:T(8,128)S(1)} %get-tuple-element.15, s32[128]{0:T(128)S(1)} %fusion.54), kind=kOutput, calls=%fused_computation.27 | convolution fusion | flops 50364416 | bytes 197120 | tf_op jit(solution)/shard_map/dot_general | solution.py:129
  44.2 4.9 %all-to-all-start.1 = ((f32[16,16,128]{2,1,0:T(8,128)}), f32[16,16,128]{2,1,0:T(8,128)S(1)}, u32[]{:S(2)}, u32[]{:S(2)}) async-start(f32[16,16,128]{2,1,0:T(8,128)} %bitcast.5), calls=%async_computation.1 | async-start | bytes 262144 | tf_op jit(solution)/shard_map/all_to_all | solution.py:130
  49.3 3.7 %cholesky.31 = f32[40,40]{1,0:T(8,128)S(1)} custom-call(f32[40,40]{1,0:T(8,128)S(1)} %copy.21), custom_call_target="Cholesky" | custom-call | tf_op jit(solution)/shard_map/jit(cholesky)/cholesky | solution.py:40
  53.0 0.7 compare_reduce_fusion.1
  53.9 0.7 fusion.38
  54.6 3.1 %custom-call.12 = f32[1,40,40]{1,2,0:T(8,128)S(1)} custom-call(f32[1,40,40]{2,1,0:T(8,128)S(1)} %fusion.38), custom_call_target="InvertDiagBlocksLowerTriangular" | custom-call | tf_op jit(solution)/shard_map/triangular_solve | solution.py:42
  57.7 2.7 %cholesky.65 = f32[30,30]{1,0:T(8,128)S(1)} custom-call(f32[30,30]{1,0:T(8,128)S(1)} %fusion.48), custom_call_target="Cholesky" | custom-call | tf_op jit(solution)/shard_map/jit(cholesky)/cholesky | solution.py:40
  60.4 0.2 fusion.41
  60.8 3.7 %convolution_bitcast_fusion = f32[70]{0:T(128)S(1)} fusion(bf16[70,32768]{1,0:T(8,128)(2,1)} %copy-done, bf16[32768,1]{0,1:T(2,128)(2,1)S(1)} %reshape.113), kind=kOutput, calls=%fused_computation.7 | convolution fusion | flops 4587520 | bytes 4653336 | tf_op jit(solution)/shard_map/dot_general | solution.py:132
  64.5 0.4 collective-permute-start.8
  65.0 0.8 collective-permute-done.8
  65.8 1.9 %collective-permute-start.9 = (f32[70]{0:T(128)S(1)}, f32[70]{0:T(128)S(1)}, u32[]{:S(2)}, u32[]{:S(2)}) collective-permute-start(f32[70]{0:T(128)S(1)} %add.178), channel_id=1, source_target_pairs={{0,2},{1,3},{2,0},{3,1},{4,6},{5,7},{6,4},{7,5},{8,10},{9,11},{10,... | collective-permute-start | bytes 848 | tf_op jit(solution)/shard_map/ppermute | solution.py:20
  67.6 0.6 compare_reduce_fusion
  68.2 1.1 %collective-permute-done.9 = f32[70]{0:T(128)S(1)} collective-permute-done((f32[70]{0:T(128)S(1)}, f32[70]{0:T(128)S(1)}, u32[]{:S(2)}, u32[]{:S(2)}) %collective-permute-start.9) | collective-permute-done | bytes 312 | tf_op jit(solution)/shard_map/ppermute | solution.py:20
  69.3 1.9 %collective-permute-start.10 = (f32[70]{0:T(128)S(1)}, f32[70]{0:T(128)S(1)}, u32[]{:S(2)}, u32[]{:S(2)}) collective-permute-start(f32[70]{0:T(128)S(1)} %add.179), channel_id=1, source_target_pairs={{0,4},{1,5},{2,6},{3,7},{4,0},{5,1},{6,2},{7,3},{8,12},{9,13},{10,... | collective-permute-start | bytes 848 | tf_op jit(solution)/shard_map/ppermute | solution.py:20
  71.2 0.7 fusion.44
  71.8 2.3 %custom-call.13 = f32[1,30,30]{1,2,0:T(8,128)S(1)} custom-call(f32[1,30,30]{2,1,0:T(8,128)S(1)} %fusion.44), custom_call_target="InvertDiagBlocksLowerTriangular" | custom-call | tf_op jit(solution)/shard_map/triangular_solve | solution.py:42
  74.2 2.4 %collective-permute-start.11 = (f32[70]{0:T(128)S(1)}, f32[70]{0:T(128)S(1)}, u32[]{:S(2)}, u32[]{:S(2)}) collective-permute-start(f32[70]{0:T(128)S(1)} %add.180), channel_id=1, source_target_pairs={{0,8},{1,9},{2,10},{3,11},{4,12},{5,13},{6,14},{7,15},{8,0},{9,1},... | collective-permute-start | bytes 848 | tf_op jit(solution)/shard_map/ppermute | solution.py:20
  76.8 1.9 %collective-permute-done.11 = f32[70]{0:T(128)S(1)} collective-permute-done((f32[70]{0:T(128)S(1)}, f32[70]{0:T(128)S(1)}, u32[]{:S(2)}, u32[]{:S(2)}) %collective-permute-start.11) | collective-permute-done | bytes 312 | tf_op jit(solution)/shard_map/ppermute | solution.py:20
  79.0 0.2 convolution_bitcast_fusion.3
  79.2 3.5 %fusion = f32[1,32768]{1,0:T(1,128)S(1)} fusion(bf16[5,8,256,128]{3,2,1,0:T(8,128)(2,1)} %bitcast.112, f32[40]{0:T(128)S(1)} %fusion.4), kind=kOutput, calls=%fused_computation | convolution fusion | flops 2621480 | bytes 2752672 | tf_op jit(solution)/shard_map/dot_general | solution.py:138
  83.0 0.4 fusion.78
  83.4 0.8 fusion.7
  (76 shorter events, 2.9 us)
Async XLA Ops:
  4.0 17.7 %all-to-all-start = ((f32[16,17,128]{2,1,0:T(8,128)}), f32[16,17,128]{2,1,0:T(8,128)S(1)}, u32[]{:S(2)}, u32[]{:S(2)}) async-start(f32[16,17,128]{2,1,0:T(8,128)} %select_maximum_fusion), calls=%async_computation | async-start | bytes 393216 | tf_op jit(solution)/shard_map/all_to_all | solution.py:90
  13.9 7.7 %collective-permute-start = (f32[4,384]{1,0:T(4,128)S(1)}, f32[4,384]{1,0:T(4,128)S(1)}, u32[]{:S(2)}, u32[]{:S(2)}) collective-permute-start(f32[4,384]{1,0:T(4,128)S(1)} %get-tuple-element.27), channel_id=1, source_target_pairs={{0,1},{1,2},{2,3},{3,4},{4,5},{5,6},{6,7},{7,8},{8,9},{9,10},{10,1... | collective-permute-start | bytes 18440 | tf_op jit(solution)/shard_map/ppermute | solution.py:27
  14.4 7.3 %collective-permute-start.2 = (f32[4,384]{1,0:T(4,128)S(1)}, f32[4,384]{1,0:T(4,128)S(1)}, u32[]{:S(2)}, u32[]{:S(2)}) collective-permute-start(f32[4,384]{1,0:T(4,128)S(1)} %get-tuple-element.28), channel_id=1, source_target_pairs={{1,0},{2,1},{3,2},{4,3},{5,4},{6,5},{7,6},{8,7},{9,8},{10,9},{11,1... | collective-permute-start | bytes 18440 | tf_op jit(solution)/shard_map/ppermute | solution.py:28
  22.0 10.4 %collective-permute-start.3 = (f32[4,128]{1,0:T(4,128)S(1)}, f32[4,128]{1,0:T(4,128)S(1)}, u32[]{:S(2)}, u32[]{:S(2)}) collective-permute-start(f32[4,128]{1,0:T(4,128)S(1)} %get-tuple-element.48), channel_id=1, source_target_pairs={{1,0},{2,1},{3,2},{4,3},{5,4},{6,5},{7,6},{8,7},{9,8},{10,9},{11,1... | collective-permute-start | bytes 6152 | tf_op jit(solution)/shard_map/ppermute | solution.py:28
  24.5 7.8 %collective-permute-start.1 = (f32[4,128]{1,0:T(4,128)S(1)}, f32[4,128]{1,0:T(4,128)S(1)}, u32[]{:S(2)}, u32[]{:S(2)}) collective-permute-start(f32[4,128]{1,0:T(4,128)S(1)} %get-tuple-element.47), channel_id=1, source_target_pairs={{0,1},{1,2},{2,3},{3,4},{4,5},{5,6},{6,7},{7,8},{8,9},{9,10},{10,1... | collective-permute-start | bytes 6152 | tf_op jit(solution)/shard_map/ppermute | solution.py:27
  26.7 1.5 %copy-start.1 = (bf16[30,256,128]{2,1,0:T(8,128)(2,1)S(1)}, bf16[30,256,128]{2,1,0:T(8,128)(2,1)}, u32[]{:S(2)}) copy-start(bf16[30,256,128]{2,1,0:T(8,128)(2,1)} %param.20) | copy-start | bytes 5898244
  30.2 2.1 %copy-start = (bf16[70,32768]{1,0:T(8,128)(2,1)}, bf16[70,32768]{1,0:T(8,128)(2,1)S(1)}, u32[]{:S(2)}) copy-start(bf16[70,32768]{1,0:T(8,128)(2,1)S(1)} %constant_dynamic-update-slice_fusion.3) | copy-start | bytes 13762564
  30.3 2.1 %copy-start.2 = (f32[128,128]{1,0:T(8,128)S(1)}, f32[128,128]{1,0:T(8,128)}, u32[]{:S(2)}) copy-start(f32[128,128]{1,0:T(8,128)} %param.14) | copy-start | bytes 196612
  30.3 2.1 %copy-start.3 = (f32[128,128]{1,0:T(8,128)S(1)}, f32[128,128]{1,0:T(8,128)}, u32[]{:S(2)}) copy-start(f32[128,128]{1,0:T(8,128)} %param.15) | copy-start | bytes 196612
  30.3 2.1 %copy-start.4 = (f32[128,128]{1,0:T(8,128)S(1)}, f32[128,128]{1,0:T(8,128)}, u32[]{:S(2)}) copy-start(f32[128,128]{1,0:T(8,128)} %param.16) | copy-start | bytes 196612
  32.4 1.2 %collective-permute-start.4 = (f32[70,70]{0,1:T(8,128)S(1)}, f32[70,70]{0,1:T(8,128)S(1)}, u32[]{:S(2)}, u32[]{:S(2)}) collective-permute-start(f32[70,70]{0,1:T(8,128)S(1)} %fusion.77), channel_id=1, source_target_pairs={{0,1},{1,0},{2,3},{3,2},{4,5},{5,4},{6,7},{7,6},{8,9},{9,8},{10,11... | collective-permute-start | bytes 58808 | tf_op jit(solution)/shard_map/ppermute | solution.py:20
  32.7 28.0 %copy-start.6 = (f32[256,128]{1,0:T(8,128)S(1)}, f32[256,128]{1,0:T(8,128)}, u32[]{:S(2)}) copy-start(f32[256,128]{1,0:T(8,128)} %param.13) | copy-start | bytes 393220
  33.6 4.0 %collective-permute-start.5 = (f32[70,70]{0,1:T(8,128)S(1)}, f32[70,70]{0,1:T(8,128)S(1)}, u32[]{:S(2)}, u32[]{:S(2)}) collective-permute-start(f32[70,70]{0,1:T(8,128)S(1)} %add.173), channel_id=1, source_target_pairs={{0,2},{1,3},{2,0},{3,1},{4,6},{5,7},{6,4},{7,5},{8,10},{9,11},{10,... | collective-permute-start | bytes 58808 | tf_op jit(solution)/shard_map/ppermute | solution.py:20
  37.6 4.0 %collective-permute-start.6 = (f32[70,70]{0,1:T(8,128)S(1)}, f32[70,70]{0,1:T(8,128)S(1)}, u32[]{:S(2)}, u32[]{:S(2)}) collective-permute-start(f32[70,70]{0,1:T(8,128)S(1)} %add.174), channel_id=1, source_target_pairs={{0,4},{1,5},{2,6},{3,7},{4,0},{5,1},{6,2},{7,3},{8,12},{9,13},{10,... | collective-permute-start | bytes 58808 | tf_op jit(solution)/shard_map/ppermute | solution.py:20
  38.2 26.3 %copy-start.5 = (f32[128,128]{1,0:T(8,128)}, f32[128,128]{1,0:T(8,128)S(1)}, u32[]{:S(2)}) copy-start(f32[128,128]{1,0:T(8,128)S(1)} %get-tuple-element.15) | copy-start | bytes 196612
  41.5 7.5 %collective-permute-start.7 = (f32[70,70]{0,1:T(8,128)S(1)}, f32[70,70]{0,1:T(8,128)S(1)}, u32[]{:S(2)}, u32[]{:S(2)}) collective-permute-start(f32[70,70]{0,1:T(8,128)S(1)} %add.175), channel_id=1, source_target_pairs={{0,8},{1,9},{2,10},{3,11},{4,12},{5,13},{6,14},{7,15},{8,0},{9,1},... | collective-permute-start | bytes 58808 | tf_op jit(solution)/shard_map/ppermute | solution.py:20
  44.2 16.5 %all-to-all-start.1 = ((f32[16,16,128]{2,1,0:T(8,128)}), f32[16,16,128]{2,1,0:T(8,128)S(1)}, u32[]{:S(2)}, u32[]{:S(2)}) async-start(f32[16,16,128]{2,1,0:T(8,128)} %bitcast.5), calls=%async_computation.1 | async-start | bytes 262144 | tf_op jit(solution)/shard_map/all_to_all | solution.py:130
  64.5 1.2 %collective-permute-start.8 = (f32[70]{0:T(128)S(1)}, f32[70]{0:T(128)S(1)}, u32[]{:S(2)}, u32[]{:S(2)}) collective-permute-start(f32[70]{0:T(128)S(1)} %convolution_bitcast_fusion), channel_id=1, source_target_pairs={{0,1},{1,0},{2,3},{3,2},{4,5},{5,4},{6,7},{7,6},{8,9},{9,8},{10,11... | collective-permute-start | bytes 848 | tf_op jit(solution)/shard_map/ppermute | solution.py:20
  65.8 3.6 %collective-permute-start.9 = (f32[70]{0:T(128)S(1)}, f32[70]{0:T(128)S(1)}, u32[]{:S(2)}, u32[]{:S(2)}) collective-permute-start(f32[70]{0:T(128)S(1)} %add.178), channel_id=1, source_target_pairs={{0,2},{1,3},{2,0},{3,1},{4,6},{5,7},{6,4},{7,5},{8,10},{9,11},{10,... | collective-permute-start | bytes 848 | tf_op jit(solution)/shard_map/ppermute | solution.py:20
  69.3 4.8 %collective-permute-start.10 = (f32[70]{0:T(128)S(1)}, f32[70]{0:T(128)S(1)}, u32[]{:S(2)}, u32[]{:S(2)}) collective-permute-start(f32[70]{0:T(128)S(1)} %add.179), channel_id=1, source_target_pairs={{0,4},{1,5},{2,6},{3,7},{4,0},{5,1},{6,2},{7,3},{8,12},{9,13},{10,... | collective-permute-start | bytes 848 | tf_op jit(solution)/shard_map/ppermute | solution.py:20
  74.2 4.5 %collective-permute-start.11 = (f32[70]{0:T(128)S(1)}, f32[70]{0:T(128)S(1)}, u32[]{:S(2)}, u32[]{:S(2)}) collective-permute-start(f32[70]{0:T(128)S(1)} %add.180), channel_id=1, source_target_pairs={{0,8},{1,9},{2,10},{3,11},{4,12},{5,13},{6,14},{7,15},{8,0},{9,1},... | collective-permute-start | bytes 848 | tf_op jit(solution)/shard_map/ppermute | solution.py:20

commit v4 on v3

--- a/solution.py
+++ b/solution.py
@@ -2,7 +2,6 @@
 import jax.numpy as jnp
 from jax import lax
 from jax.sharding import PartitionSpec as P
-
 
 SUBSTEPS = 4
 
@@ -92,18 +91,24 @@
     mask = got[:, per_pair, :per_pair].reshape(slot_count)
     mask_half = mask.astype(jnp.bfloat16)
 
-    cols = jnp.concatenate(
-        [
-            (diff_cur * mask_half[None, :, None]).reshape(n_cur, -1),
-            (diff_past * mask_half[None, :, None]).reshape(diff_past.shape[0], -1),
-        ],
-        axis=0,
+    both = (((1, 2), (1, 2)), ((), ()))
+    cur_half = diff_cur * mask_half[None, :, None]
+    past_half = diff_past * mask_half[None, :, None]
+    gram_cur = lax.dot_general(cur_half, diff_cur, both, preferred_element_type=jnp.float32)
+    gram_past = lax.dot_general(past_half, diff_past, both, preferred_element_type=jnp.float32)
+    cross = lax.dot_general(past_half, diff_cur, both, preferred_element_type=jnp.float32)
+    n_past = diff_past.shape[0]
+    summed = tree_sum(
+        jnp.concatenate([gram_cur.reshape(-1), gram_past.reshape(-1), cross.reshape(-1)]), "tile"
     )
-    gram = lax.dot_general(cols, cols, (((1,), (1,)), ((), ())), preferred_element_type=jnp.float32)
-    gram = tree_sum(gram, "tile")
-    cross = gram[n_cur:, :n_cur]
-    inv_cur = inverse_factor(gram[:n_cur, :n_cur])
-    inv_past = inverse_factor(gram[n_cur:, n_cur:])
+    gram_cur = summed[: n_cur * n_cur].reshape(n_cur, n_cur)
+    gram_past = summed[n_cur * n_cur : n_cur * n_cur + n_past * n_past].reshape(n_past, n_past)
+    cross = summed[n_cur * n_cur + n_past * n_past :].reshape(n_past, n_cur)
+    blocks = jnp.zeros((n_cur + n_past, n_cur + n_past), jnp.float32)
+    blocks = blocks.at[:n_cur, :n_cur].set(gram_cur).at[n_cur:, n_cur:].set(gram_past)
+    inverse = inverse_factor(blocks)
+    inv_cur = inverse[:n_cur, :n_cur]
+    inv_past = inverse[n_cur:, n_cur:]
 
     pressure = jnp.dot(chooser, returned, precision=high)
     press_below, press_above = halo_pair(pressure, width, "tile")
@@ -128,8 +133,15 @@
 
     outgoing = jnp.dot(chooser.T, field, precision=high)
     x_tilde = lax.all_to_all(outgoing, "tile", split_axis=0, concat_axis=0, tiled=True)
-    resid = (mask[:, None] * (x_tilde - iterate)).astype(jnp.bfloat16).reshape(-1)
-    inner = tree_sum(jnp.dot(cols, resid, preferred_element_type=jnp.float32), "tile")
+    resid = (mask[:, None] * (x_tilde - iterate)).astype(jnp.bfloat16)
+    lhs = (((1, 2), (0, 1)), ((), ()))
+    inner = jnp.concatenate(
+        [
+            lax.dot_general(diff_cur, resid, lhs, preferred_element_type=jnp.float32),
+            lax.dot_general(diff_past, resid, lhs, preferred_element_type=jnp.float32),
+        ]
+    )
+    inner = tree_sum(inner, "tile")
     rhs_cur = inner[:n_cur]
     rhs_past = inner[n_cur:]
     coeff = -solve_spd(inv_cur, rhs_cur)

time: 84.8 us -> 91.7 us (1.081)
  matrix products: 12.4 us -> 20.5 us
  waiting for transfers between devices: 11.3 us -> 17.1 us
  local copies, waits for them, and re-layouts: 10.7 us -> 6.62 us
  other arithmetic: 21.2 us -> 19.6 us
  starting transfers between devices: 27.5 us -> 26.2 us
    dot_general x2 -> x5, matrix products: 5.15 us -> 13.4 us  [the longest x1 3.87 us: body(): lax.dot_general(diff_cur, resid, lhs, preferred_element_type=jnp.float32)]
    unnamed x21 -> x22, local copies, waits for them, and re-layouts: 8.69 us -> 3.32 us
    ppermute x2, waiting for transfers between devices: 0.01 us -> 4.4 us  [halo_pair(): lax.ppermute(cells[-width:], axis, [(i, (i + 1) % count) for i in range(c...]
    ppermute x2, starting transfers between devices: 6.56 us -> 8.83 us  [halo_pair(): lax.ppermute(cells[:width], axis, [((i + 1) % count, i) for i in range(co...]
    ppermute x8, starting transfers between devices: 8.22 us -> 6.2 us  [tree_sum(): lax.ppermute(value, axis, [(i, i ^ stride) for i in range(count)])]
    ppermute x2, waiting for transfers between devices: 0.01 us -> 1.35 us  [halo_pair(): lax.ppermute(cells[:width], axis, [((i + 1) % count, i) for i in range(co...]
    all_to_all x1, starting transfers between devices: 4.87 us -> 3.69 us  [body(): lax.all_to_all(outgoing, 'tile', split_axis=0, concat_axis=0, tiled=True)]
    another operation x6 -> x3, other arithmetic: 7.82 us -> 7.07 us  [inverse_factor(): factor = jnp.linalg.cholesky(matrix)]
  transfers between devices with their start and end apart: 14 -> 14, of which waited for: 6 -> 8; matrix products, arithmetic and copies ran while one was open for 36% -> 35% of each run, Pallas kernels for 0% -> 0%
where the time goes in v4:
time: 91.7 us; the launch traced here: 91.2 us
  starting transfers between devices  26.2 us (29%)
  matrix products  20.5 us (22%)
  other arithmetic  19.6 us (21%)
  waiting for transfers between devices  17.1 us (19%)
  local copies, waits for them, and re-layouts  6.62 us (7%)
  between operations  1.1 us (1%)
    ppermute x8, waiting for transfers between devices, tree_sum(): lax.ppermute(value, axis, [(i, i ^ stride) for i in range(count)])  11.4 us
    ppermute x2, starting transfers between devices, halo_pair(): lax.ppermute(cells[:width], axis, [((i + 1) % count, i) for i in range(co...  8.83 us
    all_to_all x1, starting transfers between devices, body(): got = lax.all_to_all(sent, 'tile', split_axis=0, concat_axis=0, tiled=True)  7.41 us
    another operation x3, other arithmetic, inverse_factor(): factor = jnp.linalg.cholesky(matrix)  7.07 us
    ppermute x8, starting transfers between devices, tree_sum(): lax.ppermute(value, axis, [(i, i ^ stride) for i in range(count)])  6.2 us
    another operation x2, other arithmetic, inverse_factor(): return lax.linalg.triangular_solve(factor, eye, left_side=True, lower=True)  6.02 us
    ppermute x2, waiting for transfers between devices, halo_pair(): lax.ppermute(cells[-width:], axis, [(i, (i + 1) % count) for i in range(c...  4.4 us
    dot_general x1, matrix products, body(): lax.dot_general(diff_cur, resid, lhs, preferred_element_type=jnp.float32)  3.87 us
  transfers between devices with their start and end apart: 14, of which 8 were waited for; matrix products, arithmetic and copies ran while one was open for 35% of the time, Pallas kernels for 0%

profile of v4, /device:TPU:0, one launch (start us, length us, event | category | flops | bytes accessed | tf_op | source)
XLA Modules:
  0.0 91.2 jit_solution(6276672845404405580)
XLA Ops:
  0.6 0.9 fusion.31
  1.5 0.7 fusion.89
  2.4 1.6 %select_maximum_fusion = f32[16,17,128]{2,1,0:T(8,128)} fusion(f32[16,1,16]{2,1,0:T(1,128)S(1)} %reshape.162, f32[16,16,128]{2,1,0:T(8,128)} %bitcast.101), kind=kLoop, calls=%fused_computation.34 | loop fusion | flops 104448 | bytes 271360 | tf_op jit(solution)/shard_map/concatenate | solution.py:88
  4.0 7.4 %all-to-all-start = ((f32[16,17,128]{2,1,0:T(8,128)}), f32[16,17,128]{2,1,0:T(8,128)S(1)}, u32[]{:S(2)}, u32[]{:S(2)}) async-start(f32[16,17,128]{2,1,0:T(8,128)} %select_maximum_fusion), calls=%async_computation | async-start | bytes 393216 | tf_op jit(solution)/shard_map/all_to_all | solution.py:89
  11.4 0.8 constant_dynamic-update-slice_fusion.2
  12.3 0.8 constant_dynamic-update-slice_fusion.1
  13.1 0.8 constant_dynamic-update-slice_fusion
  13.9 4.4 %collective-permute-start.2 = (f32[4,384]{1,0:T(4,128)S(1)}, f32[4,384]{1,0:T(4,128)S(1)}, u32[]{:S(2)}, u32[]{:S(2)}) collective-permute-start(f32[4,384]{1,0:T(4,128)S(1)} %get-tuple-element.52), channel_id=1, source_target_pairs={{1,0},{2,1},{3,2},{4,3},{5,4},{6,5},{7,6},{8,7},{9,8},{10,9},{11,1... | collective-permute-start | bytes 18440 | tf_op jit(solution)/shard_map/ppermute | solution.py:27
  18.4 1.3 %collective-permute-done.2 = f32[4,384]{1,0:T(4,128)S(1)} collective-permute-done((f32[4,384]{1,0:T(4,128)S(1)}, f32[4,384]{1,0:T(4,128)S(1)}, u32[]{:S(2)}, u32[]{:S(2)}) %collective-permute-start.2) | collective-permute-done | bytes 6176 | tf_op jit(solution)/shard_map/ppermute | solution.py:27
  19.7 4.4 %collective-permute-done = f32[4,384]{1,0:T(4,128)S(1)} collective-permute-done((f32[4,384]{1,0:T(4,128)S(1)}, f32[4,384]{1,0:T(4,128)S(1)}, u32[]{:S(2)}, u32[]{:S(2)}) %collective-permute-start) | collective-permute-done | bytes 6176 | tf_op jit(solution)/shard_map/ppermute | solution.py:26
  24.1 0.3 fusion.45
  24.5 4.4 %collective-permute-start.3 = (f32[4,128]{1,0:T(4,128)S(1)}, f32[4,128]{1,0:T(4,128)S(1)}, u32[]{:S(2)}, u32[]{:S(2)}) collective-permute-start(f32[4,128]{1,0:T(4,128)S(1)} %get-tuple-element.72), channel_id=1, source_target_pairs={{1,0},{2,1},{3,2},{4,3},{5,4},{6,5},{7,6},{8,7},{9,8},{10,9},{11,1... | collective-permute-start | bytes 6152 | tf_op jit(solution)/shard_map/ppermute | solution.py:27
  29.0 1.8 %broadcast_multiply_fusion.1 = bf16[30,256,128]{2,1,0:T(8,128)(2,1)S(1)} fusion(bf16[30,256,128]{2,1,0:T(8,128)(2,1)} %param.24, bf16[256]{0:T(256)(128)(2,1)S(1)} %convert_element_type.38), kind=kLoop, calls=%fused_computation.32 | loop fusion | flops 983040 | bytes 3932672 | tf_op jit(solution)/shard_map/mul | solution.py:96
  30.8 0.3 broadcast_multiply_fusion
  31.1 2.5 %fusion.26 = f32[30,40]{1,0:T(8,128)S(1)} fusion(bf16[40,256,128]{2,1,0:T(8,128)(2,1)S(1)} %copy-done, bf16[30,256,128]{2,1,0:T(8,128)(2,1)S(1)} %broadcast_multiply_fusion.1), kind=kOutput, calls=%fused_computation.19 | convolution fusion | flops 78643200 | bytes 4592320 | tf_op jit(solution)/shard_map/dot_general | solution.py:99
  33.6 3.2 %fusion.16 = f32[40,40]{1,0:T(8,128)S(1)} fusion(bf16[40,256,128]{2,1,0:T(8,128)(2,1)S(1)} %copy-done, bf16[40,256,128]{2,1,0:T(8,128)(2,1)S(1)} %broadcast_multiply_fusion), kind=kOutput, calls=%fused_computation.17 | convolution fusion | flops 104857600 | bytes 5249280 | tf_op jit(solution)/shard_map/dot_general | solution.py:97
  36.8 2.3 %fusion.21 = f32[30,30]{1,0:T(8,128)S(1)} fusion(bf16[30,256,128]{2,1,0:T(8,128)(2,1)S(1)} %copy-done.2, bf16[30,256,128]{2,1,0:T(8,128)(2,1)S(1)} %broadcast_multiply_fusion.1), kind=kOutput, calls=%fused_computation.18 | convolution fusion | flops 58982400 | bytes 3935760 | tf_op jit(solution)/shard_map/dot_general | solution.py:98
  40.5 0.2 collective-permute-done.4
  40.7 0.6 slice_add_fusion
  41.3 3.1 %collective-permute-done.5 = f32[3700]{0:T(1024)S(1)} collective-permute-done((f32[3700]{0:T(1024)S(1)}, f32[3700]{0:T(1024)S(1)}, u32[]{:S(2)}, u32[]{:S(2)}) %collective-permute-start.5) | collective-permute-done | bytes 14832 | tf_op jit(solution)/shard_map/ppermute | solution.py:19
  44.4 1.0 %fusion.44 = f32[256,128]{1,0:T(8,128)} fusion(f32[128,128]{1,0:T(8,128)S(1)} %get-tuple-element.39, s32[128]{0:T(128)S(1)} %fusion.89), kind=kOutput, calls=%fused_computation.43 | convolution fusion | flops 50364416 | bytes 197120 | tf_op jit(solution)/shard_map/dot_general | solution.py:134
  45.5 3.7 %all-to-all-start.1 = ((f32[16,16,128]{2,1,0:T(8,128)}), f32[16,16,128]{2,1,0:T(8,128)S(1)}, u32[]{:S(2)}, u32[]{:S(2)}) async-start(f32[16,16,128]{2,1,0:T(8,128)} %bitcast.5), calls=%async_computation.1 | async-start | bytes 262144 | tf_op jit(solution)/shard_map/all_to_all | solution.py:135
  49.2 2.6 %collective-permute-start.7 = (f32[3700]{0:T(1024)S(1)}, f32[3700]{0:T(1024)S(1)}, u32[]{:S(2)}, u32[]{:S(2)}) collective-permute-start(f32[3700]{0:T(1024)S(1)} %add.170), channel_id=1, source_target_pairs={{0,8},{1,9},{2,10},{3,11},{4,12},{5,13},{6,14},{7,15},{8,0},{9,1},... | collective-permute-start | bytes 44408 | tf_op jit(solution)/shard_map/ppermute | solution.py:19
  51.8 0.2 pad.52
  52.1 1.4 %copy.40 = bf16[4,8,256,128]{3,1,2,0:T(8,128)(2,1)S(1)} copy(bf16[4,8,256,128]{3,2,1,0:T(8,128)(2,1)S(1)} %bitcast.96) | data formatting | bytes 4194304
  53.4 3.0 %collective-permute-done.7 = f32[3700]{0:T(1024)S(1)} collective-permute-done((f32[3700]{0:T(1024)S(1)}, f32[3700]{0:T(1024)S(1)}, u32[]{:S(2)}, u32[]{:S(2)}) %collective-permute-start.7) | collective-permute-done | bytes 14832 | tf_op jit(solution)/shard_map/ppermute | solution.py:19
  56.9 0.8 scatter.14
  57.8 6.4 %cholesky.16 = f32[70,70]{1,0:T(8,128)S(1)} custom-call(f32[70,70]{1,0:T(8,128)S(1)} %fusion.77), custom_call_target="Cholesky" | custom-call | tf_op jit(solution)/shard_map/jit(cholesky)/cholesky | solution.py:39
  64.3 3.9 %fusion.32 = f32[40]{0:T(128)S(1)} fusion(bf16[40,256,128]{2,1,0:T(8,128)(2,1)} %param.22, bf16[256,128,1]{1,0,2:T(8,128)(2,1)S(1)} %bitcast.102), kind=kOutput, calls=%fused_computation.22 | convolution fusion | flops 2621440 | bytes 2687136 | tf_op jit(solution)/shard_map/dot_general | solution.py:140
  68.2 1.5 %fusion.38 = f32[30]{0:T(128)S(1)} fusion(bf16[30,256,128]{2,1,0:T(8,128)(2,1)S(1)} %copy-done.3, bf16[256,128,1]{1,0,2:T(8,128)(2,1)S(1)} %bitcast.103), kind=kOutput, calls=%fused_computation.31 | convolution fusion | flops 1966080 | bytes 2031736 | tf_op jit(solution)/shard_map/dot_general | solution.py:141
  69.8 1.1 %collective-permute-done.8 = f32[70]{0:T(128)S(1)} collective-permute-done((f32[70]{0:T(128)S(1)}, f32[70]{0:T(128)S(1)}, u32[]{:S(2)}, u32[]{:S(2)}) %collective-permute-start.8) | collective-permute-done | bytes 312 | tf_op jit(solution)/shard_map/ppermute | solution.py:19
  71.0 1.5 %collective-permute-start.9 = (f32[70]{0:T(128)S(1)}, f32[70]{0:T(128)S(1)}, u32[]{:S(2)}, u32[]{:S(2)}) collective-permute-start(f32[70]{0:T(128)S(1)} %fusion.120), channel_id=1, source_target_pairs={{0,2},{1,3},{2,0},{3,1},{4,6},{5,7},{6,4},{7,5},{8,10},{9,11},{10,... | collective-permute-start | bytes 848 | tf_op jit(solution)/shard_map/ppermute | solution.py:19
  72.5 0.6 compare_reduce_fusion
  73.2 1.5 %collective-permute-done.9 = f32[70]{0:T(128)S(1)} collective-permute-done((f32[70]{0:T(128)S(1)}, f32[70]{0:T(128)S(1)}, u32[]{:S(2)}, u32[]{:S(2)}) %collective-permute-start.9) | collective-permute-done | bytes 312 | tf_op jit(solution)/shard_map/ppermute | solution.py:19
  74.6 0.4 collective-permute-start.10
  75.1 0.7 fusion.74
  75.7 5.4 %custom-call.6 = f32[1,70,70]{1,2,0:T(8,128)S(1)} custom-call(f32[1,70,70]{2,1,0:T(8,128)S(1)} %fusion.74), custom_call_target="InvertDiagBlocksLowerTriangular" | custom-call | tf_op jit(solution)/shard_map/triangular_solve | solution.py:41
  81.1 1.6 %collective-permute-start.11 = (f32[70]{0:T(128)S(1)}, f32[70]{0:T(128)S(1)}, u32[]{:S(2)}, u32[]{:S(2)}) collective-permute-start(f32[70]{0:T(128)S(1)} %add.175), channel_id=1, source_target_pairs={{0,8},{1,9},{2,10},{3,11},{4,12},{5,13},{6,14},{7,15},{8,0},{9,1},... | collective-permute-start | bytes 848 | tf_op jit(solution)/shard_map/ppermute | solution.py:19
  82.7 0.2 fusion.75
  83.1 2.5 %collective-permute-done.11 = f32[70]{0:T(128)S(1)} collective-permute-done((f32[70]{0:T(128)S(1)}, f32[70]{0:T(128)S(1)}, u32[]{:S(2)}, u32[]{:S(2)}) %collective-permute-start.11) | collective-permute-done | bytes 312 | tf_op jit(solution)/shard_map/ppermute | solution.py:19
  85.7 0.1 convolution_bitcast_fusion.4
  85.8 0.1 fusion.35
  85.9 0.1 convolution_bitcast_fusion.2
  86.1 0.2 convolution_bitcast_fusion.1
  86.3 0.2 fusion.37
  86.5 3.5 %fusion = f32[1,32768]{1,0:T(1,128)S(1)} fusion(bf16[5,8,256,128]{3,2,1,0:T(8,128)(2,1)} %bitcast.97, f32[40]{0:T(128)S(1)} %fusion.35), kind=kOutput, calls=%fused_computation | convolution fusion | flops 2621480 | bytes 2752672 | tf_op jit(solution)/shard_map/dot_general | solution.py:150
  90.0 0.4 fusion.112
  90.4 0.8 fusion.41
  (82 shorter events, 2.7 us)
Async XLA Ops:
  4.0 20.1 %all-to-all-start = ((f32[16,17,128]{2,1,0:T(8,128)}), f32[16,17,128]{2,1,0:T(8,128)S(1)}, u32[]{:S(2)}, u32[]{:S(2)}) async-start(f32[16,17,128]{2,1,0:T(8,128)} %select_maximum_fusion), calls=%async_computation | async-start | bytes 393216 | tf_op jit(solution)/shard_map/all_to_all | solution.py:89
  13.9 5.7 %collective-permute-start.2 = (f32[4,384]{1,0:T(4,128)S(1)}, f32[4,384]{1,0:T(4,128)S(1)}, u32[]{:S(2)}, u32[]{:S(2)}) collective-permute-start(f32[4,384]{1,0:T(4,128)S(1)} %get-tuple-element.52), channel_id=1, source_target_pairs={{1,0},{2,1},{3,2},{4,3},{5,4},{6,5},{7,6},{8,7},{9,8},{10,9},{11,1... | collective-permute-start | bytes 18440 | tf_op jit(solution)/shard_map/ppermute | solution.py:27
  18.4 5.8 %collective-permute-start = (f32[4,384]{1,0:T(4,128)S(1)}, f32[4,384]{1,0:T(4,128)S(1)}, u32[]{:S(2)}, u32[]{:S(2)}) collective-permute-start(f32[4,384]{1,0:T(4,128)S(1)} %get-tuple-element.51), channel_id=1, source_target_pairs={{0,1},{1,2},{2,3},{3,4},{4,5},{5,6},{6,7},{7,8},{8,9},{9,10},{10,1... | collective-permute-start | bytes 18440 | tf_op jit(solution)/shard_map/ppermute | solution.py:26
  24.1 6.7 %copy-start = (bf16[40,256,128]{2,1,0:T(8,128)(2,1)S(1)}, bf16[40,256,128]{2,1,0:T(8,128)(2,1)}, u32[]{:S(2)}) copy-start(bf16[40,256,128]{2,1,0:T(8,128)(2,1)} %param.22) | copy-start | bytes 7864324
  24.4 15.1 %collective-permute-start.1 = (f32[4,128]{1,0:T(4,128)S(1)}, f32[4,128]{1,0:T(4,128)S(1)}, u32[]{:S(2)}, u32[]{:S(2)}) collective-permute-start(f32[4,128]{1,0:T(4,128)S(1)} %get-tuple-element.71), channel_id=1, source_target_pairs={{0,1},{1,2},{2,3},{3,4},{4,5},{5,6},{6,7},{7,8},{8,9},{9,10},{10,1... | collective-permute-start | bytes 6152 | tf_op jit(solution)/shard_map/ppermute | solution.py:26
  24.5 15.0 %collective-permute-start.3 = (f32[4,128]{1,0:T(4,128)S(1)}, f32[4,128]{1,0:T(4,128)S(1)}, u32[]{:S(2)}, u32[]{:S(2)}) collective-permute-start(f32[4,128]{1,0:T(4,128)S(1)} %get-tuple-element.72), channel_id=1, source_target_pairs={{1,0},{2,1},{3,2},{4,3},{5,4},{6,5},{7,6},{8,7},{9,8},{10,9},{11,1... | collective-permute-start | bytes 6152 | tf_op jit(solution)/shard_map/ppermute | solution.py:27
  33.6 3.2 %copy-start.2 = (bf16[30,256,128]{2,1,0:T(8,128)(2,1)S(1)}, bf16[30,256,128]{2,1,0:T(8,128)(2,1)}, u32[]{:S(2)}) copy-start(bf16[30,256,128]{2,1,0:T(8,128)(2,1)} %param.24) | copy-start | bytes 5898244
  36.8 2.8 %copy-start.4 = (f32[128,128]{1,0:T(8,128)S(1)}, f32[128,128]{1,0:T(8,128)}, u32[]{:S(2)}) copy-start(f32[128,128]{1,0:T(8,128)} %param.18) | copy-start | bytes 196612
  36.8 2.8 %copy-start.5 = (f32[128,128]{1,0:T(8,128)S(1)}, f32[128,128]{1,0:T(8,128)}, u32[]{:S(2)}) copy-start(f32[128,128]{1,0:T(8,128)} %param.19) | copy-start | bytes 196612
  36.8 2.8 %copy-start.6 = (f32[128,128]{1,0:T(8,128)S(1)}, f32[128,128]{1,0:T(8,128)}, u32[]{:S(2)}) copy-start(f32[128,128]{1,0:T(8,128)} %param.20) | copy-start | bytes 196612
  39.5 1.2 %collective-permute-start.4 = (f32[3700]{0:T(1024)S(1)}, f32[3700]{0:T(1024)S(1)}, u32[]{:S(2)}, u32[]{:S(2)}) collective-permute-start(f32[3700]{0:T(1024)S(1)} %concatenate.103), channel_id=1, source_target_pairs={{0,1},{1,0},{2,3},{3,2},{4,5},{5,4},{6,7},{7,6},{8,9},{9,8},{10,11... | collective-permute-start | bytes 44408 | tf_op jit(solution)/shard_map/ppermute | solution.py:19
  39.9 11.9 %copy-start.1 = (bf16[30,256,128]{2,1,0:T(8,128)(2,1)S(1)}, bf16[30,256,128]{2,1,0:T(8,128)(2,1)}, u32[]{:S(2)}) copy-start(bf16[30,256,128]{2,1,0:T(8,128)(2,1)} %param.25) | copy-start | bytes 5898244
  40.7 3.7 %collective-permute-start.5 = (f32[3700]{0:T(1024)S(1)}, f32[3700]{0:T(1024)S(1)}, u32[]{:S(2)}, u32[]{:S(2)}) collective-permute-start(f32[3700]{0:T(1024)S(1)} %add.168), channel_id=1, source_target_pairs={{0,2},{1,3},{2,0},{3,1},{4,6},{5,7},{6,4},{7,5},{8,10},{9,11},{10,... | collective-permute-start | bytes 44408 | tf_op jit(solution)/shard_map/ppermute | solution.py:19
  41.3 10.7 %copy-start.7 = (f32[128,128]{1,0:T(8,128)}, f32[128,128]{1,0:T(8,128)S(1)}, u32[]{:S(2)}) copy-start(f32[128,128]{1,0:T(8,128)S(1)} %get-tuple-element.39) | copy-start | bytes 196612
  44.4 4.7 %collective-permute-start.6 = (f32[3700]{0:T(1024)S(1)}, f32[3700]{0:T(1024)S(1)}, u32[]{:S(2)}, u32[]{:S(2)}) collective-permute-start(f32[3700]{0:T(1024)S(1)} %add.169), channel_id=1, source_target_pairs={{0,4},{1,5},{2,6},{3,7},{4,0},{5,1},{6,2},{7,3},{8,12},{9,13},{10,... | collective-permute-start | bytes 44408 | tf_op jit(solution)/shard_map/ppermute | solution.py:19
  45.5 18.7 %all-to-all-start.1 = ((f32[16,16,128]{2,1,0:T(8,128)}), f32[16,16,128]{2,1,0:T(8,128)S(1)}, u32[]{:S(2)}, u32[]{:S(2)}) async-start(f32[16,16,128]{2,1,0:T(8,128)} %bitcast.5), calls=%async_computation.1 | async-start | bytes 262144 | tf_op jit(solution)/shard_map/all_to_all | solution.py:135
  49.2 7.2 %collective-permute-start.7 = (f32[3700]{0:T(1024)S(1)}, f32[3700]{0:T(1024)S(1)}, u32[]{:S(2)}, u32[]{:S(2)}) collective-permute-start(f32[3700]{0:T(1024)S(1)} %add.170), channel_id=1, source_target_pairs={{0,8},{1,9},{2,10},{3,11},{4,12},{5,13},{6,14},{7,15},{8,0},{9,1},... | collective-permute-start | bytes 44408 | tf_op jit(solution)/shard_map/ppermute | solution.py:19
  52.1 12.2 %copy-start.8 = (f32[256,128]{1,0:T(8,128)S(1)}, f32[256,128]{1,0:T(8,128)}, u32[]{:S(2)}) copy-start(f32[256,128]{1,0:T(8,128)} %param.17) | copy-start | bytes 393220
  64.2 4.0 %copy-start.3 = (bf16[30,256,128]{2,1,0:T(8,128)(2,1)S(1)}, bf16[30,256,128]{2,1,0:T(8,128)(2,1)}, u32[]{:S(2)}) copy-start(bf16[30,256,128]{2,1,0:T(8,128)(2,1)} %param.24) | copy-start | bytes 5898244
  69.8 1.2 %collective-permute-start.8 = (f32[70]{0:T(128)S(1)}, f32[70]{0:T(128)S(1)}, u32[]{:S(2)}, u32[]{:S(2)}) collective-permute-start(f32[70]{0:T(128)S(1)} %pad_maximum_fusion), channel_id=1, source_target_pairs={{0,1},{1,0},{2,3},{3,2},{4,5},{5,4},{6,7},{7,6},{8,9},{9,8},{10,11... | collective-permute-start | bytes 848 | tf_op jit(solution)/shard_map/ppermute | solution.py:19
  71.0 3.6 %collective-permute-start.9 = (f32[70]{0:T(128)S(1)}, f32[70]{0:T(128)S(1)}, u32[]{:S(2)}, u32[]{:S(2)}) collective-permute-start(f32[70]{0:T(128)S(1)} %fusion.120), channel_id=1, source_target_pairs={{0,2},{1,3},{2,0},{3,1},{4,6},{5,7},{6,4},{7,5},{8,10},{9,11},{10,... | collective-permute-start | bytes 848 | tf_op jit(solution)/shard_map/ppermute | solution.py:19
  74.6 6.5 %collective-permute-start.10 = (f32[70]{0:T(128)S(1)}, f32[70]{0:T(128)S(1)}, u32[]{:S(2)}, u32[]{:S(2)}) collective-permute-start(f32[70]{0:T(128)S(1)} %add.174), channel_id=1, source_target_pairs={{0,4},{1,5},{2,6},{3,7},{4,0},{5,1},{6,2},{7,3},{8,12},{9,13},{10,... | collective-permute-start | bytes 848 | tf_op jit(solution)/shard_map/ppermute | solution.py:19
  81.1 4.5 %collective-permute-start.11 = (f32[70]{0:T(128)S(1)}, f32[70]{0:T(128)S(1)}, u32[]{:S(2)}, u32[]{:S(2)}) collective-permute-start(f32[70]{0:T(128)S(1)} %add.175), channel_id=1, source_target_pairs={{0,8},{1,9},{2,10},{3,11},{4,12},{5,13},{6,14},{7,15},{8,0},{9,1},... | collective-permute-start | bytes 848 | tf_op jit(solution)/shard_map/ppermute | solution.py:19

commit v5 on v3

--- a/solution.py
+++ b/solution.py
@@ -22,10 +22,12 @@
     return value
 
 
-def halo_pair(cells, width, axis):
+def halo_pair(parts, width, axis):
     count = lax.axis_size(axis)
-    below = lax.ppermute(cells[-width:], axis, [(i, (i + 1) % count) for i in range(count)])
-    above = lax.ppermute(cells[:width], axis, [((i + 1) % count, i) for i in range(count)])
+    tail = jnp.concatenate([part[-width:] for part in parts], axis=1)
+    head = jnp.concatenate([part[:width] for part in parts], axis=1)
+    below = lax.ppermute(tail, axis, [(i, (i + 1) % count) for i in range(count)])
+    above = lax.ppermute(head, axis, [((i + 1) % count, i) for i in range(count)])
     return below, above
 
 
@@ -81,8 +83,7 @@
     lanes = fluid_press.shape[1]
     width = SUBSTEPS
 
-    edge = jnp.concatenate([displace, velocity, stiffness], axis=1)
-    edge_below, edge_above = halo_pair(edge, width, "tile")
+    edge_below, edge_above = halo_pair((displace, velocity, stiffness), width, "tile")
 
     flag_rows = jnp.zeros((tile_count, 1, lanes), jnp.float32)
     flag_rows = flag_rows.at[:, 0, :per_pair].set(flags.reshape(tile_count, per_pair))
@@ -106,19 +107,16 @@
     inv_past = inverse_factor(gram[n_cur:, n_cur:])
 
     pressure = jnp.dot(chooser, returned, precision=high)
-    press_below, press_above = halo_pair(pressure, width, "tile")
-    packed = jnp.concatenate(
-        [
-            jnp.concatenate([edge_below, press_below], axis=1),
-            jnp.concatenate([edge, pressure], axis=1),
-            jnp.concatenate([edge_above, press_above], axis=1),
-        ],
-        axis=0,
-    )
-    field = packed[:, :lanes]
-    speed = packed[:, lanes : 2 * lanes]
-    stiff = packed[:, 2 * lanes : 3 * lanes]
-    press = packed[:, 3 * lanes :]
+    press_below, press_above = halo_pair((pressure,), width, "tile")
+
+    def extended(middle, which):
+        cut = slice(which * lanes, (which + 1) * lanes)
+        return jnp.concatenate([edge_below[:, cut], middle, edge_above[:, cut]], axis=0)
+
+    field = extended(displace, 0)
+    speed = extended(velocity, 1)
+    stiff = extended(stiffness, 2)
+    press = jnp.concatenate([press_below, pressure, press_above], axis=0)
     for _ in range(SUBSTEPS):
         lapl = jnp.roll(field, 1, 0) + jnp.roll(field, -1, 0) + sides(field) - 4.0 * field
         speed = speed + step_dt * (stiff * lapl + press - damping * speed)

time: 84.8 us -> 87.2 us (1.028)
  waiting for transfers between devices: 11.3 us -> 14.5 us
  local copies, waits for them, and re-layouts: 10.7 us -> 9.61 us
    all_to_all x1, waiting for transfers between devices: 0.01 us -> 5.52 us  [body(): got = lax.all_to_all(sent, 'tile', split_axis=0, concat_axis=0, tiled=True)]
    ppermute x8, starting transfers between devices: 8.22 us -> 10.6 us  [tree_sum(): lax.ppermute(value, axis, [(i, i ^ stride) for i in range(count)])]
    ppermute x8, waiting for transfers between devices: 11.3 us -> 9 us  [tree_sum(): lax.ppermute(value, axis, [(i, i ^ stride) for i in range(count)])]
    unnamed x21 -> x19, local copies, waits for them, and re-layouts: 8.69 us -> 7.04 us
    all_to_all x1, starting transfers between devices: 7.41 us -> 5.82 us  [body(): got = lax.all_to_all(sent, 'tile', split_axis=0, concat_axis=0, tiled=True)]
    slice x2 -> x5, local copies, waits for them, and re-layouts: 0.01 us -> 1.46 us  [the longest x3 1.45 us: halo_pair(): tail = jnp.concatenate([part[-width:] for part in parts], axis=1)]
  transfers between devices with their start and end apart: 14 -> 14, of which waited for: 6 -> 7; matrix products, arithmetic and copies ran while one was open for 36% -> 36% of each run, Pallas kernels for 0% -> 0%
where the time goes in v5:
time: 87.2 us; the launch traced here: 86.6 us
  starting transfers between devices  27.9 us (32%)
  other arithmetic  21.1 us (24%)
  waiting for transfers between devices  14.5 us (17%)
  matrix products  12.4 us (14%)
  local copies, waits for them, and re-layouts  9.61 us (11%)
  between operations  1.06 us (1%)
    ppermute x8, starting transfers between devices, tree_sum(): lax.ppermute(value, axis, [(i, i ^ stride) for i in range(count)])  10.6 us
    ppermute x8, waiting for transfers between devices, tree_sum(): lax.ppermute(value, axis, [(i, i ^ stride) for i in range(count)])  9 us
    another operation x6, other arithmetic, inverse_factor(): factor = jnp.linalg.cholesky(matrix)  7.76 us
    unnamed x19, local copies, waits for them, and re-layouts  7.04 us
    another operation x4, other arithmetic, inverse_factor(): return lax.linalg.triangular_solve(factor, eye, left_side=True, lower=True)  6.63 us
    ppermute x2, starting transfers between devices, halo_pair(): lax.ppermute(head, axis, [((i + 1) % count, i) for i in range(count)])  6.61 us
    all_to_all x1, starting transfers between devices, body(): got = lax.all_to_all(sent, 'tile', split_axis=0, concat_axis=0, tiled=True)  5.82 us
    all_to_all x1, waiting for transfers between devices, body(): got = lax.all_to_all(sent, 'tile', split_axis=0, concat_axis=0, tiled=True)  5.52 us
  transfers between devices with their start and end apart: 14, of which 7 were waited for; matrix products, arithmetic and copies ran while one was open for 36% of the time, Pallas kernels for 0%

profile of v5, /device:TPU:0, one launch (start us, length us, event | category | flops | bytes accessed | tf_op | source)
XLA Modules:
  0.0 86.6 jit_solution(14503672535049071532)
XLA Ops:
  0.6 0.7 fusion.79
  1.3 0.7 fusion.77
  2.1 5.5 %collective-permute-start.1 = (f32[4,384]{1,0:T(4,128)S(1)}, f32[4,384]{1,0:T(4,128)S(1)}, u32[]{:S(2)}, u32[]{:S(2)}) collective-permute-start(f32[4,384]{1,0:T(4,128)S(1)} %pad_maximum_fusion.5), channel_id=1, source_target_pairs={{1,0},{2,1},{3,2},{4,3},{5,4},{6,5},{7,6},{8,7},{9,8},{10,9},{11,1... | collective-permute-start | bytes 18440 | tf_op jit(solution)/shard_map/ppermute | solution.py:30
  7.6 0.9 %fusion.3 = f32[128]{0:T(128)S(1)} fusion(s32[128]{0:T(128)} %bitcast.118), kind=kOutput, calls=%fused_computation.6 | convolution fusion | flops 548736 | bytes 1024 | tf_op jit(solution)/shard_map/dot_general | solution.py:76
  8.5 0.7 fusion.54
  9.4 1.6 %select_maximum_fusion = f32[16,17,128]{2,1,0:T(8,128)} fusion(f32[16,1,16]{2,1,0:T(1,128)S(1)} %reshape.105, f32[16,16,128]{2,1,0:T(8,128)} %bitcast.117), kind=kLoop, calls=%fused_computation.17 | loop fusion | flops 104448 | bytes 271360 | tf_op jit(solution)/shard_map/concatenate | solution.py:90
  11.0 5.8 %all-to-all-start = ((f32[16,17,128]{2,1,0:T(8,128)}), f32[16,17,128]{2,1,0:T(8,128)S(1)}, u32[]{:S(2)}, u32[]{:S(2)}) async-start(f32[16,17,128]{2,1,0:T(8,128)} %select_maximum_fusion), calls=%async_computation | async-start | bytes 393216 | tf_op jit(solution)/shard_map/all_to_all | solution.py:91
  16.8 1.9 %pad.51 = bf16[32,256,128]{2,1,0:T(8,128)(2,1)S(1)} pad(bf16[30,256,128]{2,1,0:T(8,128)(2,1)} %param.21, bf16[]{:T(256)} %constant.154), padding=0_2x0_0x0_0 | pad | bytes 4063234
  18.7 1.4 %copy.27 = bf16[4,8,256,128]{3,1,2,0:T(8,128)(2,1)S(1)} copy(bf16[4,8,256,128]{3,2,1,0:T(8,128)(2,1)S(1)} %bitcast.111) | data formatting | bytes 4194304
  20.2 5.5 %all-to-all-done = f32[16,17,128]{2,1,0:T(8,128)S(1)} async-done(((f32[16,17,128]{2,1,0:T(8,128)}), f32[16,17,128]{2,1,0:T(8,128)S(1)}, u32[]{:S(2)}, u32[]{:S(2)}) %all-to-all-start) | async-done | bytes 139296 | tf_op jit(solution)/shard_map/all_to_all | solution.py:91
  25.8 0.3 fusion.11
  26.1 1.1 %collective-permute-start.3 = (f32[4,128]{1,0:T(4,128)S(1)}, f32[4,128]{1,0:T(4,128)S(1)}, u32[]{:S(2)}, u32[]{:S(2)}) collective-permute-start(f32[4,128]{1,0:T(4,128)S(1)} %get-tuple-element.46), channel_id=1, source_target_pairs={{1,0},{2,1},{3,2},{4,3},{5,4},{6,5},{7,6},{8,7},{9,8},{10,9},{11,1... | collective-permute-start | bytes 6152 | tf_op jit(solution)/shard_map/ppermute | solution.py:30
  27.3 2.0 %broadcast_multiply_fusion = bf16[40,256,128]{2,1,0:T(8,128)(2,1)S(1)} fusion(bf16[40,256,128]{2,1,0:T(8,128)(2,1)} %param.18, bf16[256]{0:T(256)(128)(2,1)S(1)} %convert_element_type.39), kind=kLoop, calls=%fused_computation.4 | loop fusion | flops 1310720 | bytes 5243392 | tf_op jit(solution)/shard_map/mul | solution.py:98
  29.3 1.5 %bitcast_dynamic-update-slice_fusion = bf16[70,32768]{1,0:T(8,128)(2,1)S(1)} fusion(bf16[5,8,256,128]{3,2,1,0:T(8,128)(2,1)S(1)} %bitcast.107), kind=kLoop, calls=%fused_computation.3 | loop fusion | bytes 5242880
  31.0 0.3 pad.50
  31.3 1.4 %copy.25 = bf16[4,8,256,128]{3,1,2,0:T(8,128)(2,1)S(1)} copy(bf16[4,8,256,128]{3,2,1,0:T(8,128)(2,1)S(1)} %bitcast.109) | data formatting | bytes 4194304
  32.9 1.5 %fusion.82 = f32[70,70]{0,1:T(8,128)S(1)} fusion(bf16[70,32768]{1,0:T(8,128)(2,1)S(1)} %constant_dynamic-update-slice_fusion), kind=kOutput, calls=%fused_computation.123 | convolution fusion | flops 321126400 | bytes 4607120 | tf_op jit(solution)/shard_map/dot_general | solution.py:103
  34.4 0.6 copy-done
  35.0 0.4 collective-permute-start.4
  36.3 1.4 %collective-permute-start.5 = (f32[70,70]{0,1:T(8,128)S(1)}, f32[70,70]{0,1:T(8,128)S(1)}, u32[]{:S(2)}, u32[]{:S(2)}) collective-permute-start(f32[70,70]{0,1:T(8,128)S(1)} %add.173), channel_id=1, source_target_pairs={{0,2},{1,3},{2,0},{3,1},{4,6},{5,7},{6,4},{7,5},{8,10},{9,11},{10,... | collective-permute-start | bytes 58808 | tf_op jit(solution)/shard_map/ppermute | solution.py:20
  37.8 2.4 %collective-permute-done.5 = f32[70,70]{0,1:T(8,128)S(1)} collective-permute-done((f32[70,70]{0,1:T(8,128)S(1)}, f32[70,70]{0,1:T(8,128)S(1)}, u32[]{:S(2)}, u32[]{:S(2)}) %collective-permute-start.5) | collective-permute-done | bytes 19632 | tf_op jit(solution)/shard_map/ppermute | solution.py:20
  40.3 0.7 collective-permute-start.6
  40.9 0.6 slice_add_fusion
  41.6 2.6 %collective-permute-done.6 = f32[70,70]{0,1:T(8,128)S(1)} collective-permute-done((f32[70,70]{0,1:T(8,128)S(1)}, f32[70,70]{0,1:T(8,128)S(1)}, u32[]{:S(2)}, u32[]{:S(2)}) %collective-permute-start.6) | collective-permute-done | bytes 19632 | tf_op jit(solution)/shard_map/ppermute | solution.py:20
  44.2 1.5 %collective-permute-start.7 = (f32[70,70]{0,1:T(8,128)S(1)}, f32[70,70]{0,1:T(8,128)S(1)}, u32[]{:S(2)}, u32[]{:S(2)}) collective-permute-start(f32[70,70]{0,1:T(8,128)S(1)} %add.175), channel_id=1, source_target_pairs={{0,8},{1,9},{2,10},{3,11},{4,12},{5,13},{6,14},{7,15},{8,0},{9,1},... | collective-permute-start | bytes 58808 | tf_op jit(solution)/shard_map/ppermute | solution.py:20
  45.8 1.0 %fusion.10 = f32[256,128]{1,0:T(8,128)} fusion(f32[128,128]{1,0:T(8,128)S(1)} %get-tuple-element.15, s32[128]{0:T(128)S(1)} %fusion.54), kind=kOutput, calls=%fused_computation.26 | convolution fusion | flops 50364416 | bytes 197120 | tf_op jit(solution)/shard_map/dot_general | solution.py:127
  46.8 4.8 %all-to-all-start.1 = ((f32[16,16,128]{2,1,0:T(8,128)}), f32[16,16,128]{2,1,0:T(8,128)S(1)}, u32[]{:S(2)}, u32[]{:S(2)}) async-start(f32[16,16,128]{2,1,0:T(8,128)} %bitcast.5), calls=%async_computation.1 | async-start | bytes 262144 | tf_op jit(solution)/shard_map/all_to_all | solution.py:128
  51.9 3.7 %cholesky.31 = f32[40,40]{1,0:T(8,128)S(1)} custom-call(f32[40,40]{1,0:T(8,128)S(1)} %copy.21), custom_call_target="Cholesky" | custom-call | tf_op jit(solution)/shard_map/jit(cholesky)/cholesky | solution.py:42
  55.5 0.7 compare_reduce_fusion.1
  56.4 0.6 fusion.38
  57.0 3.1 %custom-call.12 = f32[1,40,40]{1,2,0:T(8,128)S(1)} custom-call(f32[1,40,40]{2,1,0:T(8,128)S(1)} %fusion.38), custom_call_target="InvertDiagBlocksLowerTriangular" | custom-call | tf_op jit(solution)/shard_map/triangular_solve | solution.py:44
  60.1 2.7 %cholesky.65 = f32[30,30]{1,0:T(8,128)S(1)} custom-call(f32[30,30]{1,0:T(8,128)S(1)} %fusion.48), custom_call_target="Cholesky" | custom-call | tf_op jit(solution)/shard_map/jit(cholesky)/cholesky | solution.py:42
  62.8 0.2 fusion.41
  63.3 3.7 %convolution_bitcast_fusion = f32[70]{0:T(128)S(1)} fusion(bf16[70,32768]{1,0:T(8,128)(2,1)} %copy-done, bf16[32768,1]{0,1:T(2,128)(2,1)S(1)} %reshape.113), kind=kOutput, calls=%fused_computation.7 | convolution fusion | flops 4587520 | bytes 4653336 | tf_op jit(solution)/shard_map/dot_general | solution.py:130
  66.9 0.4 collective-permute-start.8
  67.4 0.8 collective-permute-done.8
  68.2 1.9 %collective-permute-start.9 = (f32[70]{0:T(128)S(1)}, f32[70]{0:T(128)S(1)}, u32[]{:S(2)}, u32[]{:S(2)}) collective-permute-start(f32[70]{0:T(128)S(1)} %add.178), channel_id=1, source_target_pairs={{0,2},{1,3},{2,0},{3,1},{4,6},{5,7},{6,4},{7,5},{8,10},{9,11},{10,... | collective-permute-start | bytes 848 | tf_op jit(solution)/shard_map/ppermute | solution.py:20
  70.0 0.6 compare_reduce_fusion
  70.7 1.1 %collective-permute-done.9 = f32[70]{0:T(128)S(1)} collective-permute-done((f32[70]{0:T(128)S(1)}, f32[70]{0:T(128)S(1)}, u32[]{:S(2)}, u32[]{:S(2)}) %collective-permute-start.9) | collective-permute-done | bytes 312 | tf_op jit(solution)/shard_map/ppermute | solution.py:20
  71.8 1.9 %collective-permute-start.10 = (f32[70]{0:T(128)S(1)}, f32[70]{0:T(128)S(1)}, u32[]{:S(2)}, u32[]{:S(2)}) collective-permute-start(f32[70]{0:T(128)S(1)} %add.179), channel_id=1, source_target_pairs={{0,4},{1,5},{2,6},{3,7},{4,0},{5,1},{6,2},{7,3},{8,12},{9,13},{10,... | collective-permute-start | bytes 848 | tf_op jit(solution)/shard_map/ppermute | solution.py:20
  73.6 0.7 fusion.44
  74.3 2.3 %custom-call.13 = f32[1,30,30]{1,2,0:T(8,128)S(1)} custom-call(f32[1,30,30]{2,1,0:T(8,128)S(1)} %fusion.44), custom_call_target="InvertDiagBlocksLowerTriangular" | custom-call | tf_op jit(solution)/shard_map/triangular_solve | solution.py:44
  76.6 2.4 %collective-permute-start.11 = (f32[70]{0:T(128)S(1)}, f32[70]{0:T(128)S(1)}, u32[]{:S(2)}, u32[]{:S(2)}) collective-permute-start(f32[70]{0:T(128)S(1)} %add.180), channel_id=1, source_target_pairs={{0,8},{1,9},{2,10},{3,11},{4,12},{5,13},{6,14},{7,15},{8,0},{9,1},... | collective-permute-start | bytes 848 | tf_op jit(solution)/shard_map/ppermute | solution.py:20
  79.2 1.9 %collective-permute-done.11 = f32[70]{0:T(128)S(1)} collective-permute-done((f32[70]{0:T(128)S(1)}, f32[70]{0:T(128)S(1)}, u32[]{:S(2)}, u32[]{:S(2)}) %collective-permute-start.11) | collective-permute-done | bytes 312 | tf_op jit(solution)/shard_map/ppermute | solution.py:20
  81.4 0.2 convolution_bitcast_fusion.3
  81.6 3.5 %fusion = f32[1,32768]{1,0:T(1,128)S(1)} fusion(bf16[5,8,256,128]{3,2,1,0:T(8,128)(2,1)} %bitcast.112, f32[40]{0:T(128)S(1)} %fusion.4), kind=kOutput, calls=%fused_computation | convolution fusion | flops 2621480 | bytes 2752672 | tf_op jit(solution)/shard_map/dot_general | solution.py:136
  85.5 0.4 fusion.83
  85.8 0.8 fusion.7
  (78 shorter events, 3.2 us)
Async XLA Ops:
  2.1 18.0 %collective-permute-start.1 = (f32[4,384]{1,0:T(4,128)S(1)}, f32[4,384]{1,0:T(4,128)S(1)}, u32[]{:S(2)}, u32[]{:S(2)}) collective-permute-start(f32[4,384]{1,0:T(4,128)S(1)} %pad_maximum_fusion.5), channel_id=1, source_target_pairs={{1,0},{2,1},{3,2},{4,3},{5,4},{6,5},{7,6},{8,7},{9,8},{10,9},{11,1... | collective-permute-start | bytes 18440 | tf_op jit(solution)/shard_map/ppermute | solution.py:30
  7.6 12.5 %collective-permute-start = (f32[4,384]{1,0:T(4,128)S(1)}, f32[4,384]{1,0:T(4,128)S(1)}, u32[]{:S(2)}, u32[]{:S(2)}) collective-permute-start(f32[4,384]{1,0:T(4,128)S(1)} %pad_maximum_fusion.4), channel_id=1, source_target_pairs={{0,1},{1,2},{2,3},{3,4},{4,5},{5,6},{6,7},{7,8},{8,9},{9,10},{10,1... | collective-permute-start | bytes 18440 | tf_op jit(solution)/shard_map/ppermute | solution.py:29
  11.0 14.8 %all-to-all-start = ((f32[16,17,128]{2,1,0:T(8,128)}), f32[16,17,128]{2,1,0:T(8,128)S(1)}, u32[]{:S(2)}, u32[]{:S(2)}) async-start(f32[16,17,128]{2,1,0:T(8,128)} %select_maximum_fusion), calls=%async_computation | async-start | bytes 393216 | tf_op jit(solution)/shard_map/all_to_all | solution.py:91
  18.7 1.4 %copy-start.3 = (f32[128,128]{1,0:T(8,128)S(1)}, f32[128,128]{1,0:T(8,128)}, u32[]{:S(2)}) copy-start(f32[128,128]{1,0:T(8,128)} %param.14) | copy-start | bytes 196612
  26.1 9.4 %collective-permute-start.3 = (f32[4,128]{1,0:T(4,128)S(1)}, f32[4,128]{1,0:T(4,128)S(1)}, u32[]{:S(2)}, u32[]{:S(2)}) collective-permute-start(f32[4,128]{1,0:T(4,128)S(1)} %get-tuple-element.46), channel_id=1, source_target_pairs={{1,0},{2,1},{3,2},{4,3},{5,4},{6,5},{7,6},{8,7},{9,8},{10,9},{11,1... | collective-permute-start | bytes 6152 | tf_op jit(solution)/shard_map/ppermute | solution.py:30
  27.1 8.3 %collective-permute-start.2 = (f32[4,128]{1,0:T(4,128)S(1)}, f32[4,128]{1,0:T(4,128)S(1)}, u32[]{:S(2)}, u32[]{:S(2)}) collective-permute-start(f32[4,128]{1,0:T(4,128)S(1)} %get-tuple-element.45), channel_id=1, source_target_pairs={{0,1},{1,2},{2,3},{3,4},{4,5},{5,6},{6,7},{7,8},{8,9},{9,10},{10,1... | collective-permute-start | bytes 6152 | tf_op jit(solution)/shard_map/ppermute | solution.py:29
  29.3 1.5 %copy-start.1 = (bf16[30,256,128]{2,1,0:T(8,128)(2,1)S(1)}, bf16[30,256,128]{2,1,0:T(8,128)(2,1)}, u32[]{:S(2)}) copy-start(bf16[30,256,128]{2,1,0:T(8,128)(2,1)} %param.20) | copy-start | bytes 5898244
  32.8 2.1 %copy-start = (bf16[70,32768]{1,0:T(8,128)(2,1)}, bf16[70,32768]{1,0:T(8,128)(2,1)S(1)}, u32[]{:S(2)}) copy-start(bf16[70,32768]{1,0:T(8,128)(2,1)S(1)} %constant_dynamic-update-slice_fusion) | copy-start | bytes 13762564
  32.8 2.6 %copy-start.2 = (f32[128,128]{1,0:T(8,128)S(1)}, f32[128,128]{1,0:T(8,128)}, u32[]{:S(2)}) copy-start(f32[128,128]{1,0:T(8,128)} %param.16) | copy-start | bytes 196612
  32.9 2.6 %copy-start.6 = (f32[128,128]{1,0:T(8,128)S(1)}, f32[128,128]{1,0:T(8,128)}, u32[]{:S(2)}) copy-start(f32[128,128]{1,0:T(8,128)} %param.15) | copy-start | bytes 196612
  35.0 1.3 %collective-permute-start.4 = (f32[70,70]{0,1:T(8,128)S(1)}, f32[70,70]{0,1:T(8,128)S(1)}, u32[]{:S(2)}, u32[]{:S(2)}) collective-permute-start(f32[70,70]{0,1:T(8,128)S(1)} %fusion.82), channel_id=1, source_target_pairs={{0,1},{1,0},{2,3},{3,2},{4,5},{5,4},{6,7},{7,6},{8,9},{9,8},{10,11... | collective-permute-start | bytes 58808 | tf_op jit(solution)/shard_map/ppermute | solution.py:20
  35.6 27.5 %copy-start.5 = (f32[256,128]{1,0:T(8,128)S(1)}, f32[256,128]{1,0:T(8,128)}, u32[]{:S(2)}) copy-start(f32[256,128]{1,0:T(8,128)} %param.13) | copy-start | bytes 393220
  36.3 4.0 %collective-permute-start.5 = (f32[70,70]{0,1:T(8,128)S(1)}, f32[70,70]{0,1:T(8,128)S(1)}, u32[]{:S(2)}, u32[]{:S(2)}) collective-permute-start(f32[70,70]{0,1:T(8,128)S(1)} %add.173), channel_id=1, source_target_pairs={{0,2},{1,3},{2,0},{3,1},{4,6},{5,7},{6,4},{7,5},{8,10},{9,11},{10,... | collective-permute-start | bytes 58808 | tf_op jit(solution)/shard_map/ppermute | solution.py:20
  40.3 4.0 %collective-permute-start.6 = (f32[70,70]{0,1:T(8,128)S(1)}, f32[70,70]{0,1:T(8,128)S(1)}, u32[]{:S(2)}, u32[]{:S(2)}) collective-permute-start(f32[70,70]{0,1:T(8,128)S(1)} %add.174), channel_id=1, source_target_pairs={{0,4},{1,5},{2,6},{3,7},{4,0},{5,1},{6,2},{7,3},{8,12},{9,13},{10,... | collective-permute-start | bytes 58808 | tf_op jit(solution)/shard_map/ppermute | solution.py:20
  41.6 25.4 %copy-start.4 = (f32[128,128]{1,0:T(8,128)}, f32[128,128]{1,0:T(8,128)S(1)}, u32[]{:S(2)}) copy-start(f32[128,128]{1,0:T(8,128)S(1)} %get-tuple-element.15) | copy-start | bytes 196612
  44.2 7.4 %collective-permute-start.7 = (f32[70,70]{0,1:T(8,128)S(1)}, f32[70,70]{0,1:T(8,128)S(1)}, u32[]{:S(2)}, u32[]{:S(2)}) collective-permute-start(f32[70,70]{0,1:T(8,128)S(1)} %add.175), channel_id=1, source_target_pairs={{0,8},{1,9},{2,10},{3,11},{4,12},{5,13},{6,14},{7,15},{8,0},{9,1},... | collective-permute-start | bytes 58808 | tf_op jit(solution)/shard_map/ppermute | solution.py:20
  46.8 16.3 %all-to-all-start.1 = ((f32[16,16,128]{2,1,0:T(8,128)}), f32[16,16,128]{2,1,0:T(8,128)S(1)}, u32[]{:S(2)}, u32[]{:S(2)}) async-start(f32[16,16,128]{2,1,0:T(8,128)} %bitcast.5), calls=%async_computation.1 | async-start | bytes 262144 | tf_op jit(solution)/shard_map/all_to_all | solution.py:128
  66.9 1.2 %collective-permute-start.8 = (f32[70]{0:T(128)S(1)}, f32[70]{0:T(128)S(1)}, u32[]{:S(2)}, u32[]{:S(2)}) collective-permute-start(f32[70]{0:T(128)S(1)} %convolution_bitcast_fusion), channel_id=1, source_target_pairs={{0,1},{1,0},{2,3},{3,2},{4,5},{5,4},{6,7},{7,6},{8,9},{9,8},{10,11... | collective-permute-start | bytes 848 | tf_op jit(solution)/shard_map/ppermute | solution.py:20
  68.2 3.6 %collective-permute-start.9 = (f32[70]{0:T(128)S(1)}, f32[70]{0:T(128)S(1)}, u32[]{:S(2)}, u32[]{:S(2)}) collective-permute-start(f32[70]{0:T(128)S(1)} %add.178), channel_id=1, source_target_pairs={{0,2},{1,3},{2,0},{3,1},{4,6},{5,7},{6,4},{7,5},{8,10},{9,11},{10,... | collective-permute-start | bytes 848 | tf_op jit(solution)/shard_map/ppermute | solution.py:20
  71.8 4.8 %collective-permute-start.10 = (f32[70]{0:T(128)S(1)}, f32[70]{0:T(128)S(1)}, u32[]{:S(2)}, u32[]{:S(2)}) collective-permute-start(f32[70]{0:T(128)S(1)} %add.179), channel_id=1, source_target_pairs={{0,4},{1,5},{2,6},{3,7},{4,0},{5,1},{6,2},{7,3},{8,12},{9,13},{10,... | collective-permute-start | bytes 848 | tf_op jit(solution)/shard_map/ppermute | solution.py:20
  76.6 4.5 %collective-permute-start.11 = (f32[70]{0:T(128)S(1)}, f32[70]{0:T(128)S(1)}, u32[]{:S(2)}, u32[]{:S(2)}) collective-permute-start(f32[70]{0:T(128)S(1)} %add.180), channel_id=1, source_target_pairs={{0,8},{1,9},{2,10},{3,11},{4,12},{5,13},{6,14},{7,15},{8,0},{9,1},... | collective-permute-start | bytes 848 | tf_op jit(solution)/shard_map/ppermute | solution.py:20

commit v6 on v2

--- a/solution.py
+++ b/solution.py
@@ -26,6 +26,10 @@
     below = lax.ppermute(cells[-width:], axis, [(i, (i + 1) % count) for i in range(count)])
     above = lax.ppermute(cells[:width], axis, [((i + 1) % count, i) for i in range(count)])
     return below, above
+
+
+def to_half(value):
+    return lax.reduce_precision(value, exponent_bits=8, mantissa_bits=7)
 
 
 def sides(center):
@@ -127,24 +131,24 @@
 
     outgoing = jnp.dot(chooser.T, field, precision=high)
     x_tilde = lax.all_to_all(outgoing, "tile", split_axis=0, concat_axis=0, tiled=True)
-    resid = (mask[:, None] * (x_tilde - iterate)).astype(jnp.bfloat16).reshape(-1)
-    inner = tree_sum(jnp.dot(cols, resid, preferred_element_type=jnp.float32), "tile")
+    resid = to_half(mask[:, None] * (x_tilde - iterate))
+    inner = jnp.concatenate(
+        [
+            jnp.sum(diff_cur.astype(jnp.float32) * resid[None], axis=(1, 2)),
+            jnp.sum(diff_past.astype(jnp.float32) * resid[None], axis=(1, 2)),
+        ]
+    )
+    inner = tree_sum(inner, "tile")
     rhs_cur = inner[:n_cur]
     rhs_past = inner[n_cur:]
     coeff = -solve_spd(inv_cur, rhs_cur)
     projected = rhs_past + jnp.dot(cross, coeff, precision=high)
     past = solve_spd(inv_past, projected)
-    upd_cur = jnp.dot(
-        coeff.astype(jnp.bfloat16),
-        step_cur.reshape(step_cur.shape[0], -1),
-        preferred_element_type=jnp.float32,
-    )
-    upd_past = jnp.dot(
-        past.astype(jnp.bfloat16),
-        step_past.reshape(step_past.shape[0], -1),
-        preferred_element_type=jnp.float32,
-    )
-    update = (upd_cur - upd_past).reshape(x_tilde.shape)
+    coeff_half = to_half(coeff)
+    past_half = to_half(past)
+    upd_cur = jnp.sum(coeff_half[:, None, None] * step_cur.astype(jnp.float32), axis=0)
+    upd_past = jnp.sum(past_half[:, None, None] * step_past.astype(jnp.float32), axis=0)
+    update = upd_cur - upd_past
     new_iterate = mask[:, None] * (x_tilde + update)
     return (new_iterate, field, speed)
 

time: 84.8 us -> 82.7 us (0.975)
  matrix products: 12.4 us -> 4.79 us
  other arithmetic: 21.2 us -> 27.1 us
  local copies, waits for them, and re-layouts: 10.7 us -> 7.14 us
  waiting for transfers between devices: 11.3 us -> 13.2 us
  starting transfers between devices: 27.5 us -> 28.9 us
    dot_general x3 -> x0, matrix products: 7.53 us -> none  [the longest x1 3.66 us: local(): jnp.dot(cols, resid, preferred_element_type=jnp.float32)]
    reduce_sum x0 -> x4, other arithmetic: none -> 5.94 us  [the longest x1 2.38 us: local(): jnp.sum(coeff_half[:, None, None] * step_cur.astype(jnp.float32), axis=0)]
    unnamed x21 -> x19, local copies, waits for them, and re-layouts: 8.69 us -> 5.38 us
    mul x1, other arithmetic: 1.99 us -> 0.25 us  [local(): diff_cur * mask_half[None, :, None]]
    mul x1, other arithmetic: 0.21 us -> 1.76 us  [local(): diff_past * mask_half[None, :, None]]
    ppermute x2, waiting for transfers between devices: 0.01 us -> 1.48 us  [halo_pair(): lax.ppermute(cells[-width:], axis, [(i, (i + 1) % count) for i in range(c...]
    ppermute x2, starting transfers between devices: 6.56 us -> 7.86 us  [halo_pair(): lax.ppermute(cells[:width], axis, [((i + 1) % count, i) for i in range(co...]
  transfers between devices with their start and end apart: 14 -> 14, of which waited for: 6 -> 8; matrix products, arithmetic and copies ran while one was open for 36% -> 33% of each run, Pallas kernels for 0% -> 0%
where the time goes in v6:
time: 82.7 us; the launch traced here: 82.1 us
  starting transfers between devices  28.9 us (35%)
  other arithmetic  27.1 us (33%)
  waiting for transfers between devices  13.2 us (16%)
  local copies, waits for them, and re-layouts  7.14 us (9%)
  matrix products  4.79 us (6%)
  between operations  1.01 us (1%)
    ppermute x8, waiting for transfers between devices, tree_sum(): lax.ppermute(value, axis, [(i, i ^ stride) for i in range(count)])  11.3 us
    ppermute x8, starting transfers between devices, tree_sum(): lax.ppermute(value, axis, [(i, i ^ stride) for i in range(count)])  8.27 us
    ppermute x2, starting transfers between devices, halo_pair(): lax.ppermute(cells[:width], axis, [((i + 1) % count, i) for i in range(co...  7.86 us
    another operation x6, other arithmetic, inverse_factor(): factor = jnp.linalg.cholesky(matrix)  7.81 us
    all_to_all x1, starting transfers between devices, local(): got = lax.all_to_all(sent, 'tile', split_axis=0, concat_axis=0, tiled=True)  7.41 us
    another operation x4, other arithmetic, inverse_factor(): return lax.linalg.triangular_solve(factor, eye, left_side=True, lower=True)  6.68 us
    unnamed x19, local copies, waits for them, and re-layouts  5.38 us
    all_to_all x1, starting transfers between devices, local(): lax.all_to_all(outgoing, 'tile', split_axis=0, concat_axis=0, tiled=True)  4.87 us
  transfers between devices with their start and end apart: 14, of which 8 were waited for; matrix products, arithmetic and copies ran while one was open for 33% of the time, Pallas kernels for 0%

profile of v6, /device:TPU:0, one launch (start us, length us, event | category | flops | bytes accessed | tf_op | source)
XLA Modules:
  0.0 82.1 jit_solution(12504729941210386623)
XLA Ops:
  0.6 0.9 %fusion.4 = f32[128]{0:T(128)S(1)} fusion(s32[128]{0:T(128)} %bitcast.89), kind=kOutput, calls=%fused_computation.11 | convolution fusion | flops 548736 | bytes 1024 | tf_op jit(solution)/shard_map/dot_general | solution.py:77
  1.5 0.7 fusion.53
  2.4 1.6 %select_maximum_fusion = f32[16,17,128]{2,1,0:T(8,128)} fusion(f32[16,1,16]{2,1,0:T(1,128)S(1)} %reshape.96, f32[16,16,128]{2,1,0:T(8,128)} %bitcast.88), kind=kLoop, calls=%fused_computation.21 | loop fusion | flops 104448 | bytes 271360 | tf_op jit(solution)/shard_map/concatenate | solution.py:92
  4.0 7.4 %all-to-all-start = ((f32[16,17,128]{2,1,0:T(8,128)}), f32[16,17,128]{2,1,0:T(8,128)S(1)}, u32[]{:S(2)}, u32[]{:S(2)}) async-start(f32[16,17,128]{2,1,0:T(8,128)} %select_maximum_fusion), calls=%async_computation | async-start | bytes 393216 | tf_op jit(solution)/shard_map/all_to_all | solution.py:93
  11.4 0.8 %constant_dynamic-update-slice_fusion.2 = f32[128,384]{1,0:T(8,128)S(1)} fusion(f32[128,128]{1,0:T(8,128)} %param.14), kind=kLoop, calls=%fused_computation.89 | loop fusion | bytes 131072
  12.2 0.8 %constant_dynamic-update-slice_fusion.1 = f32[128,384]{1,0:T(8,128)S(1)} fusion(f32[128,384]{1,0:T(8,128)S(1)} %constant_dynamic-update-slice_fusion.2, f32[128,128]{1,0:T(8,128)} %param.15), kind=kLoop, calls=%fused_computation.88 | loop fusion | bytes 131072
  13.1 0.8 %constant_dynamic-update-slice_fusion = f32[128,384]{1,0:T(8,128)S(1)} fusion(f32[128,384]{1,0:T(8,128)S(1)} %constant_dynamic-update-slice_fusion.1, f32[128,128]{1,0:T(8,128)} %param.16), kind=kLoop, calls=%fused_computation.87 | loop fusion | bytes 131072 | tf_op jit(solution)/shard_map/concatenate | solution.py:87
  13.9 0.5 collective-permute-start
  14.4 4.0 %collective-permute-start.2 = (f32[4,384]{1,0:T(4,128)S(1)}, f32[4,384]{1,0:T(4,128)S(1)}, u32[]{:S(2)}, u32[]{:S(2)}) collective-permute-start(f32[4,384]{1,0:T(4,128)S(1)} %get-tuple-element.28), channel_id=1, source_target_pairs={{1,0},{2,1},{3,2},{4,3},{5,4},{6,5},{7,6},{8,7},{9,8},{10,9},{11,1... | collective-permute-start | bytes 18440 | tf_op jit(solution)/shard_map/ppermute | solution.py:27
  18.4 1.5 %collective-permute-done = f32[4,384]{1,0:T(4,128)S(1)} collective-permute-done((f32[4,384]{1,0:T(4,128)S(1)}, f32[4,384]{1,0:T(4,128)S(1)}, u32[]{:S(2)}, u32[]{:S(2)}) %collective-permute-start) | collective-permute-done | bytes 6176 | tf_op jit(solution)/shard_map/ppermute | solution.py:26
  19.9 0.5 all-to-all-done
  20.4 0.3 fusion.11
  20.7 3.8 %collective-permute-start.3 = (f32[4,128]{1,0:T(4,128)S(1)}, f32[4,128]{1,0:T(4,128)S(1)}, u32[]{:S(2)}, u32[]{:S(2)}) collective-permute-start(f32[4,128]{1,0:T(4,128)S(1)} %get-tuple-element.48), channel_id=1, source_target_pairs={{1,0},{2,1},{3,2},{4,3},{5,4},{6,5},{7,6},{8,7},{9,8},{10,9},{11,1... | collective-permute-start | bytes 6152 | tf_op jit(solution)/shard_map/ppermute | solution.py:27
  24.7 1.8 %broadcast_multiply_fusion.1 = bf16[30,256,128]{2,1,0:T(8,128)(2,1)S(1)} fusion(bf16[30,256,128]{2,1,0:T(8,128)(2,1)} %param.20, bf16[256]{0:T(256)(128)(2,1)S(1)} %convert_element_type.42), kind=kLoop, calls=%fused_computation.19 | loop fusion | flops 983040 | bytes 3932672 | tf_op jit(solution)/shard_map/mul | solution.py:101
  26.4 0.2 pad.44
  26.7 1.4 %copy.25 = bf16[4,8,256,128]{3,1,2,0:T(8,128)(2,1)S(1)} copy(bf16[4,8,256,128]{3,2,1,0:T(8,128)(2,1)S(1)} %bitcast.84) | data formatting | bytes 4194304
  28.0 0.4 copy-done
  28.4 0.2 broadcast_multiply_fusion
  28.7 1.7 %copy.27 = bf16[5,8,256,128]{3,1,2,0:T(8,128)(2,1)S(1)} copy(bf16[5,8,256,128]{3,2,1,0:T(8,128)(2,1)S(1)} %bitcast.83) | data formatting | bytes 5242880
  30.4 1.4 %fusion = f32[70,70]{0,1:T(8,128)S(1)} fusion(bf16[30,32768]{1,0:T(8,128)(2,1)S(1)} %bitcast.86, bf16[40,32768]{1,0:T(8,128)(2,1)S(1)} %bitcast.85), kind=kOutput, calls=%fused_computation.2 | convolution fusion | flops 330301440 | bytes 4607120 | tf_op jit(solution)/shard_map/dot_general | solution.py:105
  32.7 0.3 collective-permute-done.4
  33.2 3.8 %collective-permute-done.5 = f32[70,70]{0,1:T(8,128)S(1)} collective-permute-done((f32[70,70]{0,1:T(8,128)S(1)}, f32[70,70]{0,1:T(8,128)S(1)}, u32[]{:S(2)}, u32[]{:S(2)}) %collective-permute-start.5) | collective-permute-done | bytes 19632 | tf_op jit(solution)/shard_map/ppermute | solution.py:19
  37.0 0.6 slice_add_fusion
  37.7 3.3 %collective-permute-done.6 = f32[70,70]{0,1:T(8,128)S(1)} collective-permute-done((f32[70,70]{0,1:T(8,128)S(1)}, f32[70,70]{0,1:T(8,128)S(1)}, u32[]{:S(2)}, u32[]{:S(2)}) %collective-permute-start.6) | collective-permute-done | bytes 19632 | tf_op jit(solution)/shard_map/ppermute | solution.py:19
  41.0 1.6 %collective-permute-start.7 = (f32[70,70]{0,1:T(8,128)S(1)}, f32[70,70]{0,1:T(8,128)S(1)}, u32[]{:S(2)}, u32[]{:S(2)}) collective-permute-start(f32[70,70]{0,1:T(8,128)S(1)} %add.175), channel_id=1, source_target_pairs={{0,8},{1,9},{2,10},{3,11},{4,12},{5,13},{6,14},{7,15},{8,0},{9,1},... | collective-permute-start | bytes 58808 | tf_op jit(solution)/shard_map/ppermute | solution.py:19
  42.6 1.0 %fusion.10 = f32[256,128]{1,0:T(8,128)} fusion(f32[128,128]{1,0:T(8,128)S(1)} %get-tuple-element.15, s32[128]{0:T(128)S(1)} %fusion.53), kind=kOutput, calls=%fused_computation.30 | convolution fusion | flops 50364416 | bytes 197120 | tf_op jit(solution)/shard_map/dot_general | solution.py:132
  43.7 4.9 %all-to-all-start.1 = ((f32[16,16,128]{2,1,0:T(8,128)}), f32[16,16,128]{2,1,0:T(8,128)S(1)}, u32[]{:S(2)}, u32[]{:S(2)}) async-start(f32[16,16,128]{2,1,0:T(8,128)} %bitcast.5), calls=%async_computation.1 | async-start | bytes 262144 | tf_op jit(solution)/shard_map/all_to_all | solution.py:133
  48.8 3.7 %cholesky.31 = f32[40,40]{1,0:T(8,128)S(1)} custom-call(f32[40,40]{1,0:T(8,128)S(1)} %copy.21), custom_call_target="Cholesky" | custom-call | tf_op jit(solution)/shard_map/jit(cholesky)/cholesky | solution.py:43
  52.5 0.7 compare_reduce_fusion.1
  53.4 0.7 fusion.38
  54.1 3.1 %custom-call.12 = f32[1,40,40]{1,2,0:T(8,128)S(1)} custom-call(f32[1,40,40]{2,1,0:T(8,128)S(1)} %fusion.38), custom_call_target="InvertDiagBlocksLowerTriangular" | custom-call | tf_op jit(solution)/shard_map/triangular_solve | solution.py:45
  57.1 2.7 %cholesky.65 = f32[30,30]{1,0:T(8,128)S(1)} custom-call(f32[30,30]{1,0:T(8,128)S(1)} %fusion.48), custom_call_target="Cholesky" | custom-call | tf_op jit(solution)/shard_map/jit(cholesky)/cholesky | solution.py:43
  59.9 0.2 fusion.41
  60.2 2.2 %multiply_reduce_fusion.3 = f32[30]{0:T(128)S(1)} fusion(bf16[30,256,128]{2,1,0:T(8,128)(2,1)} %param.20, f32[256,128]{1,0:T(8,128)S(1)} %fusion.8), kind=kLoop, calls=%fused_computation.7 | loop fusion | flops 2949090 | bytes 2097272 | tf_op jit(solution)/shard_map/reduce_sum | solution.py:138
  62.4 0.8 %multiply_reduce_fusion.1 = f32[40]{0:T(128)S(1)} fusion(bf16[40,256,128]{2,1,0:T(8,128)(2,1)S(1)} %copy-done, f32[256,128]{1,0:T(8,128)S(1)} %fusion.8), kind=kLoop, calls=%fused_computation.1 | loop fusion | flops 3932120 | bytes 2752672 | tf_op jit(solution)/shard_map/reduce_sum | solution.py:137
  63.3 0.4 collective-permute-start.8
  63.8 0.8 collective-permute-done.8
  64.6 1.9 %collective-permute-start.9 = (f32[70]{0:T(128)S(1)}, f32[70]{0:T(128)S(1)}, u32[]{:S(2)}, u32[]{:S(2)}) collective-permute-start(f32[70]{0:T(128)S(1)} %fusion.83), channel_id=1, source_target_pairs={{0,2},{1,3},{2,0},{3,1},{4,6},{5,7},{6,4},{7,5},{8,10},{9,11},{10,... | collective-permute-start | bytes 848 | tf_op jit(solution)/shard_map/ppermute | solution.py:19
  66.5 0.6 compare_reduce_fusion
  67.1 1.1 %collective-permute-done.9 = f32[70]{0:T(128)S(1)} collective-permute-done((f32[70]{0:T(128)S(1)}, f32[70]{0:T(128)S(1)}, u32[]{:S(2)}, u32[]{:S(2)}) %collective-permute-start.9) | collective-permute-done | bytes 312 | tf_op jit(solution)/shard_map/ppermute | solution.py:19
  68.2 1.9 %collective-permute-start.10 = (f32[70]{0:T(128)S(1)}, f32[70]{0:T(128)S(1)}, u32[]{:S(2)}, u32[]{:S(2)}) collective-permute-start(f32[70]{0:T(128)S(1)} %add.179), channel_id=1, source_target_pairs={{0,4},{1,5},{2,6},{3,7},{4,0},{5,1},{6,2},{7,3},{8,12},{9,13},{10,... | collective-permute-start | bytes 848 | tf_op jit(solution)/shard_map/ppermute | solution.py:19
  70.1 0.7 fusion.44
  70.7 2.3 %custom-call.13 = f32[1,30,30]{1,2,0:T(8,128)S(1)} custom-call(f32[1,30,30]{2,1,0:T(8,128)S(1)} %fusion.44), custom_call_target="InvertDiagBlocksLowerTriangular" | custom-call | tf_op jit(solution)/shard_map/triangular_solve | solution.py:45
  73.1 2.4 %collective-permute-start.11 = (f32[70]{0:T(128)S(1)}, f32[70]{0:T(128)S(1)}, u32[]{:S(2)}, u32[]{:S(2)}) collective-permute-start(f32[70]{0:T(128)S(1)} %add.180), channel_id=1, source_target_pairs={{0,8},{1,9},{2,10},{3,11},{4,12},{5,13},{6,14},{7,15},{8,0},{9,1},... | collective-permute-start | bytes 848 | tf_op jit(solution)/shard_map/ppermute | solution.py:19
  75.7 1.9 %collective-permute-done.11 = f32[70]{0:T(128)S(1)} collective-permute-done((f32[70]{0:T(128)S(1)}, f32[70]{0:T(128)S(1)}, u32[]{:S(2)}, u32[]{:S(2)}) %collective-permute-start.11) | collective-permute-done | bytes 312 | tf_op jit(solution)/shard_map/ppermute | solution.py:19
  78.5 2.4 %multiply_reduce_fusion = f32[256,128]{1,0:T(8,128)S(1)} fusion(bf16[40,256,128]{2,1,0:T(8,128)(2,1)} %param.19, f32[40]{0:T(128)S(1)} %get-tuple-element.49), kind=kLoop, calls=%fused_computation | loop fusion | flops 3899392 | bytes 2752672 | tf_op jit(solution)/shard_map/reduce_sum | solution.py:149
  80.8 0.5 multiply_reduce_fusion.2
  81.4 0.8 fusion.9
  (74 shorter events, 3.1 us)
Async XLA Ops:
  4.0 16.4 %all-to-all-start = ((f32[16,17,128]{2,1,0:T(8,128)}), f32[16,17,128]{2,1,0:T(8,128)S(1)}, u32[]{:S(2)}, u32[]{:S(2)}) async-start(f32[16,17,128]{2,1,0:T(8,128)} %select_maximum_fusion), calls=%async_computation | async-start | bytes 393216 | tf_op jit(solution)/shard_map/all_to_all | solution.py:93
  13.9 6.0 %collective-permute-start = (f32[4,384]{1,0:T(4,128)S(1)}, f32[4,384]{1,0:T(4,128)S(1)}, u32[]{:S(2)}, u32[]{:S(2)}) collective-permute-start(f32[4,384]{1,0:T(4,128)S(1)} %get-tuple-element.27), channel_id=1, source_target_pairs={{0,1},{1,2},{2,3},{3,4},{4,5},{5,6},{6,7},{7,8},{8,9},{9,10},{10,1... | collective-permute-start | bytes 18440 | tf_op jit(solution)/shard_map/ppermute | solution.py:26
  14.4 5.5 %collective-permute-start.2 = (f32[4,384]{1,0:T(4,128)S(1)}, f32[4,384]{1,0:T(4,128)S(1)}, u32[]{:S(2)}, u32[]{:S(2)}) collective-permute-start(f32[4,384]{1,0:T(4,128)S(1)} %get-tuple-element.28), channel_id=1, source_target_pairs={{1,0},{2,1},{3,2},{4,3},{5,4},{6,5},{7,6},{8,7},{9,8},{10,9},{11,1... | collective-permute-start | bytes 18440 | tf_op jit(solution)/shard_map/ppermute | solution.py:27
  20.7 11.2 %collective-permute-start.3 = (f32[4,128]{1,0:T(4,128)S(1)}, f32[4,128]{1,0:T(4,128)S(1)}, u32[]{:S(2)}, u32[]{:S(2)}) collective-permute-start(f32[4,128]{1,0:T(4,128)S(1)} %get-tuple-element.48), channel_id=1, source_target_pairs={{1,0},{2,1},{3,2},{4,3},{5,4},{6,5},{7,6},{8,7},{9,8},{10,9},{11,1... | collective-permute-start | bytes 6152 | tf_op jit(solution)/shard_map/ppermute | solution.py:27
  24.5 7.3 %collective-permute-start.1 = (f32[4,128]{1,0:T(4,128)S(1)}, f32[4,128]{1,0:T(4,128)S(1)}, u32[]{:S(2)}, u32[]{:S(2)}) collective-permute-start(f32[4,128]{1,0:T(4,128)S(1)} %get-tuple-element.47), channel_id=1, source_target_pairs={{0,1},{1,2},{2,3},{3,4},{4,5},{5,6},{6,7},{7,8},{8,9},{9,10},{10,1... | collective-permute-start | bytes 6152 | tf_op jit(solution)/shard_map/ppermute | solution.py:26
  26.7 1.7 %copy-start = (bf16[40,256,128]{2,1,0:T(8,128)(2,1)S(1)}, bf16[40,256,128]{2,1,0:T(8,128)(2,1)}, u32[]{:S(2)}) copy-start(bf16[40,256,128]{2,1,0:T(8,128)(2,1)} %param.18) | copy-start | bytes 7864324
  30.4 1.5 %copy-start.2 = (f32[128,128]{1,0:T(8,128)S(1)}, f32[128,128]{1,0:T(8,128)}, u32[]{:S(2)}) copy-start(f32[128,128]{1,0:T(8,128)} %param.14) | copy-start | bytes 196612
  30.4 1.5 %copy-start.3 = (f32[128,128]{1,0:T(8,128)S(1)}, f32[128,128]{1,0:T(8,128)}, u32[]{:S(2)}) copy-start(f32[128,128]{1,0:T(8,128)} %param.15) | copy-start | bytes 196612
  30.4 1.5 %copy-start.4 = (f32[128,128]{1,0:T(8,128)S(1)}, f32[128,128]{1,0:T(8,128)}, u32[]{:S(2)}) copy-start(f32[128,128]{1,0:T(8,128)} %param.16) | copy-start | bytes 196612
  31.8 1.3 %collective-permute-start.4 = (f32[70,70]{0,1:T(8,128)S(1)}, f32[70,70]{0,1:T(8,128)S(1)}, u32[]{:S(2)}, u32[]{:S(2)}) collective-permute-start(f32[70,70]{0,1:T(8,128)S(1)} %fusion), channel_id=1, source_target_pairs={{0,1},{1,0},{2,3},{3,2},{4,5},{5,4},{6,7},{7,6},{8,9},{9,8},{10,11... | collective-permute-start | bytes 58808 | tf_op jit(solution)/shard_map/ppermute | solution.py:19
  32.2 28.0 %copy-start.6 = (f32[256,128]{1,0:T(8,128)S(1)}, f32[256,128]{1,0:T(8,128)}, u32[]{:S(2)}) copy-start(f32[256,128]{1,0:T(8,128)} %param.13) | copy-start | bytes 393220
  33.1 4.0 %collective-permute-start.5 = (f32[70,70]{0,1:T(8,128)S(1)}, f32[70,70]{0,1:T(8,128)S(1)}, u32[]{:S(2)}, u32[]{:S(2)}) collective-permute-start(f32[70,70]{0,1:T(8,128)S(1)} %add.173), channel_id=1, source_target_pairs={{0,2},{1,3},{2,0},{3,1},{4,6},{5,7},{6,4},{7,5},{8,10},{9,11},{10,... | collective-permute-start | bytes 58808 | tf_op jit(solution)/shard_map/ppermute | solution.py:19
  37.0 4.0 %collective-permute-start.6 = (f32[70,70]{0,1:T(8,128)S(1)}, f32[70,70]{0,1:T(8,128)S(1)}, u32[]{:S(2)}, u32[]{:S(2)}) collective-permute-start(f32[70,70]{0,1:T(8,128)S(1)} %add.174), channel_id=1, source_target_pairs={{0,4},{1,5},{2,6},{3,7},{4,0},{5,1},{6,2},{7,3},{8,12},{9,13},{10,... | collective-permute-start | bytes 58808 | tf_op jit(solution)/shard_map/ppermute | solution.py:19
  37.7 25.6 %copy-start.5 = (f32[128,128]{1,0:T(8,128)}, f32[128,128]{1,0:T(8,128)S(1)}, u32[]{:S(2)}) copy-start(f32[128,128]{1,0:T(8,128)S(1)} %get-tuple-element.15) | copy-start | bytes 196612
  41.0 7.5 %collective-permute-start.7 = (f32[70,70]{0,1:T(8,128)S(1)}, f32[70,70]{0,1:T(8,128)S(1)}, u32[]{:S(2)}, u32[]{:S(2)}) collective-permute-start(f32[70,70]{0,1:T(8,128)S(1)} %add.175), channel_id=1, source_target_pairs={{0,8},{1,9},{2,10},{3,11},{4,12},{5,13},{6,14},{7,15},{8,0},{9,1},... | collective-permute-start | bytes 58808 | tf_op jit(solution)/shard_map/ppermute | solution.py:19
  43.7 16.5 %all-to-all-start.1 = ((f32[16,16,128]{2,1,0:T(8,128)}), f32[16,16,128]{2,1,0:T(8,128)S(1)}, u32[]{:S(2)}, u32[]{:S(2)}) async-start(f32[16,16,128]{2,1,0:T(8,128)} %bitcast.5), calls=%async_computation.1 | async-start | bytes 262144 | tf_op jit(solution)/shard_map/all_to_all | solution.py:133
  63.3 17.6 %copy-start.1 = (bf16[30,256,128]{2,1,0:T(8,128)(2,1)S(1)}, bf16[30,256,128]{2,1,0:T(8,128)(2,1)}, u32[]{:S(2)}) copy-start(bf16[30,256,128]{2,1,0:T(8,128)(2,1)} %param.21) | copy-start | bytes 5898244
  63.3 1.2 %collective-permute-start.8 = (f32[70]{0:T(128)S(1)}, f32[70]{0:T(128)S(1)}, u32[]{:S(2)}, u32[]{:S(2)}) collective-permute-start(f32[70]{0:T(128)S(1)} %pad_maximum_fusion), channel_id=1, source_target_pairs={{0,1},{1,0},{2,3},{3,2},{4,5},{5,4},{6,7},{7,6},{8,9},{9,8},{10,11... | collective-permute-start | bytes 848 | tf_op jit(solution)/shard_map/ppermute | solution.py:19
  64.6 3.6 %collective-permute-start.9 = (f32[70]{0:T(128)S(1)}, f32[70]{0:T(128)S(1)}, u32[]{:S(2)}, u32[]{:S(2)}) collective-permute-start(f32[70]{0:T(128)S(1)} %fusion.83), channel_id=1, source_target_pairs={{0,2},{1,3},{2,0},{3,1},{4,6},{5,7},{6,4},{7,5},{8,10},{9,11},{10,... | collective-permute-start | bytes 848 | tf_op jit(solution)/shard_map/ppermute | solution.py:19
  68.2 4.8 %collective-permute-start.10 = (f32[70]{0:T(128)S(1)}, f32[70]{0:T(128)S(1)}, u32[]{:S(2)}, u32[]{:S(2)}) collective-permute-start(f32[70]{0:T(128)S(1)} %add.179), channel_id=1, source_target_pairs={{0,4},{1,5},{2,6},{3,7},{4,0},{5,1},{6,2},{7,3},{8,12},{9,13},{10,... | collective-permute-start | bytes 848 | tf_op jit(solution)/shard_map/ppermute | solution.py:19
  73.1 4.5 %collective-permute-start.11 = (f32[70]{0:T(128)S(1)}, f32[70]{0:T(128)S(1)}, u32[]{:S(2)}, u32[]{:S(2)}) collective-permute-start(f32[70]{0:T(128)S(1)} %add.180), channel_id=1, source_target_pairs={{0,8},{1,9},{2,10},{3,11},{4,12},{5,13},{6,14},{7,15},{8,0},{9,1},... | collective-permute-start | bytes 848 | tf_op jit(solution)/shard_map/ppermute | solution.py:19

commit v7 on v6

--- a/solution.py
+++ b/solution.py
@@ -2,6 +2,7 @@
 import jax.numpy as jnp
 from jax import lax
 from jax.sharding import PartitionSpec as P
+
 
 SUBSTEPS = 4
 
@@ -51,7 +52,7 @@
     return jnp.dot(inverse.T, inner, precision=high)
 
 
-def local(
+def body(
     fluid_press,
     iterate,
     displace,
@@ -122,7 +123,7 @@
     speed = packed[:, lanes : 2 * lanes]
     stiff = packed[:, 2 * lanes : 3 * lanes]
     press = packed[:, 3 * lanes :]
-    for substep in range(SUBSTEPS):
+    for _ in range(SUBSTEPS):
         lapl = jnp.roll(field, 1, 0) + jnp.roll(field, -1, 0) + sides(field) - 4.0 * field
         speed = speed + step_dt * (stiff * lapl + press - damping * speed)
         field = field + step_dt * speed
@@ -167,7 +168,7 @@
         P(None, ("runs", "tile"), None),
     )
     return jax.shard_map(
-        local,
+        body,
         mesh=mesh,
         in_specs=placed,
         out_specs=(P(("runs", "tile"), None), P(("runs", "tile"), None), P(("runs", "tile"), None)),

time: 82.7 us -> 82.7 us (level)
  no operation moved by 1% of the time
where the time goes in v7:
time: 82.7 us; the launch traced here: 82.1 us
  starting transfers between devices  28.9 us (35%)
  other arithmetic  27.1 us (33%)
  waiting for transfers between devices  13.2 us (16%)
  local copies, waits for them, and re-layouts  7.14 us (9%)
  matrix products  4.79 us (6%)
  between operations  1.01 us (1%)
    ppermute x8, waiting for transfers between devices, tree_sum(): lax.ppermute(value, axis, [(i, i ^ stride) for i in range(count)])  11.3 us
    ppermute x8, starting transfers between devices, tree_sum(): lax.ppermute(value, axis, [(i, i ^ stride) for i in range(count)])  8.27 us
    ppermute x2, starting transfers between devices, halo_pair(): lax.ppermute(cells[:width], axis, [((i + 1) % count, i) for i in range(co...  7.86 us
    another operation x6, other arithmetic, inverse_factor(): factor = jnp.linalg.cholesky(matrix)  7.81 us
    all_to_all x1, starting transfers between devices, body(): got = lax.all_to_all(sent, 'tile', split_axis=0, concat_axis=0, tiled=True)  7.41 us
    another operation x4, other arithmetic, inverse_factor(): return lax.linalg.triangular_solve(factor, eye, left_side=True, lower=True)  6.68 us
    unnamed x19, local copies, waits for them, and re-layouts  5.38 us
    all_to_all x1, starting transfers between devices, body(): lax.all_to_all(outgoing, 'tile', split_axis=0, concat_axis=0, tiled=True)  4.87 us
  transfers between devices with their start and end apart: 14, of which 8 were waited for; matrix products, arithmetic and copies ran while one was open for 33% of the time, Pallas kernels for 0%

profile of v7, /device:TPU:0, one launch (start us, length us, event | category | flops | bytes accessed | tf_op | source)
XLA Modules:
  0.0 82.1 jit_solution(12504729941210386623)
XLA Ops:
  0.6 0.9 %fusion.4 = f32[128]{0:T(128)S(1)} fusion(s32[128]{0:T(128)} %bitcast.89), kind=kOutput, calls=%fused_computation.11 | convolution fusion | flops 548736 | bytes 1024 | tf_op jit(solution)/shard_map/dot_general | solution.py:78
  1.5 0.7 fusion.53
  2.4 1.6 %select_maximum_fusion = f32[16,17,128]{2,1,0:T(8,128)} fusion(f32[16,1,16]{2,1,0:T(1,128)S(1)} %reshape.96, f32[16,16,128]{2,1,0:T(8,128)} %bitcast.88), kind=kLoop, calls=%fused_computation.21 | loop fusion | flops 104448 | bytes 271360 | tf_op jit(solution)/shard_map/concatenate | solution.py:93
  4.0 7.4 %all-to-all-start = ((f32[16,17,128]{2,1,0:T(8,128)}), f32[16,17,128]{2,1,0:T(8,128)S(1)}, u32[]{:S(2)}, u32[]{:S(2)}) async-start(f32[16,17,128]{2,1,0:T(8,128)} %select_maximum_fusion), calls=%async_computation | async-start | bytes 393216 | tf_op jit(solution)/shard_map/all_to_all | solution.py:94
  11.4 0.8 %constant_dynamic-update-slice_fusion.2 = f32[128,384]{1,0:T(8,128)S(1)} fusion(f32[128,128]{1,0:T(8,128)} %param.14), kind=kLoop, calls=%fused_computation.89 | loop fusion | bytes 131072
  12.2 0.8 %constant_dynamic-update-slice_fusion.1 = f32[128,384]{1,0:T(8,128)S(1)} fusion(f32[128,384]{1,0:T(8,128)S(1)} %constant_dynamic-update-slice_fusion.2, f32[128,128]{1,0:T(8,128)} %param.15), kind=kLoop, calls=%fused_computation.88 | loop fusion | bytes 131072
  13.1 0.8 %constant_dynamic-update-slice_fusion = f32[128,384]{1,0:T(8,128)S(1)} fusion(f32[128,384]{1,0:T(8,128)S(1)} %constant_dynamic-update-slice_fusion.1, f32[128,128]{1,0:T(8,128)} %param.16), kind=kLoop, calls=%fused_computation.87 | loop fusion | bytes 131072 | tf_op jit(solution)/shard_map/concatenate | solution.py:88
  13.9 0.5 collective-permute-start
  14.4 4.0 %collective-permute-start.2 = (f32[4,384]{1,0:T(4,128)S(1)}, f32[4,384]{1,0:T(4,128)S(1)}, u32[]{:S(2)}, u32[]{:S(2)}) collective-permute-start(f32[4,384]{1,0:T(4,128)S(1)} %get-tuple-element.28), channel_id=1, source_target_pairs={{1,0},{2,1},{3,2},{4,3},{5,4},{6,5},{7,6},{8,7},{9,8},{10,9},{11,1... | collective-permute-start | bytes 18440 | tf_op jit(solution)/shard_map/ppermute | solution.py:28
  18.4 1.5 %collective-permute-done = f32[4,384]{1,0:T(4,128)S(1)} collective-permute-done((f32[4,384]{1,0:T(4,128)S(1)}, f32[4,384]{1,0:T(4,128)S(1)}, u32[]{:S(2)}, u32[]{:S(2)}) %collective-permute-start) | collective-permute-done | bytes 6176 | tf_op jit(solution)/shard_map/ppermute | solution.py:27
  19.9 0.5 all-to-all-done
  20.4 0.3 fusion.11
  20.7 3.8 %collective-permute-start.3 = (f32[4,128]{1,0:T(4,128)S(1)}, f32[4,128]{1,0:T(4,128)S(1)}, u32[]{:S(2)}, u32[]{:S(2)}) collective-permute-start(f32[4,128]{1,0:T(4,128)S(1)} %get-tuple-element.48), channel_id=1, source_target_pairs={{1,0},{2,1},{3,2},{4,3},{5,4},{6,5},{7,6},{8,7},{9,8},{10,9},{11,1... | collective-permute-start | bytes 6152 | tf_op jit(solution)/shard_map/ppermute | solution.py:28
  24.7 1.8 %broadcast_multiply_fusion.1 = bf16[30,256,128]{2,1,0:T(8,128)(2,1)S(1)} fusion(bf16[30,256,128]{2,1,0:T(8,128)(2,1)} %param.20, bf16[256]{0:T(256)(128)(2,1)S(1)} %convert_element_type.42), kind=kLoop, calls=%fused_computation.19 | loop fusion | flops 983040 | bytes 3932672 | tf_op jit(solution)/shard_map/mul | solution.py:102
  26.4 0.2 pad.44
  26.7 1.4 %copy.25 = bf16[4,8,256,128]{3,1,2,0:T(8,128)(2,1)S(1)} copy(bf16[4,8,256,128]{3,2,1,0:T(8,128)(2,1)S(1)} %bitcast.84) | data formatting | bytes 4194304
  28.0 0.4 copy-done
  28.4 0.2 broadcast_multiply_fusion
  28.7 1.7 %copy.27 = bf16[5,8,256,128]{3,1,2,0:T(8,128)(2,1)S(1)} copy(bf16[5,8,256,128]{3,2,1,0:T(8,128)(2,1)S(1)} %bitcast.83) | data formatting | bytes 5242880
  30.4 1.4 %fusion = f32[70,70]{0,1:T(8,128)S(1)} fusion(bf16[30,32768]{1,0:T(8,128)(2,1)S(1)} %bitcast.86, bf16[40,32768]{1,0:T(8,128)(2,1)S(1)} %bitcast.85), kind=kOutput, calls=%fused_computation.2 | convolution fusion | flops 330301440 | bytes 4607120 | tf_op jit(solution)/shard_map/dot_general | solution.py:106
  32.7 0.3 collective-permute-done.4
  33.2 3.8 %collective-permute-done.5 = f32[70,70]{0,1:T(8,128)S(1)} collective-permute-done((f32[70,70]{0,1:T(8,128)S(1)}, f32[70,70]{0,1:T(8,128)S(1)}, u32[]{:S(2)}, u32[]{:S(2)}) %collective-permute-start.5) | collective-permute-done | bytes 19632 | tf_op jit(solution)/shard_map/ppermute | solution.py:20
  37.0 0.6 slice_add_fusion
  37.7 3.3 %collective-permute-done.6 = f32[70,70]{0,1:T(8,128)S(1)} collective-permute-done((f32[70,70]{0,1:T(8,128)S(1)}, f32[70,70]{0,1:T(8,128)S(1)}, u32[]{:S(2)}, u32[]{:S(2)}) %collective-permute-start.6) | collective-permute-done | bytes 19632 | tf_op jit(solution)/shard_map/ppermute | solution.py:20
  41.0 1.6 %collective-permute-start.7 = (f32[70,70]{0,1:T(8,128)S(1)}, f32[70,70]{0,1:T(8,128)S(1)}, u32[]{:S(2)}, u32[]{:S(2)}) collective-permute-start(f32[70,70]{0,1:T(8,128)S(1)} %add.175), channel_id=1, source_target_pairs={{0,8},{1,9},{2,10},{3,11},{4,12},{5,13},{6,14},{7,15},{8,0},{9,1},... | collective-permute-start | bytes 58808 | tf_op jit(solution)/shard_map/ppermute | solution.py:20
  42.6 1.0 %fusion.10 = f32[256,128]{1,0:T(8,128)} fusion(f32[128,128]{1,0:T(8,128)S(1)} %get-tuple-element.15, s32[128]{0:T(128)S(1)} %fusion.53), kind=kOutput, calls=%fused_computation.30 | convolution fusion | flops 50364416 | bytes 197120 | tf_op jit(solution)/shard_map/dot_general | solution.py:133
  43.7 4.9 %all-to-all-start.1 = ((f32[16,16,128]{2,1,0:T(8,128)}), f32[16,16,128]{2,1,0:T(8,128)S(1)}, u32[]{:S(2)}, u32[]{:S(2)}) async-start(f32[16,16,128]{2,1,0:T(8,128)} %bitcast.5), calls=%async_computation.1 | async-start | bytes 262144 | tf_op jit(solution)/shard_map/all_to_all | solution.py:134
  48.8 3.7 %cholesky.31 = f32[40,40]{1,0:T(8,128)S(1)} custom-call(f32[40,40]{1,0:T(8,128)S(1)} %copy.21), custom_call_target="Cholesky" | custom-call | tf_op jit(solution)/shard_map/jit(cholesky)/cholesky | solution.py:44
  52.5 0.7 compare_reduce_fusion.1
  53.4 0.7 fusion.38
  54.1 3.1 %custom-call.12 = f32[1,40,40]{1,2,0:T(8,128)S(1)} custom-call(f32[1,40,40]{2,1,0:T(8,128)S(1)} %fusion.38), custom_call_target="InvertDiagBlocksLowerTriangular" | custom-call | tf_op jit(solution)/shard_map/triangular_solve | solution.py:46
  57.1 2.7 %cholesky.65 = f32[30,30]{1,0:T(8,128)S(1)} custom-call(f32[30,30]{1,0:T(8,128)S(1)} %fusion.48), custom_call_target="Cholesky" | custom-call | tf_op jit(solution)/shard_map/jit(cholesky)/cholesky | solution.py:44
  59.9 0.2 fusion.41
  60.2 2.2 %multiply_reduce_fusion.3 = f32[30]{0:T(128)S(1)} fusion(bf16[30,256,128]{2,1,0:T(8,128)(2,1)} %param.20, f32[256,128]{1,0:T(8,128)S(1)} %fusion.8), kind=kLoop, calls=%fused_computation.7 | loop fusion | flops 2949090 | bytes 2097272 | tf_op jit(solution)/shard_map/reduce_sum | solution.py:139
  62.4 0.8 %multiply_reduce_fusion.1 = f32[40]{0:T(128)S(1)} fusion(bf16[40,256,128]{2,1,0:T(8,128)(2,1)S(1)} %copy-done, f32[256,128]{1,0:T(8,128)S(1)} %fusion.8), kind=kLoop, calls=%fused_computation.1 | loop fusion | flops 3932120 | bytes 2752672 | tf_op jit(solution)/shard_map/reduce_sum | solution.py:138
  63.3 0.4 collective-permute-start.8
  63.8 0.8 collective-permute-done.8
  64.6 1.9 %collective-permute-start.9 = (f32[70]{0:T(128)S(1)}, f32[70]{0:T(128)S(1)}, u32[]{:S(2)}, u32[]{:S(2)}) collective-permute-start(f32[70]{0:T(128)S(1)} %fusion.83), channel_id=1, source_target_pairs={{0,2},{1,3},{2,0},{3,1},{4,6},{5,7},{6,4},{7,5},{8,10},{9,11},{10,... | collective-permute-start | bytes 848 | tf_op jit(solution)/shard_map/ppermute | solution.py:20
  66.5 0.6 compare_reduce_fusion
  67.1 1.1 %collective-permute-done.9 = f32[70]{0:T(128)S(1)} collective-permute-done((f32[70]{0:T(128)S(1)}, f32[70]{0:T(128)S(1)}, u32[]{:S(2)}, u32[]{:S(2)}) %collective-permute-start.9) | collective-permute-done | bytes 312 | tf_op jit(solution)/shard_map/ppermute | solution.py:20
  68.2 1.9 %collective-permute-start.10 = (f32[70]{0:T(128)S(1)}, f32[70]{0:T(128)S(1)}, u32[]{:S(2)}, u32[]{:S(2)}) collective-permute-start(f32[70]{0:T(128)S(1)} %add.179), channel_id=1, source_target_pairs={{0,4},{1,5},{2,6},{3,7},{4,0},{5,1},{6,2},{7,3},{8,12},{9,13},{10,... | collective-permute-start | bytes 848 | tf_op jit(solution)/shard_map/ppermute | solution.py:20
  70.1 0.7 fusion.44
  70.7 2.3 %custom-call.13 = f32[1,30,30]{1,2,0:T(8,128)S(1)} custom-call(f32[1,30,30]{2,1,0:T(8,128)S(1)} %fusion.44), custom_call_target="InvertDiagBlocksLowerTriangular" | custom-call | tf_op jit(solution)/shard_map/triangular_solve | solution.py:46
  73.1 2.4 %collective-permute-start.11 = (f32[70]{0:T(128)S(1)}, f32[70]{0:T(128)S(1)}, u32[]{:S(2)}, u32[]{:S(2)}) collective-permute-start(f32[70]{0:T(128)S(1)} %add.180), channel_id=1, source_target_pairs={{0,8},{1,9},{2,10},{3,11},{4,12},{5,13},{6,14},{7,15},{8,0},{9,1},... | collective-permute-start | bytes 848 | tf_op jit(solution)/shard_map/ppermute | solution.py:20
  75.7 1.9 %collective-permute-done.11 = f32[70]{0:T(128)S(1)} collective-permute-done((f32[70]{0:T(128)S(1)}, f32[70]{0:T(128)S(1)}, u32[]{:S(2)}, u32[]{:S(2)}) %collective-permute-start.11) | collective-permute-done | bytes 312 | tf_op jit(solution)/shard_map/ppermute | solution.py:20
  78.5 2.4 %multiply_reduce_fusion = f32[256,128]{1,0:T(8,128)S(1)} fusion(bf16[40,256,128]{2,1,0:T(8,128)(2,1)} %param.19, f32[40]{0:T(128)S(1)} %get-tuple-element.49), kind=kLoop, calls=%fused_computation | loop fusion | flops 3899392 | bytes 2752672 | tf_op jit(solution)/shard_map/reduce_sum | solution.py:150
  80.8 0.5 multiply_reduce_fusion.2
  81.4 0.8 fusion.9
  (74 shorter events, 3.1 us)
Async XLA Ops:
  4.0 16.4 %all-to-all-start = ((f32[16,17,128]{2,1,0:T(8,128)}), f32[16,17,128]{2,1,0:T(8,128)S(1)}, u32[]{:S(2)}, u32[]{:S(2)}) async-start(f32[16,17,128]{2,1,0:T(8,128)} %select_maximum_fusion), calls=%async_computation | async-start | bytes 393216 | tf_op jit(solution)/shard_map/all_to_all | solution.py:94
  13.9 6.0 %collective-permute-start = (f32[4,384]{1,0:T(4,128)S(1)}, f32[4,384]{1,0:T(4,128)S(1)}, u32[]{:S(2)}, u32[]{:S(2)}) collective-permute-start(f32[4,384]{1,0:T(4,128)S(1)} %get-tuple-element.27), channel_id=1, source_target_pairs={{0,1},{1,2},{2,3},{3,4},{4,5},{5,6},{6,7},{7,8},{8,9},{9,10},{10,1... | collective-permute-start | bytes 18440 | tf_op jit(solution)/shard_map/ppermute | solution.py:27
  14.4 5.5 %collective-permute-start.2 = (f32[4,384]{1,0:T(4,128)S(1)}, f32[4,384]{1,0:T(4,128)S(1)}, u32[]{:S(2)}, u32[]{:S(2)}) collective-permute-start(f32[4,384]{1,0:T(4,128)S(1)} %get-tuple-element.28), channel_id=1, source_target_pairs={{1,0},{2,1},{3,2},{4,3},{5,4},{6,5},{7,6},{8,7},{9,8},{10,9},{11,1... | collective-permute-start | bytes 18440 | tf_op jit(solution)/shard_map/ppermute | solution.py:28
  20.7 11.2 %collective-permute-start.3 = (f32[4,128]{1,0:T(4,128)S(1)}, f32[4,128]{1,0:T(4,128)S(1)}, u32[]{:S(2)}, u32[]{:S(2)}) collective-permute-start(f32[4,128]{1,0:T(4,128)S(1)} %get-tuple-element.48), channel_id=1, source_target_pairs={{1,0},{2,1},{3,2},{4,3},{5,4},{6,5},{7,6},{8,7},{9,8},{10,9},{11,1... | collective-permute-start | bytes 6152 | tf_op jit(solution)/shard_map/ppermute | solution.py:28
  24.5 7.3 %collective-permute-start.1 = (f32[4,128]{1,0:T(4,128)S(1)}, f32[4,128]{1,0:T(4,128)S(1)}, u32[]{:S(2)}, u32[]{:S(2)}) collective-permute-start(f32[4,128]{1,0:T(4,128)S(1)} %get-tuple-element.47), channel_id=1, source_target_pairs={{0,1},{1,2},{2,3},{3,4},{4,5},{5,6},{6,7},{7,8},{8,9},{9,10},{10,1... | collective-permute-start | bytes 6152 | tf_op jit(solution)/shard_map/ppermute | solution.py:27
  26.7 1.7 %copy-start = (bf16[40,256,128]{2,1,0:T(8,128)(2,1)S(1)}, bf16[40,256,128]{2,1,0:T(8,128)(2,1)}, u32[]{:S(2)}) copy-start(bf16[40,256,128]{2,1,0:T(8,128)(2,1)} %param.18) | copy-start | bytes 7864324
  30.4 1.5 %copy-start.2 = (f32[128,128]{1,0:T(8,128)S(1)}, f32[128,128]{1,0:T(8,128)}, u32[]{:S(2)}) copy-start(f32[128,128]{1,0:T(8,128)} %param.14) | copy-start | bytes 196612
  30.4 1.5 %copy-start.3 = (f32[128,128]{1,0:T(8,128)S(1)}, f32[128,128]{1,0:T(8,128)}, u32[]{:S(2)}) copy-start(f32[128,128]{1,0:T(8,128)} %param.15) | copy-start | bytes 196612
  30.4 1.5 %copy-start.4 = (f32[128,128]{1,0:T(8,128)S(1)}, f32[128,128]{1,0:T(8,128)}, u32[]{:S(2)}) copy-start(f32[128,128]{1,0:T(8,128)} %param.16) | copy-start | bytes 196612
  31.8 1.3 %collective-permute-start.4 = (f32[70,70]{0,1:T(8,128)S(1)}, f32[70,70]{0,1:T(8,128)S(1)}, u32[]{:S(2)}, u32[]{:S(2)}) collective-permute-start(f32[70,70]{0,1:T(8,128)S(1)} %fusion), channel_id=1, source_target_pairs={{0,1},{1,0},{2,3},{3,2},{4,5},{5,4},{6,7},{7,6},{8,9},{9,8},{10,11... | collective-permute-start | bytes 58808 | tf_op jit(solution)/shard_map/ppermute | solution.py:20
  32.2 28.0 %copy-start.6 = (f32[256,128]{1,0:T(8,128)S(1)}, f32[256,128]{1,0:T(8,128)}, u32[]{:S(2)}) copy-start(f32[256,128]{1,0:T(8,128)} %param.13) | copy-start | bytes 393220
  33.1 4.0 %collective-permute-start.5 = (f32[70,70]{0,1:T(8,128)S(1)}, f32[70,70]{0,1:T(8,128)S(1)}, u32[]{:S(2)}, u32[]{:S(2)}) collective-permute-start(f32[70,70]{0,1:T(8,128)S(1)} %add.173), channel_id=1, source_target_pairs={{0,2},{1,3},{2,0},{3,1},{4,6},{5,7},{6,4},{7,5},{8,10},{9,11},{10,... | collective-permute-start | bytes 58808 | tf_op jit(solution)/shard_map/ppermute | solution.py:20
  37.0 4.0 %collective-permute-start.6 = (f32[70,70]{0,1:T(8,128)S(1)}, f32[70,70]{0,1:T(8,128)S(1)}, u32[]{:S(2)}, u32[]{:S(2)}) collective-permute-start(f32[70,70]{0,1:T(8,128)S(1)} %add.174), channel_id=1, source_target_pairs={{0,4},{1,5},{2,6},{3,7},{4,0},{5,1},{6,2},{7,3},{8,12},{9,13},{10,... | collective-permute-start | bytes 58808 | tf_op jit(solution)/shard_map/ppermute | solution.py:20
  37.7 25.6 %copy-start.5 = (f32[128,128]{1,0:T(8,128)}, f32[128,128]{1,0:T(8,128)S(1)}, u32[]{:S(2)}) copy-start(f32[128,128]{1,0:T(8,128)S(1)} %get-tuple-element.15) | copy-start | bytes 196612
  41.0 7.5 %collective-permute-start.7 = (f32[70,70]{0,1:T(8,128)S(1)}, f32[70,70]{0,1:T(8,128)S(1)}, u32[]{:S(2)}, u32[]{:S(2)}) collective-permute-start(f32[70,70]{0,1:T(8,128)S(1)} %add.175), channel_id=1, source_target_pairs={{0,8},{1,9},{2,10},{3,11},{4,12},{5,13},{6,14},{7,15},{8,0},{9,1},... | collective-permute-start | bytes 58808 | tf_op jit(solution)/shard_map/ppermute | solution.py:20
  43.7 16.5 %all-to-all-start.1 = ((f32[16,16,128]{2,1,0:T(8,128)}), f32[16,16,128]{2,1,0:T(8,128)S(1)}, u32[]{:S(2)}, u32[]{:S(2)}) async-start(f32[16,16,128]{2,1,0:T(8,128)} %bitcast.5), calls=%async_computation.1 | async-start | bytes 262144 | tf_op jit(solution)/shard_map/all_to_all | solution.py:134
  63.3 17.6 %copy-start.1 = (bf16[30,256,128]{2,1,0:T(8,128)(2,1)S(1)}, bf16[30,256,128]{2,1,0:T(8,128)(2,1)}, u32[]{:S(2)}) copy-start(bf16[30,256,128]{2,1,0:T(8,128)(2,1)} %param.21) | copy-start | bytes 5898244
  63.3 1.2 %collective-permute-start.8 = (f32[70]{0:T(128)S(1)}, f32[70]{0:T(128)S(1)}, u32[]{:S(2)}, u32[]{:S(2)}) collective-permute-start(f32[70]{0:T(128)S(1)} %pad_maximum_fusion), channel_id=1, source_target_pairs={{0,1},{1,0},{2,3},{3,2},{4,5},{5,4},{6,7},{7,6},{8,9},{9,8},{10,11... | collective-permute-start | bytes 848 | tf_op jit(solution)/shard_map/ppermute | solution.py:20
  64.6 3.6 %collective-permute-start.9 = (f32[70]{0:T(128)S(1)}, f32[70]{0:T(128)S(1)}, u32[]{:S(2)}, u32[]{:S(2)}) collective-permute-start(f32[70]{0:T(128)S(1)} %fusion.83), channel_id=1, source_target_pairs={{0,2},{1,3},{2,0},{3,1},{4,6},{5,7},{6,4},{7,5},{8,10},{9,11},{10,... | collective-permute-start | bytes 848 | tf_op jit(solution)/shard_map/ppermute | solution.py:20
  68.2 4.8 %collective-permute-start.10 = (f32[70]{0:T(128)S(1)}, f32[70]{0:T(128)S(1)}, u32[]{:S(2)}, u32[]{:S(2)}) collective-permute-start(f32[70]{0:T(128)S(1)} %add.179), channel_id=1, source_target_pairs={{0,4},{1,5},{2,6},{3,7},{4,0},{5,1},{6,2},{7,3},{8,12},{9,13},{10,... | collective-permute-start | bytes 848 | tf_op jit(solution)/shard_map/ppermute | solution.py:20
  73.1 4.5 %collective-permute-start.11 = (f32[70]{0:T(128)S(1)}, f32[70]{0:T(128)S(1)}, u32[]{:S(2)}, u32[]{:S(2)}) collective-permute-start(f32[70]{0:T(128)S(1)} %add.180), channel_id=1, source_target_pairs={{0,8},{1,9},{2,10},{3,11},{4,12},{5,13},{6,14},{7,15},{8,0},{9,1},... | collective-permute-start | bytes 848 | tf_op jit(solution)/shard_map/ppermute | solution.py:20

commit v8 on v7

--- a/solution.py
+++ b/solution.py
@@ -1,6 +1,7 @@
 import jax
 import jax.numpy as jnp
 from jax import lax
+from jax.experimental import pallas as pl
 from jax.sharding import PartitionSpec as P
 
 
@@ -40,10 +41,33 @@
     return left + right
 
 
-def inverse_factor(matrix):
-    factor = jnp.linalg.cholesky(matrix)
-    eye = jnp.eye(matrix.shape[0], dtype=matrix.dtype)
-    return lax.linalg.triangular_solve(factor, eye, left_side=True, lower=True)
+def eliminate(a):
+    n = a.shape[0]
+    rows = lax.broadcasted_iota(jnp.int32, (n, n), 0)
+    cols = lax.broadcasted_iota(jnp.int32, (n, n), 1)
+    m = jnp.where(rows == cols, 1.0, 0.0).astype(jnp.float32)
+    for j in range(n):
+        on_row = rows == j
+        row = jnp.sum(jnp.where(on_row, a, 0.0), axis=0, keepdims=True)
+        col = jnp.sum(jnp.where(cols == j, a, 0.0), axis=1, keepdims=True)
+        pivot = jnp.sum(jnp.where(cols[:1] == j, row, 0.0), axis=1, keepdims=True)
+        scale = 1.0 / jnp.sqrt(pivot)
+        row = jnp.where(cols[:1] >= j, row * scale, 0.0)
+        lower = jnp.where(rows[:, :1] > j, col * scale, 0.0)
+        m_row = jnp.sum(jnp.where(on_row, m, 0.0), axis=0, keepdims=True) * scale
+        a = jnp.where(on_row, row, a - lower * row)
+        m = jnp.where(on_row, m_row, m - lower * m_row)
+    return m
+
+
+def factor_kernel(cur_ref, past_ref, inv_cur_ref, inv_past_ref):
+    inv_cur_ref[...] = eliminate(cur_ref[...])
+    inv_past_ref[...] = eliminate(past_ref[...])
+
+
+def inverse_factors(cur, past):
+    shapes = (jax.ShapeDtypeStruct(cur.shape, jnp.float32), jax.ShapeDtypeStruct(past.shape, jnp.float32))
+    return pl.pallas_call(factor_kernel, out_shape=shapes)(cur, past)
 
 
 def solve_spd(inverse, vector):
@@ -106,8 +130,7 @@
     gram = lax.dot_general(cols, cols, (((1,), (1,)), ((), ())), preferred_element_type=jnp.float32)
     gram = tree_sum(gram, "tile")
     cross = gram[n_cur:, :n_cur]
-    inv_cur = inverse_factor(gram[:n_cur, :n_cur])
-    inv_past = inverse_factor(gram[n_cur:, n_cur:])
+    inv_cur, inv_past = inverse_factors(gram[:n_cur, :n_cur], gram[n_cur:, n_cur:])
 
     pressure = jnp.dot(chooser, returned, precision=high)
     press_below, press_above = halo_pair(pressure, width, "tile")

time: 82.7 us -> 80.5 us (0.973)
  other arithmetic: 27.1 us -> 12.8 us
  Pallas kernels: 0 us -> 5.88 us
  matrix products: 4.79 us -> 9.46 us
  waiting for transfers between devices: 13.2 us -> 9.99 us
  starting transfers between devices: 28.9 us -> 31.3 us
  local copies, waits for them, and re-layouts: 7.14 us -> 9.3 us
    another operation x10 -> x0, other arithmetic: 14.5 us -> none  [the longest x6 7.81 us: inverse_factor(): factor = jnp.linalg.cholesky(matrix)]
    pallas_call x0 -> x1, Pallas kernels: none -> 5.88 us  [inverse_factors(): return pl.pallas_call(factor_kernel, out_shape=shapes)(cur, past)]
    ppermute x8, waiting for transfers between devices: 11.3 us -> 8.01 us  [tree_sum(): lax.ppermute(value, axis, [(i, i ^ stride) for i in range(count)])]
    dot_general x1, matrix products: 1.38 us -> 3.64 us  [body(): lax.dot_general(cols, cols, (((1,), (1,)), ((), ())), preferred_element_t...]
    mul x1, other arithmetic: 0.25 us -> 2.13 us  [body(): diff_cur * mask_half[None, :, None]]
    mul x1, other arithmetic: 1.76 us -> 0.21 us  [body(): diff_past * mask_half[None, :, None]]
    ppermute x8, starting transfers between devices: 8.27 us -> 9.78 us  [tree_sum(): lax.ppermute(value, axis, [(i, i ^ stride) for i in range(count)])]
    dot_general x2, matrix products: 0.34 us -> 1.79 us  [solve_spd(): inner = jnp.dot(inverse, vector, precision=high)]
  transfers between devices with their start and end apart: 14 -> 14, of which waited for: 8 -> 6; matrix products, arithmetic and copies ran while one was open for 33% -> 22% of each run, Pallas kernels for 0% -> 7%
where the time goes in v8:
time: 80.5 us; the launch traced here: 79.7 us
  starting transfers between devices  31.3 us (39%)
  other arithmetic  12.8 us (16%)
  waiting for transfers between devices  9.99 us (12%)
  matrix products  9.46 us (12%)
  local copies, waits for them, and re-layouts  9.3 us (12%)
  Pallas kernels  5.88 us (7%)
  between operations  0.93 us (1%)
    ppermute x8, starting transfers between devices, tree_sum(): lax.ppermute(value, axis, [(i, i ^ stride) for i in range(count)])  9.78 us
    ppermute x8, waiting for transfers between devices, tree_sum(): lax.ppermute(value, axis, [(i, i ^ stride) for i in range(count)])  8.01 us
    ppermute x2, starting transfers between devices, halo_pair(): lax.ppermute(cells[:width], axis, [((i + 1) % count, i) for i in range(co...  7.86 us
    all_to_all x1, starting transfers between devices, body(): got = lax.all_to_all(sent, 'tile', split_axis=0, concat_axis=0, tiled=True)  7.41 us
    unnamed x21, local copies, waits for them, and re-layouts  6.57 us
    pallas_call x1, Pallas kernels, inverse_factors(): return pl.pallas_call(factor_kernel, out_shape=shapes)(cur, past)  5.88 us
    all_to_all x1, starting transfers between devices, body(): lax.all_to_all(outgoing, 'tile', split_axis=0, concat_axis=0, tiled=True)  5.83 us
    dot_general x1, matrix products, body(): lax.dot_general(cols, cols, (((1,), (1,)), ((), ())), preferred_element_t...  3.64 us
  transfers between devices with their start and end apart: 14, of which 6 were waited for; matrix products, arithmetic and copies ran while one was open for 22% of the time, Pallas kernels for 7%

profile of v8, /device:TPU:0, one launch (start us, length us, event | category | flops | bytes accessed | tf_op | source)
XLA Modules:
  0.0 79.7 jit_solution(18024569954153590941)
XLA Ops:
  0.6 0.9 %fusion.4 = f32[128]{0:T(128)S(1)} fusion(s32[128]{0:T(128)} %bitcast.71), kind=kOutput, calls=%fused_computation.11 | convolution fusion | flops 548736 | bytes 1024 | tf_op jit(solution)/shard_map/dot_general | solution.py:102
  1.5 0.7 fusion.45
  2.4 1.6 %select_maximum_fusion = f32[16,17,128]{2,1,0:T(8,128)} fusion(f32[16,1,16]{2,1,0:T(1,128)S(1)} %reshape.79, f32[16,16,128]{2,1,0:T(8,128)} %bitcast.70), kind=kLoop, calls=%fused_computation.21 | loop fusion | flops 104448 | bytes 271360 | tf_op jit(solution)/shard_map/concatenate | solution.py:117
  4.0 7.4 %all-to-all-start = ((f32[16,17,128]{2,1,0:T(8,128)}), f32[16,17,128]{2,1,0:T(8,128)S(1)}, u32[]{:S(2)}, u32[]{:S(2)}) async-start(f32[16,17,128]{2,1,0:T(8,128)} %select_maximum_fusion), calls=%async_computation | async-start | bytes 393216 | tf_op jit(solution)/shard_map/all_to_all | solution.py:118
  11.4 0.8 %constant_dynamic-update-slice_fusion.2 = f32[128,384]{1,0:T(8,128)S(1)} fusion(f32[128,128]{1,0:T(8,128)} %param.14), kind=kLoop, calls=%fused_computation.71 | loop fusion | bytes 131072
  12.3 0.8 %constant_dynamic-update-slice_fusion.1 = f32[128,384]{1,0:T(8,128)S(1)} fusion(f32[128,384]{1,0:T(8,128)S(1)} %constant_dynamic-update-slice_fusion.2, f32[128,128]{1,0:T(8,128)} %param.15), kind=kLoop, calls=%fused_computation.70 | loop fusion | bytes 131072
  13.1 0.8 %constant_dynamic-update-slice_fusion = f32[128,384]{1,0:T(8,128)S(1)} fusion(f32[128,384]{1,0:T(8,128)S(1)} %constant_dynamic-update-slice_fusion.1, f32[128,128]{1,0:T(8,128)} %param.16), kind=kLoop, calls=%fused_computation.69 | loop fusion | bytes 131072 | tf_op jit(solution)/shard_map/concatenate | solution.py:112
  13.9 0.5 collective-permute-start
  14.4 4.0 %collective-permute-start.2 = (f32[4,384]{1,0:T(4,128)S(1)}, f32[4,384]{1,0:T(4,128)S(1)}, u32[]{:S(2)}, u32[]{:S(2)}) collective-permute-start(f32[4,384]{1,0:T(4,128)S(1)} %get-tuple-element.32), channel_id=1, source_target_pairs={{1,0},{2,1},{3,2},{4,3},{5,4},{6,5},{7,6},{8,7},{9,8},{10,9},{11,1... | collective-permute-start | bytes 18440 | tf_op jit(solution)/shard_map/ppermute | solution.py:29
  18.4 1.5 %collective-permute-done = f32[4,384]{1,0:T(4,128)S(1)} collective-permute-done((f32[4,384]{1,0:T(4,128)S(1)}, f32[4,384]{1,0:T(4,128)S(1)}, u32[]{:S(2)}, u32[]{:S(2)}) %collective-permute-start) | collective-permute-done | bytes 6176 | tf_op jit(solution)/shard_map/ppermute | solution.py:28
  19.9 0.5 all-to-all-done
  20.4 0.3 fusion.11
  20.7 3.8 %collective-permute-start.3 = (f32[4,128]{1,0:T(4,128)S(1)}, f32[4,128]{1,0:T(4,128)S(1)}, u32[]{:S(2)}, u32[]{:S(2)}) collective-permute-start(f32[4,128]{1,0:T(4,128)S(1)} %get-tuple-element.52), channel_id=1, source_target_pairs={{1,0},{2,1},{3,2},{4,3},{5,4},{6,5},{7,6},{8,7},{9,8},{10,9},{11,1... | collective-permute-start | bytes 6152 | tf_op jit(solution)/shard_map/ppermute | solution.py:29
  24.7 2.1 %broadcast_multiply_fusion = bf16[40,256,128]{2,1,0:T(8,128)(2,1)S(1)} fusion(bf16[40,256,128]{2,1,0:T(8,128)(2,1)} %param.18, bf16[256]{0:T(256)(128)(2,1)S(1)} %convert_element_type.40), kind=kLoop, calls=%fused_computation.9 | loop fusion | flops 1310720 | bytes 5243392 | tf_op jit(solution)/shard_map/mul | solution.py:125
  26.8 0.2 copy-done.1
  27.0 0.2 broadcast_multiply_fusion.1
  27.2 0.3 pad.44
  27.5 2.7 %copy.14 = bf16[4,8,256,128]{3,1,2,0:T(8,128)(2,1)} copy(bf16[4,8,256,128]{3,2,1,0:T(8,128)(2,1)S(1)} %bitcast.66) | data formatting | bytes 4194304
  30.2 1.7 %copy.16 = bf16[5,8,256,128]{3,1,2,0:T(8,128)(2,1)S(1)} copy(bf16[5,8,256,128]{3,2,1,0:T(8,128)(2,1)S(1)} %bitcast.65) | data formatting | bytes 5242880
  32.5 0.1 fusion.50
  32.9 0.6 slice_add_fusion
  33.5 1.0 %fusion.10 = f32[256,128]{1,0:T(8,128)} fusion(f32[128,128]{1,0:T(8,128)S(1)} %get-tuple-element.19, s32[128]{0:T(128)S(1)} %fusion.45), kind=kOutput, calls=%fused_computation.30 | convolution fusion | flops 50364416 | bytes 197120 | tf_op jit(solution)/shard_map/dot_general | solution.py:156
  34.5 5.8 %all-to-all-start.1 = ((f32[16,16,128]{2,1,0:T(8,128)}), f32[16,16,128]{2,1,0:T(8,128)S(1)}, u32[]{:S(2)}, u32[]{:S(2)}) async-start(f32[16,16,128]{2,1,0:T(8,128)} %bitcast.5), calls=%async_computation.1 | async-start | bytes 262144 | tf_op jit(solution)/shard_map/all_to_all | solution.py:157
  40.4 3.6 %fusion = f32[70,70]{1,0:T(8,128)S(1)} fusion(bf16[30,32768]{1,0:T(8,128)(2,1)} %bitcast.68, bf16[40,32768]{1,0:T(8,128)(2,1)S(1)} %bitcast.67), kind=kOutput, calls=%fused_computation.2 | convolution fusion | flops 330301440 | bytes 4607120 | tf_op jit(solution)/shard_map/dot_general | solution.py:130
  44.1 0.5 collective-permute-start.4
  44.5 0.9 %collective-permute-done.4 = f32[70,70]{1,0:T(8,128)S(1)} collective-permute-done((f32[70,70]{1,0:T(8,128)S(1)}, f32[70,70]{1,0:T(8,128)S(1)}, u32[]{:S(2)}, u32[]{:S(2)}) %collective-permute-start.4) | collective-permute-done | bytes 19632 | tf_op jit(solution)/shard_map/ppermute | solution.py:21
  45.4 1.9 %collective-permute-start.5 = (f32[70,70]{1,0:T(8,128)S(1)}, f32[70,70]{1,0:T(8,128)S(1)}, u32[]{:S(2)}, u32[]{:S(2)}) collective-permute-start(f32[70,70]{1,0:T(8,128)S(1)} %add.151), channel_id=1, source_target_pairs={{0,2},{1,3},{2,0},{3,1},{4,6},{5,7},{6,4},{7,5},{8,10},{9,11},{10,... | collective-permute-start | bytes 58808 | tf_op jit(solution)/shard_map/ppermute | solution.py:21
  47.3 2.1 %collective-permute-done.5 = f32[70,70]{1,0:T(8,128)S(1)} collective-permute-done((f32[70,70]{1,0:T(8,128)S(1)}, f32[70,70]{1,0:T(8,128)S(1)}, u32[]{:S(2)}, u32[]{:S(2)}) %collective-permute-start.5) | collective-permute-done | bytes 19632 | tf_op jit(solution)/shard_map/ppermute | solution.py:21
  49.4 1.9 %collective-permute-start.6 = (f32[70,70]{1,0:T(8,128)S(1)}, f32[70,70]{1,0:T(8,128)S(1)}, u32[]{:S(2)}, u32[]{:S(2)}) collective-permute-start(f32[70,70]{1,0:T(8,128)S(1)} %add.152), channel_id=1, source_target_pairs={{0,4},{1,5},{2,6},{3,7},{4,0},{5,1},{6,2},{7,3},{8,12},{9,13},{10,... | collective-permute-start | bytes 58808 | tf_op jit(solution)/shard_map/ppermute | solution.py:21
  51.3 2.2 %multiply_reduce_fusion.3 = f32[30]{0:T(128)S(1)} fusion(bf16[30,256,128]{2,1,0:T(8,128)(2,1)} %param.20, f32[256,128]{1,0:T(8,128)S(1)} %fusion.8), kind=kLoop, calls=%fused_computation.7 | loop fusion | flops 2949090 | bytes 2097272 | tf_op jit(solution)/shard_map/reduce_sum | solution.py:162
  53.5 0.8 %multiply_reduce_fusion.1 = f32[40]{0:T(128)S(1)} fusion(bf16[40,256,128]{2,1,0:T(8,128)(2,1)S(1)} %copy-done, f32[256,128]{1,0:T(8,128)S(1)} %fusion.8), kind=kLoop, calls=%fused_computation.1 | loop fusion | flops 3932120 | bytes 2752672 | tf_op jit(solution)/shard_map/reduce_sum | solution.py:161
  54.5 2.4 %collective-permute-start.7 = (f32[70,70]{1,0:T(8,128)S(1)}, f32[70,70]{1,0:T(8,128)S(1)}, u32[]{:S(2)}, u32[]{:S(2)}) collective-permute-start(f32[70,70]{1,0:T(8,128)S(1)} %add.153), channel_id=1, source_target_pairs={{0,8},{1,9},{2,10},{3,11},{4,12},{5,13},{6,14},{7,15},{8,0},{9,1},... | collective-permute-start | bytes 58808 | tf_op jit(solution)/shard_map/ppermute | solution.py:21
  57.0 1.5 %collective-permute-start.9 = (f32[70]{0:T(128)S(1)}, f32[70]{0:T(128)S(1)}, u32[]{:S(2)}, u32[]{:S(2)}) collective-permute-start(f32[70]{0:T(128)S(1)} %fusion.75), channel_id=1, source_target_pairs={{0,2},{1,3},{2,0},{3,1},{4,6},{5,7},{6,4},{7,5},{8,10},{9,11},{10,... | collective-permute-start | bytes 848 | tf_op jit(solution)/shard_map/ppermute | solution.py:21
  58.5 2.1 %collective-permute-done.9 = f32[70]{0:T(128)S(1)} collective-permute-done((f32[70]{0:T(128)S(1)}, f32[70]{0:T(128)S(1)}, u32[]{:S(2)}, u32[]{:S(2)}) %collective-permute-start.9) | collective-permute-done | bytes 312 | tf_op jit(solution)/shard_map/ppermute | solution.py:21
  60.6 0.6 collective-permute-start.10
  61.2 2.9 %collective-permute-done.10 = f32[70]{0:T(128)S(1)} collective-permute-done((f32[70]{0:T(128)S(1)}, f32[70]{0:T(128)S(1)}, u32[]{:S(2)}, u32[]{:S(2)}) %collective-permute-start.10) | collective-permute-done | bytes 312 | tf_op jit(solution)/shard_map/ppermute | solution.py:21
  64.1 1.1 %collective-permute-start.11 = (f32[70]{0:T(128)S(1)}, f32[70]{0:T(128)S(1)}, u32[]{:S(2)}, u32[]{:S(2)}) collective-permute-start(f32[70]{0:T(128)S(1)} %add.157), channel_id=1, source_target_pairs={{0,8},{1,9},{2,10},{3,11},{4,12},{5,13},{6,14},{7,15},{8,0},{9,1},... | collective-permute-start | bytes 848 | tf_op jit(solution)/shard_map/ppermute | solution.py:21
  65.2 0.6 slice.237.cur_ref
  65.8 0.7 slice.238.past_ref
  66.5 5.9 %shard_map.121 = (f32[40,40]{1,0:T(8,128)}, f32[30,30]{1,0:T(8,128)}) custom-call(f32[40,40]{1,0:T(8,128)} %slice.237.cur_ref, f32[30,30]{1,0:T(8,128)} %slice.238.past_ref), custom_call_target="tpu_custom_call" | custom-call | tf_op jit(solution)/shard_map/pallas_call | solution.py:70
  72.4 0.9 %convolution_bitcast_fusion.4 = f32[40,1]{0,1:T(1,128)S(1)} fusion(f32[40,40]{1,0:T(8,128)} %get-tuple-element.17, f32[70]{0:T(128)S(1)} %add.158), kind=kOutput, calls=%fused_computation.16 | convolution fusion | flops 19200 | bytes 6840 | tf_op jit(solution)/shard_map/dot_general | solution.py:75
  73.2 0.9 %fusion.68 = (f32[40]{0:T(128)S(1)}, f32[40]{0:T(128)S(1)}) fusion(f32[40,1]{0,1:T(1,128)S(1)} %convolution_bitcast_fusion.4, f32[40,40]{1,0:T(8,128)} %get-tuple-element.17), kind=kOutput, calls=%fused_computation.99 | convolution fusion | flops 19280 | bytes 6880 | tf_op jit(solution)/shard_map/dot_general | solution.py:76
  74.1 0.1 convolution_bitcast_fusion.2
  74.3 0.9 %convolution_bitcast_fusion.1 = f32[30,1]{0,1:T(1,128)S(1)} fusion(f32[30,30]{1,0:T(8,128)} %get-tuple-element.18, f32[30]{0:T(128)S(1)} %convolution_bitcast_fusion.2, f32[70]{0:T(128)S(1)} %add.158), kind=kOutput, calls=%fused_computation.13 | convolution fusion | flops 10830 | bytes 4120 | tf_op jit(solution)/shard_map/dot_general | solution.py:75
  75.2 0.9 %fusion.6 = f32[30]{0:T(128)S(1)} fusion(f32[30,1]{0,1:T(1,128)S(1)} %convolution_bitcast_fusion.1, f32[30,30]{1,0:T(8,128)} %get-tuple-element.18), kind=kOutput, calls=%fused_computation.18 | convolution fusion | flops 10830 | bytes 3840 | tf_op jit(solution)/shard_map/dot_general | solution.py:76
  76.1 2.4 %multiply_reduce_fusion = f32[256,128]{1,0:T(8,128)S(1)} fusion(bf16[40,256,128]{2,1,0:T(8,128)(2,1)} %param.19, f32[40]{0:T(128)S(1)} %get-tuple-element.53), kind=kLoop, calls=%fused_computation | loop fusion | flops 3899392 | bytes 2752672 | tf_op jit(solution)/shard_map/reduce_sum | solution.py:173
  78.4 0.5 multiply_reduce_fusion.2
  79.0 0.8 fusion.9
  (60 shorter events, 1.4 us)
Async XLA Ops:
  4.0 16.4 %all-to-all-start = ((f32[16,17,128]{2,1,0:T(8,128)}), f32[16,17,128]{2,1,0:T(8,128)S(1)}, u32[]{:S(2)}, u32[]{:S(2)}) async-start(f32[16,17,128]{2,1,0:T(8,128)} %select_maximum_fusion), calls=%async_computation | async-start | bytes 393216 | tf_op jit(solution)/shard_map/all_to_all | solution.py:118
  13.9 6.0 %collective-permute-start = (f32[4,384]{1,0:T(4,128)S(1)}, f32[4,384]{1,0:T(4,128)S(1)}, u32[]{:S(2)}, u32[]{:S(2)}) collective-permute-start(f32[4,384]{1,0:T(4,128)S(1)} %get-tuple-element.31), channel_id=1, source_target_pairs={{0,1},{1,2},{2,3},{3,4},{4,5},{5,6},{6,7},{7,8},{8,9},{9,10},{10,1... | collective-permute-start | bytes 18440 | tf_op jit(solution)/shard_map/ppermute | solution.py:28
  14.4 5.5 %collective-permute-start.2 = (f32[4,384]{1,0:T(4,128)S(1)}, f32[4,384]{1,0:T(4,128)S(1)}, u32[]{:S(2)}, u32[]{:S(2)}) collective-permute-start(f32[4,384]{1,0:T(4,128)S(1)} %get-tuple-element.32), channel_id=1, source_target_pairs={{1,0},{2,1},{3,2},{4,3},{5,4},{6,5},{7,6},{8,7},{9,8},{10,9},{11,1... | collective-permute-start | bytes 18440 | tf_op jit(solution)/shard_map/ppermute | solution.py:29
  20.7 11.2 %collective-permute-start.3 = (f32[4,128]{1,0:T(4,128)S(1)}, f32[4,128]{1,0:T(4,128)S(1)}, u32[]{:S(2)}, u32[]{:S(2)}) collective-permute-start(f32[4,128]{1,0:T(4,128)S(1)} %get-tuple-element.52), channel_id=1, source_target_pairs={{1,0},{2,1},{3,2},{4,3},{5,4},{6,5},{7,6},{8,7},{9,8},{10,9},{11,1... | collective-permute-start | bytes 6152 | tf_op jit(solution)/shard_map/ppermute | solution.py:29
  24.5 7.4 %collective-permute-start.1 = (f32[4,128]{1,0:T(4,128)S(1)}, f32[4,128]{1,0:T(4,128)S(1)}, u32[]{:S(2)}, u32[]{:S(2)}) collective-permute-start(f32[4,128]{1,0:T(4,128)S(1)} %get-tuple-element.51), channel_id=1, source_target_pairs={{0,1},{1,2},{2,3},{3,4},{4,5},{5,6},{6,7},{7,8},{8,9},{9,10},{10,1... | collective-permute-start | bytes 6152 | tf_op jit(solution)/shard_map/ppermute | solution.py:28
  24.7 2.3 %copy-start.1 = (bf16[30,256,128]{2,1,0:T(8,128)(2,1)S(1)}, bf16[30,256,128]{2,1,0:T(8,128)(2,1)}, u32[]{:S(2)}) copy-start(bf16[30,256,128]{2,1,0:T(8,128)(2,1)} %param.20) | copy-start | bytes 5898244
  30.2 1.7 %copy-start.3 = (f32[128,128]{1,0:T(8,128)S(1)}, f32[128,128]{1,0:T(8,128)}, u32[]{:S(2)}) copy-start(f32[128,128]{1,0:T(8,128)} %param.14) | copy-start | bytes 196612
  30.2 1.7 %copy-start.4 = (f32[128,128]{1,0:T(8,128)S(1)}, f32[128,128]{1,0:T(8,128)}, u32[]{:S(2)}) copy-start(f32[128,128]{1,0:T(8,128)} %param.15) | copy-start | bytes 196612
  30.2 1.7 %copy-start.5 = (f32[128,128]{1,0:T(8,128)S(1)}, f32[128,128]{1,0:T(8,128)}, u32[]{:S(2)}) copy-start(f32[128,128]{1,0:T(8,128)} %param.16) | copy-start | bytes 196612
  33.5 10.5 %copy-start.6 = (f32[128,128]{1,0:T(8,128)}, f32[128,128]{1,0:T(8,128)S(1)}, u32[]{:S(2)}) copy-start(f32[128,128]{1,0:T(8,128)S(1)} %get-tuple-element.19) | copy-start | bytes 196612
  34.5 16.7 %all-to-all-start.1 = ((f32[16,16,128]{2,1,0:T(8,128)}), f32[16,16,128]{2,1,0:T(8,128)S(1)}, u32[]{:S(2)}, u32[]{:S(2)}) async-start(f32[16,16,128]{2,1,0:T(8,128)} %bitcast.5), calls=%async_computation.1 | async-start | bytes 262144 | tf_op jit(solution)/shard_map/all_to_all | solution.py:157
  40.4 10.8 %copy-start.7 = (f32[256,128]{1,0:T(8,128)S(1)}, f32[256,128]{1,0:T(8,128)}, u32[]{:S(2)}) copy-start(f32[256,128]{1,0:T(8,128)} %param.13) | copy-start | bytes 393220
  44.0 9.5 %copy-start = (bf16[40,256,128]{2,1,0:T(8,128)(2,1)S(1)}, bf16[40,256,128]{2,1,0:T(8,128)(2,1)}, u32[]{:S(2)}) copy-start(bf16[40,256,128]{2,1,0:T(8,128)(2,1)} %param.18) | copy-start | bytes 7864324
  44.1 1.3 %collective-permute-start.4 = (f32[70,70]{1,0:T(8,128)S(1)}, f32[70,70]{1,0:T(8,128)S(1)}, u32[]{:S(2)}, u32[]{:S(2)}) collective-permute-start(f32[70,70]{1,0:T(8,128)S(1)} %fusion), channel_id=1, source_target_pairs={{0,1},{1,0},{2,3},{3,2},{4,5},{5,4},{6,7},{7,6},{8,9},{9,8},{10,11... | collective-permute-start | bytes 58808 | tf_op jit(solution)/shard_map/ppermute | solution.py:21
  45.4 4.0 %collective-permute-start.5 = (f32[70,70]{1,0:T(8,128)S(1)}, f32[70,70]{1,0:T(8,128)S(1)}, u32[]{:S(2)}, u32[]{:S(2)}) collective-permute-start(f32[70,70]{1,0:T(8,128)S(1)} %add.151), channel_id=1, source_target_pairs={{0,2},{1,3},{2,0},{3,1},{4,6},{5,7},{6,4},{7,5},{8,10},{9,11},{10,... | collective-permute-start | bytes 58808 | tf_op jit(solution)/shard_map/ppermute | solution.py:21
  49.4 5.1 %collective-permute-start.6 = (f32[70,70]{1,0:T(8,128)S(1)}, f32[70,70]{1,0:T(8,128)S(1)}, u32[]{:S(2)}, u32[]{:S(2)}) collective-permute-start(f32[70,70]{1,0:T(8,128)S(1)} %add.152), channel_id=1, source_target_pairs={{0,4},{1,5},{2,6},{3,7},{4,0},{5,1},{6,2},{7,3},{8,12},{9,13},{10,... | collective-permute-start | bytes 58808 | tf_op jit(solution)/shard_map/ppermute | solution.py:21
  54.4 24.1 %copy-start.2 = (bf16[30,256,128]{2,1,0:T(8,128)(2,1)S(1)}, bf16[30,256,128]{2,1,0:T(8,128)(2,1)}, u32[]{:S(2)}) copy-start(bf16[30,256,128]{2,1,0:T(8,128)(2,1)} %param.21) | copy-start | bytes 5898244
  54.4 2.5 %collective-permute-start.8 = (f32[70]{0:T(128)S(1)}, f32[70]{0:T(128)S(1)}, u32[]{:S(2)}, u32[]{:S(2)}) collective-permute-start(f32[70]{0:T(128)S(1)} %pad_maximum_fusion), channel_id=1, source_target_pairs={{0,1},{1,0},{2,3},{3,2},{4,5},{5,4},{6,7},{7,6},{8,9},{9,8},{10,11... | collective-permute-start | bytes 848 | tf_op jit(solution)/shard_map/ppermute | solution.py:21
  54.5 10.7 %collective-permute-start.7 = (f32[70,70]{1,0:T(8,128)S(1)}, f32[70,70]{1,0:T(8,128)S(1)}, u32[]{:S(2)}, u32[]{:S(2)}) collective-permute-start(f32[70,70]{1,0:T(8,128)S(1)} %add.153), channel_id=1, source_target_pairs={{0,8},{1,9},{2,10},{3,11},{4,12},{5,13},{6,14},{7,15},{8,0},{9,1},... | collective-permute-start | bytes 58808 | tf_op jit(solution)/shard_map/ppermute | solution.py:21
  57.0 3.6 %collective-permute-start.9 = (f32[70]{0:T(128)S(1)}, f32[70]{0:T(128)S(1)}, u32[]{:S(2)}, u32[]{:S(2)}) collective-permute-start(f32[70]{0:T(128)S(1)} %fusion.75), channel_id=1, source_target_pairs={{0,2},{1,3},{2,0},{3,1},{4,6},{5,7},{6,4},{7,5},{8,10},{9,11},{10,... | collective-permute-start | bytes 848 | tf_op jit(solution)/shard_map/ppermute | solution.py:21
  60.6 3.6 %collective-permute-start.10 = (f32[70]{0:T(128)S(1)}, f32[70]{0:T(128)S(1)}, u32[]{:S(2)}, u32[]{:S(2)}) collective-permute-start(f32[70]{0:T(128)S(1)} %add.156), channel_id=1, source_target_pairs={{0,4},{1,5},{2,6},{3,7},{4,0},{5,1},{6,2},{7,3},{8,12},{9,13},{10,... | collective-permute-start | bytes 848 | tf_op jit(solution)/shard_map/ppermute | solution.py:21
  64.1 8.2 %collective-permute-start.11 = (f32[70]{0:T(128)S(1)}, f32[70]{0:T(128)S(1)}, u32[]{:S(2)}, u32[]{:S(2)}) collective-permute-start(f32[70]{0:T(128)S(1)} %add.157), channel_id=1, source_target_pairs={{0,8},{1,9},{2,10},{3,11},{4,12},{5,13},{6,14},{7,15},{8,0},{9,1},... | collective-permute-start | bytes 848 | tf_op jit(solution)/shard_map/ppermute | solution.py:21

commit v9 on v7

--- a/solution.py
+++ b/solution.py
@@ -1,8 +1,8 @@
 import jax
 import jax.numpy as jnp
 from jax import lax
+from jax.experimental import pallas as pl
 from jax.sharding import PartitionSpec as P
-
 
 SUBSTEPS = 4
 
@@ -40,10 +40,38 @@
     return left + right
 
 
-def inverse_factor(matrix):
-    factor = jnp.linalg.cholesky(matrix)
-    eye = jnp.eye(matrix.shape[0], dtype=matrix.dtype)
-    return lax.linalg.triangular_solve(factor, eye, left_side=True, lower=True)
+def eliminate(mats):
+    state = []
+    for a in mats:
+        n = a.shape[0]
+        rows = lax.broadcasted_iota(jnp.int32, (n, n), 0)
+        cols = lax.broadcasted_iota(jnp.int32, (n, n), 1)
+        state.append([a, jnp.where(rows == cols, 1.0, 0.0).astype(jnp.float32), rows, cols])
+    for j in range(max(a.shape[0] for a in mats)):
+        for item in state:
+            a, m, rows, cols = item
+            if j >= a.shape[0]:
+                continue
+            on_row = rows == j
+            row = jnp.sum(jnp.where(on_row, a, 0.0), axis=0, keepdims=True)
+            col = jnp.sum(jnp.where(cols == j, a, 0.0), axis=1, keepdims=True)
+            pivot = jnp.sum(jnp.where(cols[:1] == j, row, 0.0), axis=1, keepdims=True)
+            scale = 1.0 / jnp.sqrt(pivot)
+            row = jnp.where(cols[:1] >= j, row * scale, 0.0)
+            lower = jnp.where(rows[:, :1] > j, col * scale, 0.0)
+            m_row = jnp.sum(jnp.where(on_row, m, 0.0), axis=0, keepdims=True) * scale
+            item[0] = jnp.where(on_row, row, a - lower * row)
+            item[1] = jnp.where(on_row, m_row, m - lower * m_row)
+    return [item[1] for item in state]
+
+
+def factor_kernel(cur_ref, past_ref, inv_cur_ref, inv_past_ref):
+    inv_cur_ref[...], inv_past_ref[...] = eliminate([cur_ref[...], past_ref[...]])
+
+
+def inverse_factors(cur, past):
+    shapes = (jax.ShapeDtypeStruct(cur.shape, jnp.float32), jax.ShapeDtypeStruct(past.shape, jnp.float32))
+    return pl.pallas_call(factor_kernel, out_shape=shapes)(cur, past)
 
 
 def solve_spd(inverse, vector):
@@ -104,10 +132,6 @@
         axis=0,
     )
     gram = lax.dot_general(cols, cols, (((1,), (1,)), ((), ())), preferred_element_type=jnp.float32)
-    gram = tree_sum(gram, "tile")
-    cross = gram[n_cur:, :n_cur]
-    inv_cur = inverse_factor(gram[:n_cur, :n_cur])
-    inv_past = inverse_factor(gram[n_cur:, n_cur:])
 
     pressure = jnp.dot(chooser, returned, precision=high)
     press_below, press_above = halo_pair(pressure, width, "tile")
@@ -139,9 +163,13 @@
             jnp.sum(diff_past.astype(jnp.float32) * resid[None], axis=(1, 2)),
         ]
     )
-    inner = tree_sum(inner, "tile")
-    rhs_cur = inner[:n_cur]
-    rhs_past = inner[n_cur:]
+    n_all = gram.shape[0]
+    summed = tree_sum(jnp.concatenate([gram.reshape(-1), inner]), "tile")
+    gram = summed[: n_all * n_all].reshape(n_all, n_all)
+    rhs_cur = summed[n_all * n_all : n_all * n_all + n_cur]
+    rhs_past = summed[n_all * n_all + n_cur :]
+    cross = gram[n_cur:, :n_cur]
+    inv_cur, inv_past = inverse_factors(gram[:n_cur, :n_cur], gram[n_cur:, n_cur:])
     coeff = -solve_spd(inv_cur, rhs_cur)
     projected = rhs_past + jnp.dot(cross, coeff, precision=high)
     past = solve_spd(inv_past, projected)

time: 82.7 us -> 79.4 us (0.960)
  other arithmetic: 27.1 us -> 9.49 us
  starting transfers between devices: 28.9 us -> 22 us
  matrix products: 4.79 us -> 11.3 us
  Pallas kernels: 0 us -> 5.91 us
  local copies, waits for them, and re-layouts: 7.14 us -> 11.7 us
  waiting for transfers between devices: 13.2 us -> 17.4 us
    another operation x10 -> x0, other arithmetic: 14.5 us -> none  [the longest x6 7.81 us: inverse_factor(): factor = jnp.linalg.cholesky(matrix)]
    ppermute x8 -> x4, starting transfers between devices: 8.27 us -> 0.43 us  [tree_sum(): lax.ppermute(value, axis, [(i, i ^ stride) for i in range(count)])]
    pallas_call x0 -> x1, Pallas kernels: none -> 5.91 us  [inverse_factors(): return pl.pallas_call(factor_kernel, out_shape=shapes)(cur, past)]
    dot_general x1, matrix products: 1.38 us -> 5.29 us  [body(): lax.dot_general(cols, cols, (((1,), (1,)), ((), ())), preferred_element_t...]
    unnamed x19 -> x25, local copies, waits for them, and re-layouts: 5.38 us -> 8.66 us
    all_to_all x1, waiting for transfers between devices: 0.01 us -> 2.43 us  [body(): lax.all_to_all(outgoing, 'tile', split_axis=0, concat_axis=0, tiled=True)]
    mul x1, other arithmetic: 0.25 us -> 2.13 us  [body(): diff_cur * mask_half[None, :, None]]
    ppermute x8 -> x4, waiting for transfers between devices: 11.3 us -> 13 us  [tree_sum(): lax.ppermute(value, axis, [(i, i ^ stride) for i in range(count)])]
  transfers between devices with their start and end apart: 14 -> 10, of which waited for: 8 -> 7; matrix products, arithmetic and copies ran while one was open for 33% -> 21% of each run, Pallas kernels for 0% -> 0%
where the time goes in v9:
time: 79.4 us; the launch traced here: 78.7 us
  starting transfers between devices  22 us (28%)
  waiting for transfers between devices  17.4 us (22%)
  local copies, waits for them, and re-layouts  11.7 us (15%)
  matrix products  11.3 us (14%)
  other arithmetic  9.49 us (12%)
  Pallas kernels  5.91 us (7%)
  between operations  0.91 us (1%)
    ppermute x4, waiting for transfers between devices, tree_sum(): lax.ppermute(value, axis, [(i, i ^ stride) for i in range(count)])  13 us
    unnamed x25, local copies, waits for them, and re-layouts  8.66 us
    ppermute x2, starting transfers between devices, halo_pair(): lax.ppermute(cells[:width], axis, [((i + 1) % count, i) for i in range(co...  7.86 us
    all_to_all x1, starting transfers between devices, body(): got = lax.all_to_all(sent, 'tile', split_axis=0, concat_axis=0, tiled=True)  7.41 us
    pallas_call x1, Pallas kernels, inverse_factors(): return pl.pallas_call(factor_kernel, out_shape=shapes)(cur, past)  5.91 us
    all_to_all x1, starting transfers between devices, body(): lax.all_to_all(outgoing, 'tile', split_axis=0, concat_axis=0, tiled=True)  5.83 us
    dot_general x1, matrix products, body(): lax.dot_general(cols, cols, (((1,), (1,)), ((), ())), preferred_element_t...  5.29 us
    all_to_all x1, waiting for transfers between devices, body(): lax.all_to_all(outgoing, 'tile', split_axis=0, concat_axis=0, tiled=True)  2.43 us
  transfers between devices with their start and end apart: 10, of which 7 were waited for; matrix products, arithmetic and copies ran while one was open for 21% of the time, Pallas kernels for 0%

profile of v9, /device:TPU:0, one launch (start us, length us, event | category | flops | bytes accessed | tf_op | source)
XLA Modules:
  0.0 78.7 jit_solution(6073113971554778900)
XLA Ops:
  0.6 0.9 %fusion.4 = f32[128]{0:T(128)S(1)} fusion(s32[128]{0:T(128)} %bitcast.73), kind=kOutput, calls=%fused_computation.11 | convolution fusion | flops 548736 | bytes 1024 | tf_op jit(solution)/shard_map/dot_general | solution.py:106
  1.5 0.7 fusion.45
  2.4 1.6 %select_maximum_fusion = f32[16,17,128]{2,1,0:T(8,128)} fusion(f32[16,1,16]{2,1,0:T(1,128)S(1)} %reshape.91, f32[16,16,128]{2,1,0:T(8,128)} %bitcast.71), kind=kLoop, calls=%fused_computation.21 | loop fusion | flops 104448 | bytes 271360 | tf_op jit(solution)/shard_map/concatenate | solution.py:121
  4.0 7.4 %all-to-all-start = ((f32[16,17,128]{2,1,0:T(8,128)}), f32[16,17,128]{2,1,0:T(8,128)S(1)}, u32[]{:S(2)}, u32[]{:S(2)}) async-start(f32[16,17,128]{2,1,0:T(8,128)} %select_maximum_fusion), calls=%async_computation | async-start | bytes 393216 | tf_op jit(solution)/shard_map/all_to_all | solution.py:122
  11.4 0.8 %constant_dynamic-update-slice_fusion.2 = f32[128,384]{1,0:T(8,128)S(1)} fusion(f32[128,128]{1,0:T(8,128)} %param.14), kind=kLoop, calls=%fused_computation.71 | loop fusion | bytes 131072
  12.2 0.8 %constant_dynamic-update-slice_fusion.1 = f32[128,384]{1,0:T(8,128)S(1)} fusion(f32[128,384]{1,0:T(8,128)S(1)} %constant_dynamic-update-slice_fusion.2, f32[128,128]{1,0:T(8,128)} %param.15), kind=kLoop, calls=%fused_computation.70 | loop fusion | bytes 131072
  13.1 0.8 %constant_dynamic-update-slice_fusion = f32[128,384]{1,0:T(8,128)S(1)} fusion(f32[128,384]{1,0:T(8,128)S(1)} %constant_dynamic-update-slice_fusion.1, f32[128,128]{1,0:T(8,128)} %param.16), kind=kLoop, calls=%fused_computation.69 | loop fusion | bytes 131072 | tf_op jit(solution)/shard_map/concatenate | solution.py:116
  13.9 0.5 collective-permute-start
  14.4 4.0 %collective-permute-start.2 = (f32[4,384]{1,0:T(4,128)S(1)}, f32[4,384]{1,0:T(4,128)S(1)}, u32[]{:S(2)}, u32[]{:S(2)}) collective-permute-start(f32[4,384]{1,0:T(4,128)S(1)} %get-tuple-element.32), channel_id=1, source_target_pairs={{1,0},{2,1},{3,2},{4,3},{5,4},{6,5},{7,6},{8,7},{9,8},{10,9},{11,1... | collective-permute-start | bytes 18440 | tf_op jit(solution)/shard_map/ppermute | solution.py:28
  18.4 1.5 %collective-permute-done = f32[4,384]{1,0:T(4,128)S(1)} collective-permute-done((f32[4,384]{1,0:T(4,128)S(1)}, f32[4,384]{1,0:T(4,128)S(1)}, u32[]{:S(2)}, u32[]{:S(2)}) %collective-permute-start) | collective-permute-done | bytes 6176 | tf_op jit(solution)/shard_map/ppermute | solution.py:27
  19.9 0.5 all-to-all-done
  20.4 0.3 fusion.11
  20.7 3.8 %collective-permute-start.3 = (f32[4,128]{1,0:T(4,128)S(1)}, f32[4,128]{1,0:T(4,128)S(1)}, u32[]{:S(2)}, u32[]{:S(2)}) collective-permute-start(f32[4,128]{1,0:T(4,128)S(1)} %get-tuple-element.52), channel_id=1, source_target_pairs={{1,0},{2,1},{3,2},{4,3},{5,4},{6,5},{7,6},{8,7},{9,8},{10,9},{11,1... | collective-permute-start | bytes 6152 | tf_op jit(solution)/shard_map/ppermute | solution.py:28
  24.7 2.1 %broadcast_multiply_fusion = bf16[40,256,128]{2,1,0:T(8,128)(2,1)S(1)} fusion(bf16[40,256,128]{2,1,0:T(8,128)(2,1)} %param.18, bf16[256]{0:T(256)(128)(2,1)S(1)} %convert_element_type.40), kind=kLoop, calls=%fused_computation.9 | loop fusion | flops 1310720 | bytes 5243392 | tf_op jit(solution)/shard_map/mul | solution.py:129
  26.8 0.2 copy-done.1
  27.0 0.2 broadcast_multiply_fusion.1
  27.2 0.3 pad.42
  27.5 2.7 %copy.14 = bf16[4,8,256,128]{3,1,2,0:T(8,128)(2,1)} copy(bf16[4,8,256,128]{3,2,1,0:T(8,128)(2,1)S(1)} %bitcast.67) | data formatting | bytes 4194304
  30.2 3.2 %copy.16 = bf16[5,8,256,128]{3,1,2,0:T(8,128)(2,1)} copy(bf16[5,8,256,128]{3,2,1,0:T(8,128)(2,1)S(1)} %bitcast.66) | data formatting | bytes 5242880
  33.8 0.1 fusion.49
  34.0 0.1 fusion.47
  34.2 0.1 fusion.35
  34.4 0.6 slice_add_fusion
  35.0 1.0 %fusion.10 = f32[256,128]{1,0:T(8,128)} fusion(f32[128,128]{1,0:T(8,128)S(1)} %get-tuple-element.19, s32[128]{0:T(128)S(1)} %fusion.45), kind=kOutput, calls=%fused_computation.30 | convolution fusion | flops 50364416 | bytes 197120 | tf_op jit(solution)/shard_map/dot_general | solution.py:157
  36.0 5.8 %all-to-all-start.1 = ((f32[16,16,128]{2,1,0:T(8,128)}), f32[16,16,128]{2,1,0:T(8,128)S(1)}, u32[]{:S(2)}, u32[]{:S(2)}) async-start(f32[16,16,128]{2,1,0:T(8,128)} %bitcast.5), calls=%async_computation.1 | async-start | bytes 262144 | tf_op jit(solution)/shard_map/all_to_all | solution.py:158
  41.9 5.3 %fusion = f32[70,70]{1,0:T(8,128)S(1)} fusion(bf16[30,32768]{1,0:T(8,128)(2,1)} %bitcast.69, bf16[40,32768]{1,0:T(8,128)(2,1)} %bitcast.68), kind=kOutput, calls=%fused_computation.2 | convolution fusion | flops 330301440 | bytes 4607120 | tf_op jit(solution)/shard_map/dot_general | solution.py:134
  47.2 0.1 reshape.95
  47.3 2.4 %all-to-all-done.1 = f32[16,16,128]{2,1,0:T(8,128)S(1)} async-done(((f32[16,16,128]{2,1,0:T(8,128)}), f32[16,16,128]{2,1,0:T(8,128)S(1)}, u32[]{:S(2)}, u32[]{:S(2)}) %all-to-all-start.1) | async-done | bytes 131104 | tf_op jit(solution)/shard_map/all_to_all | solution.py:158
  49.9 0.9 %multiply_reduce_fusion.1 = f32[40]{0:T(128)S(1)} fusion(bf16[40,256,128]{2,1,0:T(8,128)(2,1)S(1)} %copy-done, f32[256,128]{1,0:T(8,128)S(1)} %fusion.8), kind=kLoop, calls=%fused_computation.1 | loop fusion | flops 3932120 | bytes 2752672 | tf_op jit(solution)/shard_map/reduce_sum | solution.py:162
  50.7 0.6 copy-done.2
  51.3 0.6 multiply_reduce_fusion.3
  52.0 1.2 %collective-permute-done.4 = f32[4970]{0:T(1024)S(1)} collective-permute-done((f32[4970]{0:T(1024)S(1)}, f32[4970]{0:T(1024)S(1)}, u32[]{:S(2)}, u32[]{:S(2)}) %collective-permute-start.4) | collective-permute-done | bytes 19912 | tf_op jit(solution)/shard_map/ppermute | solution.py:20
  53.2 3.8 %collective-permute-done.5 = f32[4970]{0:T(1024)S(1)} collective-permute-done((f32[4970]{0:T(1024)S(1)}, f32[4970]{0:T(1024)S(1)}, u32[]{:S(2)}, u32[]{:S(2)}) %collective-permute-start.5) | collective-permute-done | bytes 19912 | tf_op jit(solution)/shard_map/ppermute | solution.py:20
  57.0 3.8 %collective-permute-done.6 = f32[4970]{0:T(1024)S(1)} collective-permute-done((f32[4970]{0:T(1024)S(1)}, f32[4970]{0:T(1024)S(1)}, u32[]{:S(2)}, u32[]{:S(2)}) %collective-permute-start.6) | collective-permute-done | bytes 19912 | tf_op jit(solution)/shard_map/ppermute | solution.py:20
  60.8 0.4 collective-permute-start.7
  61.2 4.3 %collective-permute-done.7 = f32[4970]{0:T(1024)S(1)} collective-permute-done((f32[4970]{0:T(1024)S(1)}, f32[4970]{0:T(1024)S(1)}, u32[]{:S(2)}, u32[]{:S(2)}) %collective-permute-start.7) | collective-permute-done | bytes 19912 | tf_op jit(solution)/shard_map/ppermute | solution.py:20
  65.5 0.1 slice.209
  65.6 0.6 slice.253.cur_ref
  66.2 0.7 slice.254.past_ref
  66.9 5.9 %shard_map.121 = (f32[40,40]{1,0:T(8,128)}, f32[30,30]{1,0:T(8,128)}) custom-call(f32[40,40]{1,0:T(8,128)} %slice.253.cur_ref, f32[30,30]{1,0:T(8,128)} %slice.254.past_ref), custom_call_target="tpu_custom_call" | custom-call | tf_op jit(solution)/shard_map/pallas_call | solution.py:74
  72.8 1.1 %convolution_bitcast_fusion.4 = f32[40,1]{0,1:T(1,128)S(1)} fusion(f32[40,40]{1,0:T(8,128)} %get-tuple-element.17, f32[4970]{0:T(1024)S(1)} %add.142), kind=kOutput, calls=%fused_computation.16 | convolution fusion | flops 19200 | bytes 7072 | tf_op jit(solution)/shard_map/dot_general | solution.py:79
  73.8 0.9 %fusion.65 = (f32[40]{0:T(128)S(1)}, f32[40]{0:T(128)S(1)}) fusion(f32[40,1]{0,1:T(1,128)S(1)} %convolution_bitcast_fusion.4, f32[40,40]{1,0:T(8,128)} %get-tuple-element.17), kind=kOutput, calls=%fused_computation.96 | convolution fusion | flops 19280 | bytes 6880 | tf_op jit(solution)/shard_map/dot_general | solution.py:80
  74.7 0.1 convolution_bitcast_fusion.2
  74.9 0.9 %convolution_bitcast_fusion.1 = f32[30,1]{0,1:T(1,128)S(1)} fusion(f32[30,30]{1,0:T(8,128)} %get-tuple-element.18, f32[30]{0:T(128)S(1)} %convolution_bitcast_fusion.2, f32[4970]{0:T(1024)S(1)} %add.142), kind=kOutput, calls=%fused_computation.13 | convolution fusion | flops 10830 | bytes 4744 | tf_op jit(solution)/shard_map/dot_general | solution.py:79
  75.8 0.9 %fusion.6 = f32[30]{0:T(128)S(1)} fusion(f32[30,1]{0,1:T(1,128)S(1)} %convolution_bitcast_fusion.1, f32[30,30]{1,0:T(8,128)} %get-tuple-element.18), kind=kOutput, calls=%fused_computation.18 | convolution fusion | flops 10830 | bytes 3840 | tf_op jit(solution)/shard_map/dot_general | solution.py:80
  76.7 0.8 multiply_reduce_fusion
  77.4 0.5 multiply_reduce_fusion.2
  78.0 0.8 fusion.9
  (54 shorter events, 1.1 us)
Async XLA Ops:
  4.0 16.4 %all-to-all-start = ((f32[16,17,128]{2,1,0:T(8,128)}), f32[16,17,128]{2,1,0:T(8,128)S(1)}, u32[]{:S(2)}, u32[]{:S(2)}) async-start(f32[16,17,128]{2,1,0:T(8,128)} %select_maximum_fusion), calls=%async_computation | async-start | bytes 393216 | tf_op jit(solution)/shard_map/all_to_all | solution.py:122
  13.9 6.0 %collective-permute-start = (f32[4,384]{1,0:T(4,128)S(1)}, f32[4,384]{1,0:T(4,128)S(1)}, u32[]{:S(2)}, u32[]{:S(2)}) collective-permute-start(f32[4,384]{1,0:T(4,128)S(1)} %get-tuple-element.31), channel_id=1, source_target_pairs={{0,1},{1,2},{2,3},{3,4},{4,5},{5,6},{6,7},{7,8},{8,9},{9,10},{10,1... | collective-permute-start | bytes 18440 | tf_op jit(solution)/shard_map/ppermute | solution.py:27
  14.4 5.5 %collective-permute-start.2 = (f32[4,384]{1,0:T(4,128)S(1)}, f32[4,384]{1,0:T(4,128)S(1)}, u32[]{:S(2)}, u32[]{:S(2)}) collective-permute-start(f32[4,384]{1,0:T(4,128)S(1)} %get-tuple-element.32), channel_id=1, source_target_pairs={{1,0},{2,1},{3,2},{4,3},{5,4},{6,5},{7,6},{8,7},{9,8},{10,9},{11,1... | collective-permute-start | bytes 18440 | tf_op jit(solution)/shard_map/ppermute | solution.py:28
  20.7 12.7 %collective-permute-start.3 = (f32[4,128]{1,0:T(4,128)S(1)}, f32[4,128]{1,0:T(4,128)S(1)}, u32[]{:S(2)}, u32[]{:S(2)}) collective-permute-start(f32[4,128]{1,0:T(4,128)S(1)} %get-tuple-element.52), channel_id=1, source_target_pairs={{1,0},{2,1},{3,2},{4,3},{5,4},{6,5},{7,6},{8,7},{9,8},{10,9},{11,1... | collective-permute-start | bytes 6152 | tf_op jit(solution)/shard_map/ppermute | solution.py:28
  24.5 8.9 %collective-permute-start.1 = (f32[4,128]{1,0:T(4,128)S(1)}, f32[4,128]{1,0:T(4,128)S(1)}, u32[]{:S(2)}, u32[]{:S(2)}) collective-permute-start(f32[4,128]{1,0:T(4,128)S(1)} %get-tuple-element.51), channel_id=1, source_target_pairs={{0,1},{1,2},{2,3},{3,4},{4,5},{5,6},{6,7},{7,8},{8,9},{9,10},{10,1... | collective-permute-start | bytes 6152 | tf_op jit(solution)/shard_map/ppermute | solution.py:27
  24.7 2.3 %copy-start.1 = (bf16[30,256,128]{2,1,0:T(8,128)(2,1)S(1)}, bf16[30,256,128]{2,1,0:T(8,128)(2,1)}, u32[]{:S(2)}) copy-start(bf16[30,256,128]{2,1,0:T(8,128)(2,1)} %param.20) | copy-start | bytes 5898244
  30.2 3.2 %copy-start.5 = (f32[128,128]{1,0:T(8,128)S(1)}, f32[128,128]{1,0:T(8,128)}, u32[]{:S(2)}) copy-start(f32[128,128]{1,0:T(8,128)} %param.14) | copy-start | bytes 196612
  30.2 3.2 %copy-start.6 = (f32[128,128]{1,0:T(8,128)S(1)}, f32[128,128]{1,0:T(8,128)}, u32[]{:S(2)}) copy-start(f32[128,128]{1,0:T(8,128)} %param.15) | copy-start | bytes 196612
  30.2 3.2 %copy-start.7 = (f32[128,128]{1,0:T(8,128)S(1)}, f32[128,128]{1,0:T(8,128)}, u32[]{:S(2)}) copy-start(f32[128,128]{1,0:T(8,128)} %param.16) | copy-start | bytes 196612
  35.0 12.2 %copy-start.8 = (f32[128,128]{1,0:T(8,128)}, f32[128,128]{1,0:T(8,128)S(1)}, u32[]{:S(2)}) copy-start(f32[128,128]{1,0:T(8,128)S(1)} %get-tuple-element.19) | copy-start | bytes 196612
  36.0 13.7 %all-to-all-start.1 = ((f32[16,16,128]{2,1,0:T(8,128)}), f32[16,16,128]{2,1,0:T(8,128)S(1)}, u32[]{:S(2)}, u32[]{:S(2)}) async-start(f32[16,16,128]{2,1,0:T(8,128)} %bitcast.5), calls=%async_computation.1 | async-start | bytes 262144 | tf_op jit(solution)/shard_map/all_to_all | solution.py:158
  41.8 7.9 %copy-start.9 = (f32[256,128]{1,0:T(8,128)S(1)}, f32[256,128]{1,0:T(8,128)}, u32[]{:S(2)}) copy-start(f32[256,128]{1,0:T(8,128)} %param.13) | copy-start | bytes 393220
  41.9 8.0 %copy-start = (bf16[40,256,128]{2,1,0:T(8,128)(2,1)S(1)}, bf16[40,256,128]{2,1,0:T(8,128)(2,1)}, u32[]{:S(2)}) copy-start(bf16[40,256,128]{2,1,0:T(8,128)(2,1)} %param.18) | copy-start | bytes 7864324
  49.7 1.5 %copy-start.2 = (bf16[30,256,128]{2,1,0:T(8,128)(2,1)S(1)}, bf16[30,256,128]{2,1,0:T(8,128)(2,1)}, u32[]{:S(2)}) copy-start(bf16[30,256,128]{2,1,0:T(8,128)(2,1)} %param.20) | copy-start | bytes 5898244
  51.3 25.4 %copy-start.3 = (bf16[40,256,128]{2,1,0:T(8,128)(2,1)S(1)}, bf16[40,256,128]{2,1,0:T(8,128)(2,1)}, u32[]{:S(2)}) copy-start(bf16[40,256,128]{2,1,0:T(8,128)(2,1)} %param.19) | copy-start | bytes 7864324
  52.0 1.2 %collective-permute-start.4 = (f32[4970]{0:T(1024)S(1)}, f32[4970]{0:T(1024)S(1)}, u32[]{:S(2)}, u32[]{:S(2)}) collective-permute-start(f32[4970]{0:T(1024)S(1)} %concatenate.100), channel_id=1, source_target_pairs={{0,1},{1,0},{2,3},{3,2},{4,5},{5,4},{6,7},{7,6},{8,9},{9,8},{10,11... | collective-permute-start | bytes 59648 | tf_op jit(solution)/shard_map/ppermute | solution.py:20
  53.2 3.8 %collective-permute-start.5 = (f32[4970]{0:T(1024)S(1)}, f32[4970]{0:T(1024)S(1)}, u32[]{:S(2)}, u32[]{:S(2)}) collective-permute-start(f32[4970]{0:T(1024)S(1)} %add.139), channel_id=1, source_target_pairs={{0,2},{1,3},{2,0},{3,1},{4,6},{5,7},{6,4},{7,5},{8,10},{9,11},{10,... | collective-permute-start | bytes 59648 | tf_op jit(solution)/shard_map/ppermute | solution.py:20
  57.0 3.8 %collective-permute-start.6 = (f32[4970]{0:T(1024)S(1)}, f32[4970]{0:T(1024)S(1)}, u32[]{:S(2)}, u32[]{:S(2)}) collective-permute-start(f32[4970]{0:T(1024)S(1)} %add.140), channel_id=1, source_target_pairs={{0,4},{1,5},{2,6},{3,7},{4,0},{5,1},{6,2},{7,3},{8,12},{9,13},{10,... | collective-permute-start | bytes 59648 | tf_op jit(solution)/shard_map/ppermute | solution.py:20
  60.8 4.7 %collective-permute-start.7 = (f32[4970]{0:T(1024)S(1)}, f32[4970]{0:T(1024)S(1)}, u32[]{:S(2)}, u32[]{:S(2)}) collective-permute-start(f32[4970]{0:T(1024)S(1)} %add.141), channel_id=1, source_target_pairs={{0,8},{1,9},{2,10},{3,11},{4,12},{5,13},{6,14},{7,15},{8,0},{9,1},... | collective-permute-start | bytes 59648 | tf_op jit(solution)/shard_map/ppermute | solution.py:20
  72.8 4.6 %copy-start.4 = (bf16[30,256,128]{2,1,0:T(8,128)(2,1)S(1)}, bf16[30,256,128]{2,1,0:T(8,128)(2,1)}, u32[]{:S(2)}) copy-start(bf16[30,256,128]{2,1,0:T(8,128)(2,1)} %param.21) | copy-start | bytes 5898244
